TPU v7x, 256 devices: a whole 4x4x8 slice. The times are simulated.
256 devices in a mesh: level: 2 (over core), row: 16 (over z_lo, x), col: 8 (over z_hi, y).
Axes of the slice: x: 4, y: 4, z: 8 (z_hi: 2, z_lo: 4; z = z_hi * 4 + z_lo), core: 2. Of those that a mesh axis runs over, the one named last changes fastest.
Arguments:
- friction: float32 [2, 1024, 2048], P('level', 'row', 'col'), may hold values from 0.1 to 4
- height: float32 [2, 1024, 2048], P('level', 'row', 'col'), may hold values from -3 to 3
- inflow: float32 [1024], replicated, may hold values from -2 to 2
Outputs:
- fine_mean: float32 [2, 3, 512, 1024], P('level', None, 'row', 'col')
- correction: float32 [2, 3, 512, 1024], P('level', None, 'row', 'col')
All inputs are finite; a program needn't handle non-finite values.
Results may differ from a plain program's by a relative error of at most 0.0003.
Values sent between devices are 32-bit elements; how exact they have to be, the bound alone decides.
No kernel may reach another device: no remote copies, remote signals or barrier semaphores. Data moves between devices by JAX's collectives and lax.ppermute only.
A program may use at most 128 MiB of HBM per device.

v0:
```python
import jax
import jax.numpy as jnp
from jax import lax
from jax.sharding import PartitionSpec as P

step_ratio = 0.15
fine_step = 0.15
coarse_step = 0.3
HALO = 2


def shift_pairs(count, delta, place=lambda i: i):
    return [(place(i), place(i + delta)) for i in range(count) if 0 <= i + delta < count]


def strip_place(strip):
    levels = lax.axis_size("level")
    return (strip % levels) * lax.axis_size("col") + strip // levels


def pair_matrix(count):
    rows = jnp.arange(count)[:, None] // 2
    cols = jnp.arange(count // 2)[None, :]
    return (rows == cols).astype(jnp.float32)


def restrict(values):
    lead = values.shape[:-2]
    count_rows, count_cols = values.shape[-2], values.shape[-1]
    rows = values.reshape(lead + (count_rows // 2, 2, count_cols))
    rows = rows[..., 0, :] + rows[..., 1, :]
    both = jnp.einsum(
        "...ij,jk->...ik", rows, pair_matrix(count_cols), precision=lax.Precision.HIGHEST
    )
    return both * 0.25


def pair_mean(values):
    paired = values.reshape(-1, 2)
    return (paired[:, 0] + paired[:, 1]) * 0.5


def apply_walls(padded, layer, at_top, at_bottom, at_left, at_right, inflow_speed):
    count_rows = padded.shape[1]
    count_cols = padded.shape[2]
    low = count_rows - 1 - layer
    source = padded[:, layer + 1, :]
    mirror = jnp.stack([source[0], source[1], -source[2]])
    top = jnp.where(at_top, mirror, padded[:, layer, :])
    source = padded[:, low - 1, :]
    mirror = jnp.stack([source[0], source[1], -source[2]])
    bottom = jnp.where(at_bottom, mirror, padded[:, low, :])
    padded = jnp.concatenate(
        [padded[:, :layer], top[:, None], padded[:, layer + 1: low], bottom[:, None],
         padded[:, low + 1:]],
        axis=1,
    )
    right_col = count_cols - 1 - layer
    source = padded[:, :, layer + 1]
    entering = jnp.stack([source[0], source[0] * inflow_speed, jnp.zeros_like(source[0])])
    left = jnp.where(at_left, entering, padded[:, :, layer])
    right = jnp.where(at_right, padded[:, :, right_col - 1], padded[:, :, right_col])
    return jnp.concatenate(
        [padded[:, :, :layer], left[:, :, None], padded[:, :, layer + 1: right_col],
         right[:, :, None], padded[:, :, right_col + 1:]],
        axis=2,
    )


def advance(padded, friction_coef, step):
    across = padded[:, 1:-1, :]
    depth = across[0]
    velocity = across[1] / depth
    flux = jnp.stack([across[1], across[1] * velocity + 0.5 * depth * depth, across[2] * velocity])
    speed = jnp.abs(velocity) + jnp.sqrt(depth)
    face_x = 0.5 * (flux[:, :, 1:] + flux[:, :, :-1]) - 0.5 * jnp.maximum(
        speed[:, 1:], speed[:, :-1]
    ) * (across[:, :, 1:] - across[:, :, :-1])
    along = padded[:, :, 1:-1]
    depth = along[0]
    velocity = along[2] / depth
    flux = jnp.stack([along[2], along[1] * velocity, along[2] * velocity + 0.5 * depth * depth])
    speed = jnp.abs(velocity) + jnp.sqrt(depth)
    face_y = 0.5 * (flux[:, 1:, :] + flux[:, :-1, :]) - 0.5 * jnp.maximum(
        speed[1:, :], speed[:-1, :]
    ) * (along[:, 1:, :] - along[:, :-1, :])
    moved = padded[:, 1:-1, 1:-1] - step_ratio * (
        face_x[:, :, 1:] - face_x[:, :, :-1] + (face_y[:, 1:, :] - face_y[:, :-1, :])
    )
    depth = moved[0]
    speed = jnp.sqrt(moved[1] * moved[1] + moved[2] * moved[2]) / depth
    damping = 1.0 / (1.0 + step * friction_coef * speed / depth)
    return jnp.stack([depth, moved[1] * damping, moved[2] * damping])


def with_halo(noise):
    strips = lax.axis_size("col") * lax.axis_size("level")
    rows = lax.axis_size("row")
    across = ("level", "col")
    west = lax.ppermute(noise[:, :, -HALO:], across, shift_pairs(strips, 1, strip_place))
    east = lax.ppermute(noise[:, :, :HALO], across, shift_pairs(strips, -1, strip_place))
    wide = jnp.concatenate([west, noise, east], axis=2)
    north = lax.ppermute(wide[:, -HALO:, :], "row", shift_pairs(rows, 1))
    south = lax.ppermute(wide[:, :HALO, :], "row", shift_pairs(rows, -1))
    return jnp.concatenate([north, wide, south], axis=1)


def body(friction, height, inflow):
    strip = lax.axis_index("col") * lax.axis_size("level") + lax.axis_index("level")
    strips = lax.axis_size("col") * lax.axis_size("level")
    row_index = lax.axis_index("row")
    at_top = row_index == 0
    at_bottom = row_index == lax.axis_size("row") - 1
    at_left = strip == 0
    at_right = strip == strips - 1
    tile_rows = friction.shape[1]
    coarse_rows = tile_rows // 2

    noise = with_halo(jnp.concatenate([friction, height], axis=0))
    fine_coef = noise[0]
    depth = 1.0 + 0.1 * noise[1]
    state = jnp.stack([depth, 0.5 * depth, jnp.zeros_like(depth)])

    fine_inflow = 0.5 + lax.dynamic_slice_in_dim(
        jnp.pad(inflow, HALO), row_index * tile_rows, tile_rows + 2 * HALO
    )
    for turn_index in range(2):
        padded = apply_walls(
            state, HALO - 1 - turn_index, at_top, at_bottom, at_left, at_right,
            fine_inflow[turn_index: fine_inflow.shape[0] - turn_index],
        )
        inner = turn_index + 1
        coef = fine_coef[inner: fine_coef.shape[0] - inner, inner: fine_coef.shape[1] - inner]
        state = advance(padded, coef, fine_step)

    small = restrict(noise)
    coarse_coef = small[0, 1:-1, 1:-1]
    depth_coarse = 1.0 + 0.1 * small[1]
    coarse_state = jnp.stack([depth_coarse, 0.5 * depth_coarse, jnp.zeros_like(depth_coarse)])
    coarse_inflow = 0.5 + lax.dynamic_slice_in_dim(
        jnp.pad(pair_mean(inflow), 1), row_index * coarse_rows, coarse_rows + 2
    )
    padded = apply_walls(coarse_state, 0, at_top, at_bottom, at_left, at_right, coarse_inflow)
    coarse_state = advance(padded, coarse_coef, coarse_step)

    fine_mean = restrict(state)
    return (fine_mean[None], (fine_mean - coarse_state)[None])


def solution(mesh):
    in_specs = (P("level", "row", "col"), P("level", "row", "col"), P())
    out_specs = (P("level", None, "row", "col"), P("level", None, "row", "col"))
    return jax.shard_map(body, mesh=mesh, in_specs=in_specs, out_specs=out_specs, check_vma=False)
```

profile of v0, /device:TPU:31, one launch (start us, length us, event | category | flops | bytes accessed | tf_op | source)
XLA Modules:
  0.0 52.2 jit_solution(294704295870081650)
XLA Ops:
  0.6 1.0 %copy.50 = f32[1,64,256]{1,2,0:T(8,128)S(1)} copy(f32[1,64,256]{2,1,0:T(8,128)} %param.3) | data formatting | bytes 131072 | tf_op args[0]
  1.7 9.0 %collective-permute-start = (f32[2,64,2]{1,2,0:T(2,128)S(1)}, f32[2,64,2]{1,2,0:T(2,128)S(1)}, u32[]{:S(2)}, u32[]{:S(2)}) collective-permute-start(f32[2,64,2]{1,2,0:T(2,128)S(1)} %get-tuple-element.54), channel_id=1, source_target_pairs={{0,128},{128,1},{1,129},{129,2},{2,130},{130,3},{3,131},{131,4},{4... | collective-permute-start | bytes 3080 | tf_op jit(solution)/shard_map/ppermute | solution.py:100
  10.8 1.9 %collective-permute-start.1 = (f32[2,64,2]{1,2,0:T(2,128)S(1)}, f32[2,64,2]{1,2,0:T(2,128)S(1)}, u32[]{:S(2)}, u32[]{:S(2)}) collective-permute-start(f32[2,64,2]{1,2,0:T(2,128)S(1)} %get-tuple-element.55), channel_id=1, source_target_pairs={{128,0},{1,128},{129,1},{2,129},{130,2},{3,130},{131,3},{4,131},{1... | collective-permute-start | bytes 3080 | tf_op jit(solution)/shard_map/ppermute | solution.py:101
  12.9 0.8 %fusion.22 = f32[512]{0:T(512)} fusion(f32[512,2]{1,0:T(8,128)S(1)} %reshape.222), kind=kLoop, calls=%fused_computation.59 | loop fusion | flops 1024 | bytes 6144 | tf_op jit(solution)/shard_map/mul | solution.py:40
  13.7 8.0 %collective-permute-done.1 = f32[2,64,2]{1,2,0:T(2,128)S(1)} collective-permute-done((f32[2,64,2]{1,2,0:T(2,128)S(1)}, f32[2,64,2]{1,2,0:T(2,128)S(1)}, u32[]{:S(2)}, u32[]{:S(2)}) %collective-permute-start.1) | collective-permute-done | bytes 1056 | tf_op jit(solution)/shard_map/ppermute | solution.py:101
  21.9 2.6 %collective-permute-start.2 = (f32[2,2,260]{1,2,0:T(8,128)S(1)}, f32[2,2,260]{1,2,0:T(8,128)S(1)}, u32[]{:S(2)}, u32[]{:S(2)}) collective-permute-start(f32[2,2,260]{1,2,0:T(8,128)S(1)} %get-tuple-element.52), channel_id=1, source_target_pairs={{0,8},{8,16},{16,24},{24,32},{32,40},{40,48},{48,56},{56,64},{64,7... | collective-permute-start | bytes 12488 | tf_op jit(solution)/shard_map/ppermute | solution.py:103
  24.5 2.6 %collective-permute-start.3 = (f32[2,2,260]{1,2,0:T(8,128)S(1)}, f32[2,2,260]{1,2,0:T(8,128)S(1)}, u32[]{:S(2)}, u32[]{:S(2)}) collective-permute-start(f32[2,2,260]{1,2,0:T(8,128)S(1)} %get-tuple-element.53), channel_id=1, source_target_pairs={{8,0},{16,8},{24,16},{32,24},{40,32},{48,40},{56,48},{64,56},{72,6... | collective-permute-start | bytes 12488 | tf_op jit(solution)/shard_map/ppermute | solution.py:104
  27.2 0.6 %and_select_fusion = s32[256]{0:T(256)} fusion(), kind=kLoop, calls=%fused_computation.204 | loop fusion | flops 2048 | bytes 1024 | tf_op jit(solution)/shard_map/jit(floor_divide)/jit(_where)/select_n | solution.py:22
  27.9 1.2 %collective-permute-done.2 = f32[2,2,260]{1,2,0:T(8,128)S(1)} collective-permute-done((f32[2,2,260]{1,2,0:T(8,128)S(1)}, f32[2,2,260]{1,2,0:T(8,128)S(1)}, u32[]{:S(2)}, u32[]{:S(2)}) %collective-permute-start.2) | collective-permute-done | bytes 4192 | tf_op jit(solution)/shard_map/ppermute | solution.py:103
  29.1 4.8 %collective-permute-done.3 = f32[2,2,260]{1,2,0:T(8,128)S(1)} collective-permute-done((f32[2,2,260]{1,2,0:T(8,128)S(1)}, f32[2,2,260]{1,2,0:T(8,128)S(1)}, u32[]{:S(2)}, u32[]{:S(2)}) %collective-permute-start.3) | collective-permute-done | bytes 4192 | tf_op jit(solution)/shard_map/ppermute | solution.py:104
  34.3 0.3 convolution_multiply_fusion
  34.8 0.6 %copy-done.3 = f32[3,1,130]{2,1,0:T(1,128)} copy-done((f32[3,1,130]{2,1,0:T(1,128)}, f32[3,1,130]{2,1,0:T(1,128)S(1)}, u32[]{:S(2)}) %copy-start.3) | copy-done | bytes 1584
  35.4 0.8 %fusion.99 = (f32[1,34,1]{2,1,0:T(8,128)S(1)}, f32[34]{0:T(128)}) fusion(f32[3,34,130]{2,1,0:T(8,128)S(1)} %pad_maximum_fusion.21), kind=kLoop, calls=%fused_computation.223 | loop fusion | bytes 408 | tf_op jit(solution)/shard_map/slice | solution.py:60
  36.9 0.4 slice_select_fusion.2
  37.3 2.4 %concatenate.74 = f32[3,68,260]{1,2,0:T(8,128)S(1)} concatenate(f32[3,1,260]{1,2,0:T(8,128)S(1)} %get-tuple-element.48, f32[3,1,260]{1,2,0:T(8,128)S(1)} %get-tuple-element.19, f32[3,64,260]{1,2,0:T(8,128)S(1)} %slice.711, f32[3,1,260]{1,2,0:T(8,128)S(1)} %get-tuple-element.18, f32[3,1,260]{1,2,0:T(8,128)S(1)} %get-tuple-element.47), dimensions={1} | concatenate | bytes 424320 | tf_op jit(solution)/shard_map/concatenate | solution.py:53
  39.8 0.6 %copy-done.6 = f32[1024]{0:T(1024)S(1)} copy-done((f32[1024]{0:T(1024)S(1)}, f32[1024]{0:T(1024)}, u32[]{:S(2)}) %copy-start.6) | copy-done | bytes 4120
  40.5 0.6 %copy-done.8 = f32[3]{0:T(128)S(1)} copy-done((f32[3]{0:T(128)S(1)}, f32[3]{0:T(128)}, u32[]{:S(2)}) %copy-start.8) | copy-done | bytes 36
  41.2 0.5 concatenate.76
  42.2 0.3 fusion.12
  42.5 0.3 fusion.8
  42.8 0.3 fusion.6
  43.4 0.5 copy-done
  44.1 0.8 %slice-done = f32[1,66,258]{1,2,0:T(8,128)S(1)} async-done(((f32[3,66,258]{1,2,0:T(8,128)}), f32[1,66,258]{1,2,0:T(8,128)S(1)}, s32[]{:S(2)}) %slice-start) | async-done | bytes 68136 | tf_op jit(solution)/shard_map/slice | solution.py:90
  45.3 0.3 fusion.92
  46.4 0.4 fusion.19
  46.9 0.3 fusion.2
  47.2 0.3 fusion.16
  47.6 0.5 %copy-done.9 = f32[512]{0:T(512)S(1)} copy-done((f32[512]{0:T(512)S(1)}, f32[512]{0:T(512)}, u32[]{:S(2)}) %copy-start.9) | copy-done | bytes 2072
  48.7 0.7 %copy-done.4 = f32[3,1,130]{2,1,0:T(1,128)S(1)} copy-done((f32[3,1,130]{2,1,0:T(1,128)S(1)}, f32[3,1,130]{2,1,0:T(1,128)}, u32[]{:S(2)}) %copy-start.4) | copy-done | bytes 1584
  50.6 0.6 %copy-done.11 = s32[256]{0:T(256)S(1)} copy-done((s32[256]{0:T(256)S(1)}, s32[256]{0:T(256)}, u32[]{:S(2)}) %copy-start.11) | copy-done | bytes 1048
  51.2 0.3 convolution_multiply_fusion.1
  51.5 0.6 %fusion.65 = f32[1,3,32,128]{3,2,1,0:T(8,128)} fusion(f32[3,32,128]{2,1,0:T(8,128)S(1)} %convolution_multiply_fusion.1, f32[1,32,128]{2,1,0:T(8,128)S(1)} %get-tuple-element.79, f32[1,32,128]{2,1,0:T(8,128)S(1)} %get-tuple-element.2, f32[1,32,128]{2,1,0:T(8,128)S(1)} %get-tuple-element.78), kind=kLoop, calls=%fused_computation.155 | loop fusion | flops 36864 | bytes 147456 | tf_op jit(solution)/shard_map/broadcast_in_dim | solution.py:147
  (96 shorter events, 6.2 us)
Async XLA Ops:
  0.6 1.0 %copy-start.2 = (f32[1,64,256]{2,1,0:T(8,128)S(1)}, f32[1,64,256]{2,1,0:T(8,128)}, u32[]{:S(2)}) copy-start(f32[1,64,256]{2,1,0:T(8,128)} %param.4) | copy-start | bytes 196612
  1.7 11.0 %copy-start.5 = (f32[1024]{0:T(1024)S(1)}, f32[1024]{0:T(1024)}, u32[]{:S(2)}) copy-start(f32[1024]{0:T(1024)} %param.5) | copy-start | bytes 12292
  1.7 12.0 %collective-permute-start = (f32[2,64,2]{1,2,0:T(2,128)S(1)}, f32[2,64,2]{1,2,0:T(2,128)S(1)}, u32[]{:S(2)}, u32[]{:S(2)}) collective-permute-start(f32[2,64,2]{1,2,0:T(2,128)S(1)} %get-tuple-element.54), channel_id=1, source_target_pairs={{0,128},{128,1},{1,129},{129,2},{2,130},{130,3},{3,131},{131,4},{4... | collective-permute-start | bytes 3080 | tf_op jit(solution)/shard_map/ppermute | solution.py:100
  10.8 10.9 %collective-permute-start.1 = (f32[2,64,2]{1,2,0:T(2,128)S(1)}, f32[2,64,2]{1,2,0:T(2,128)S(1)}, u32[]{:S(2)}, u32[]{:S(2)}) collective-permute-start(f32[2,64,2]{1,2,0:T(2,128)S(1)} %get-tuple-element.55), channel_id=1, source_target_pairs={{128,0},{1,128},{129,1},{2,129},{130,2},{3,130},{131,3},{4,131},{1... | collective-permute-start | bytes 3080 | tf_op jit(solution)/shard_map/ppermute | solution.py:101
  21.9 7.2 %collective-permute-start.2 = (f32[2,2,260]{1,2,0:T(8,128)S(1)}, f32[2,2,260]{1,2,0:T(8,128)S(1)}, u32[]{:S(2)}, u32[]{:S(2)}) collective-permute-start(f32[2,2,260]{1,2,0:T(8,128)S(1)} %get-tuple-element.52), channel_id=1, source_target_pairs={{0,8},{8,16},{16,24},{24,32},{32,40},{40,48},{48,56},{56,64},{64,7... | collective-permute-start | bytes 12488 | tf_op jit(solution)/shard_map/ppermute | solution.py:103
  24.5 9.3 %collective-permute-start.3 = (f32[2,2,260]{1,2,0:T(8,128)S(1)}, f32[2,2,260]{1,2,0:T(8,128)S(1)}, u32[]{:S(2)}, u32[]{:S(2)}) collective-permute-start(f32[2,2,260]{1,2,0:T(8,128)S(1)} %get-tuple-element.53), channel_id=1, source_target_pairs={{8,0},{16,8},{24,16},{32,24},{40,32},{48,40},{56,48},{64,56},{72,6... | collective-permute-start | bytes 12488 | tf_op jit(solution)/shard_map/ppermute | solution.py:104
  27.8 8.5 %copy-start.7 = (f32[3]{0:T(128)}, f32[3]{0:T(128)S(1)}, u32[]{:S(2)}) copy-start(f32[3]{0:T(128)S(1)} %pad.108.clone) | copy-start | bytes 40
  34.8 0.6 %copy-start.3 = (f32[3,1,130]{2,1,0:T(1,128)}, f32[3,1,130]{2,1,0:T(1,128)S(1)}, u32[]{:S(2)}) copy-start(f32[3,1,130]{2,1,0:T(1,128)S(1)} %get-tuple-element.65) | copy-start | bytes 4684
  39.7 0.7 %copy-start.6 = (f32[1024]{0:T(1024)S(1)}, f32[1024]{0:T(1024)}, u32[]{:S(2)}) copy-start(f32[1024]{0:T(1024)} %param.5) | copy-start | bytes 12292
  40.5 0.6 %copy-start.8 = (f32[3]{0:T(128)S(1)}, f32[3]{0:T(128)}, u32[]{:S(2)}) copy-start(f32[3]{0:T(128)} %copy-done.7) | copy-start | bytes 40
  43.1 0.7 %copy-start = (f32[3,66,258]{1,2,0:T(8,128)}, f32[3,66,258]{1,2,0:T(8,128)S(1)}, u32[]{:S(2)}) copy-start(f32[3,66,258]{1,2,0:T(8,128)S(1)} %fusion.6) | copy-start | bytes 613012
  44.0 0.9 %slice-start = ((f32[3,66,258]{1,2,0:T(8,128)}), f32[1,66,258]{1,2,0:T(8,128)S(1)}, s32[]{:S(2)}) async-start(f32[3,66,258]{1,2,0:T(8,128)} %copy-done), calls=%async_computation | async-start | bytes 270336 | tf_op jit(solution)/shard_map/slice | solution.py:90
  47.4 0.7 %copy-start.9 = (f32[512]{0:T(512)S(1)}, f32[512]{0:T(512)}, u32[]{:S(2)}) copy-start(f32[512]{0:T(512)} %fusion.22) | copy-start | bytes 6148
  47.6 0.7 %copy-start.10 = (f32[34]{0:T(128)S(1)}, f32[34]{0:T(128)}, u32[]{:S(2)}) copy-start(f32[34]{0:T(128)} %get-tuple-element.69) | copy-start | bytes 412
  48.7 0.7 %copy-start.4 = (f32[3,1,130]{2,1,0:T(1,128)S(1)}, f32[3,1,130]{2,1,0:T(1,128)}, u32[]{:S(2)}) copy-start(f32[3,1,130]{2,1,0:T(1,128)} %copy-done.3) | copy-start | bytes 4684
  50.6 0.7 %copy-start.11 = (s32[256]{0:T(256)S(1)}, s32[256]{0:T(256)}, u32[]{:S(2)}) copy-start(s32[256]{0:T(256)} %and_select_fusion) | copy-start | bytes 3076
  51.5 0.7 %copy-start.1 = (f32[3,32,128]{2,1,0:T(8,128)}, f32[3,32,128]{2,1,0:T(8,128)S(1)}, u32[]{:S(2)}) copy-start(f32[3,32,128]{2,1,0:T(8,128)S(1)} %convolution_multiply_fusion.1) | copy-start | bytes 147460
where the time goes:
time: 52.6 us; the launch traced here: 52.2 us
  starting transfers between devices  16.2 us (31%)
  waiting for transfers between devices  13.9 us (26%)
  local copies, waits for them, and re-layouts  11.9 us (23%)
  other arithmetic  8.4 us (16%)
  between operations  1.2 us (2%)
  matrix products  0.55 us (1%)
    ppermute x1, starting transfers between devices, with_halo(): lax.ppermute(noise[:, :, -HALO:], across, shift_pairs(strips, 1, strip_pl...  9.04 us
    ppermute x1, waiting for transfers between devices, with_halo(): lax.ppermute(noise[:, :, :HALO], across, shift_pairs(strips, -1, strip_pl...  7.97 us
    unnamed x26, local copies, waits for them, and re-layouts  5.31 us
    ppermute x1, waiting for transfers between devices, with_halo(): south = lax.ppermute(wide[:, :HALO, :], 'row', shift_pairs(rows, -1))  4.76 us
    ppermute x1, starting transfers between devices, with_halo(): north = lax.ppermute(wide[:, -HALO:, :], 'row', shift_pairs(rows, 1))  2.65 us
    ppermute x1, starting transfers between devices, with_halo(): south = lax.ppermute(wide[:, :HALO, :], 'row', shift_pairs(rows, -1))  2.64 us
    concatenate x1, local copies, waits for them, and re-layouts, apply_walls(): jnp.concatenate([padded[:, :layer], top[:, None], padded[:, layer + 1:low...  2.42 us
    ppermute x1, starting transfers between devices, with_halo(): lax.ppermute(noise[:, :, :HALO], across, shift_pairs(strips, -1, strip_pl...  1.92 us
  transfers between devices with their start and end apart: 4, of which 3 were waited for; matrix products, arithmetic and copies ran while one was open for 3% of the time, Pallas kernels for 0%

commit v1 on v0

v1 whole, which is shorter than its diff:
```python
import jax
import jax.numpy as jnp
from jax import lax
from jax.experimental import pallas as pl
from jax.experimental.pallas import tpu as pltpu
from jax.sharding import PartitionSpec as P

step_ratio = 0.15
fine_step = 0.15
coarse_step = 0.3
HALO = 2
FINE_SHAPE = (72, 384)
COARSE_SHAPE = (40, 256)


def shift_pairs(count, delta, place=lambda i: i):
    return [(place(i), place(i + delta)) for i in range(count) if 0 <= i + delta < count]


def strip_place(strip):
    levels = lax.axis_size("level")
    return (strip % levels) * lax.axis_size("col") + strip // levels


def pair_mean(values):
    paired = values.reshape(-1, 2)
    return (paired[:, 0] + paired[:, 1]) * 0.5


def with_halo(noise):
    fields, count_rows, count_cols = noise.shape
    strips = lax.axis_size("col") * lax.axis_size("level")
    rows = lax.axis_size("row")
    across = ("level", "col")
    west = lax.ppermute(noise[:, :, -HALO:], across, shift_pairs(strips, 1, strip_place))
    east = lax.ppermute(noise[:, :, :HALO], across, shift_pairs(strips, -1, strip_place))
    gap_cols = FINE_SHAPE[1] - count_cols - 2 * HALO
    wide = jnp.concatenate(
        [noise, east, jnp.zeros((fields, count_rows, gap_cols), noise.dtype), west], axis=2
    )
    north = lax.ppermute(wide[:, -HALO:, :], "row", shift_pairs(rows, 1))
    south = lax.ppermute(wide[:, :HALO, :], "row", shift_pairs(rows, -1))
    gap_rows = FINE_SHAPE[0] - count_rows - 2 * HALO
    return jnp.concatenate(
        [wide, south, jnp.zeros((fields, gap_rows, FINE_SHAPE[1]), noise.dtype), north], axis=1
    )


def wrapped_rows(values, start, count, lead):
    padded = jnp.pad(values, lead)
    window = lax.dynamic_slice_in_dim(padded, start, count)
    return (0.5 + jnp.roll(window, -lead)).reshape(count, 1)


def next_of(values, axis):
    return pltpu.roll(values, values.shape[axis] - 1, axis)


def prev_of(values, axis):
    return pltpu.roll(values, 1, axis)


def apply_walls(state, flags, inflow_speed, bottom_row, right_col):
    depth, along_cols, along_rows = state
    shape = depth.shape
    row_at = lax.broadcasted_iota(jnp.int32, shape, 0)
    col_at = lax.broadcasted_iota(jnp.int32, shape, 1)
    top = jnp.logical_and(row_at == shape[0] - 1, flags[0] == 1)
    bottom = jnp.logical_and(row_at == bottom_row, flags[1] == 1)
    left = jnp.logical_and(col_at == shape[1] - 1, flags[2] == 1)
    right = jnp.logical_and(col_at == right_col, flags[3] == 1)

    def rows_fixed(values, sign):
        below = next_of(values, 0)
        above = prev_of(values, 0)
        if sign < 0:
            below = -below
            above = -above
        return jnp.where(top, below, jnp.where(bottom, above, values))

    depth = rows_fixed(depth, 1)
    along_cols = rows_fixed(along_cols, 1)
    along_rows = rows_fixed(along_rows, -1)
    source = next_of(depth, 1)
    entering = (source, source * inflow_speed, jnp.zeros_like(source))
    fixed = []
    for values, inflowing in zip((depth, along_cols, along_rows), entering):
        fixed.append(jnp.where(left, inflowing, jnp.where(right, prev_of(values, 1), values)))
    return tuple(fixed)


def face_flux(state, flux, speed, axis):
    reach = 0.5 * jnp.maximum(next_of(speed, axis), speed)
    return [
        0.5 * (next_of(f, axis) + f) - reach * (next_of(u, axis) - u)
        for f, u in zip(flux, state)
    ]


def advance(state, friction_coef, step):
    depth, along_cols, along_rows = state
    velocity = along_cols / depth
    flux = (along_cols, along_cols * velocity + 0.5 * depth * depth, along_rows * velocity)
    face_x = face_flux(state, flux, jnp.abs(velocity) + jnp.sqrt(depth), 1)
    velocity = along_rows / depth
    flux = (along_rows, along_cols * velocity, along_rows * velocity + 0.5 * depth * depth)
    face_y = face_flux(state, flux, jnp.abs(velocity) + jnp.sqrt(depth), 0)
    moved = [
        u - step_ratio * (fx - prev_of(fx, 1) + (fy - prev_of(fy, 0)))
        for u, fx, fy in zip(state, face_x, face_y)
    ]
    depth = moved[0]
    speed = jnp.sqrt(moved[1] * moved[1] + moved[2] * moved[2]) / depth
    damping = 1.0 / (1.0 + step * friction_coef * speed / depth)
    return (depth, moved[1] * damping, moved[2] * damping)


def pair_matrix(shape, out_axis, last_from):
    out_at = lax.broadcasted_iota(jnp.int32, shape, out_axis)
    in_at = lax.broadcasted_iota(jnp.int32, shape, 1 - out_axis)
    hit = jnp.right_shift(in_at, 1) == out_at
    if last_from is not None:
        last = shape[out_axis] - 1
        hit = jnp.logical_or(hit, jnp.logical_and(out_at == last, in_at >= last_from))
    return hit.astype(jnp.float32)


def matmul(a, b):
    return jnp.dot(a, b, precision=lax.Precision.HIGHEST, preferred_element_type=jnp.float32)


def level_kernel(flags_ref, noise_ref, fine_inflow_ref, coarse_inflow_ref, mean_ref, corr_ref):
    flags = [flags_ref[i] for i in range(4)]
    fine_rows, fine_cols = FINE_SHAPE
    coarse_rows, coarse_cols = COARSE_SHAPE
    out_rows, out_cols = mean_ref.shape[1], mean_ref.shape[2]
    tile_rows, tile_cols = 2 * out_rows, 2 * out_cols

    fine_coef = noise_ref[0]
    noise_height = noise_ref[1]
    depth = 1.0 + 0.1 * noise_height
    state = (depth, 0.5 * depth, jnp.zeros_like(depth))
    fine_inflow = jnp.broadcast_to(fine_inflow_ref[...], FINE_SHAPE)
    for _ in range(2):
        state = apply_walls(state, flags, fine_inflow, tile_rows, tile_cols)
        state = advance(state, fine_coef, fine_step)

    rows_sum = pair_matrix((coarse_rows, fine_rows), 0, fine_rows - 2)
    cols_sum = pair_matrix((fine_cols, coarse_cols), 1, fine_cols - 2)
    coarse_coef = matmul(matmul(rows_sum, fine_coef), cols_sum) * 0.25
    depth = 1.0 + 0.1 * (matmul(matmul(rows_sum, noise_height), cols_sum) * 0.25)
    coarse = (depth, 0.5 * depth, jnp.zeros_like(depth))
    coarse_inflow = jnp.broadcast_to(coarse_inflow_ref[...], COARSE_SHAPE)
    coarse = apply_walls(coarse, flags, coarse_inflow, out_rows, out_cols)
    coarse = advance(coarse, coarse_coef, coarse_step)

    rows_out = pair_matrix((out_rows, tile_rows), 0, None)
    cols_out = pair_matrix((tile_cols, out_cols), 1, None)
    for field in range(3):
        fine_part = state[field][:tile_rows, :tile_cols]
        mean = matmul(matmul(rows_out, fine_part), cols_out) * 0.25
        mean_ref[field] = mean
        corr_ref[field] = mean - coarse[field][:out_rows, :out_cols]


def body(friction, height, inflow):
    strip = lax.axis_index("col") * lax.axis_size("level") + lax.axis_index("level")
    strips = lax.axis_size("col") * lax.axis_size("level")
    row_index = lax.axis_index("row")
    flags = jnp.stack(
        [row_index == 0, row_index == lax.axis_size("row") - 1, strip == 0, strip == strips - 1]
    ).astype(jnp.int32)
    tile_rows, tile_cols = friction.shape[1], friction.shape[2]
    out_rows, out_cols = tile_rows // 2, tile_cols // 2

    noise = with_halo(jnp.concatenate([friction, height], axis=0))
    lead = FINE_SHAPE[0] - tile_rows - HALO
    fine_inflow = wrapped_rows(inflow, row_index * tile_rows, FINE_SHAPE[0], lead)
    lead = COARSE_SHAPE[0] - out_rows - 1
    coarse_inflow = wrapped_rows(pair_mean(inflow), row_index * out_rows, COARSE_SHAPE[0], lead)

    out = jax.ShapeDtypeStruct((3, out_rows, out_cols), jnp.float32)
    vmem = pl.BlockSpec(memory_space=pltpu.VMEM)
    mean, corr = pl.pallas_call(
        level_kernel,
        out_shape=(out, out),
        in_specs=[pl.BlockSpec(memory_space=pltpu.SMEM), vmem, vmem, vmem],
        out_specs=(vmem, vmem),
    )(flags, noise, fine_inflow, coarse_inflow)
    return (mean[None], corr[None])


def solution(mesh):
    in_specs = (P("level", "row", "col"), P("level", "row", "col"), P())
    out_specs = (P("level", None, "row", "col"), P("level", None, "row", "col"))
    return jax.shard_map(body, mesh=mesh, in_specs=in_specs, out_specs=out_specs, check_vma=False)
```

time: 52.6 us -> 36 us (0.68)
  local copies, waits for them, and re-layouts: 11.9 us -> 2.44 us
  other arithmetic: 8.4 us -> 3.15 us
  waiting for transfers between devices: 13.9 us -> 9.72 us
  Pallas kernels: 0 us -> 3.52 us
  matrix products: 0.55 us -> 0 us
    unnamed x26 -> x5, local copies, waits for them, and re-layouts: 5.31 us -> 1.56 us
    pallas_call x0 -> x1, Pallas kernels: none -> 3.52 us  [body(): pl.pallas_call(level_kernel, out_shape=(out, out), in_specs=[pl.BlockSpec...]
    concatenate x3 -> x8, local copies, waits for them, and re-layouts: 3.1 us -> 0.43 us  [the longest x6 0.35 us: wrapped_rows(): return (0.5 + jnp.roll(window, -lead)).reshape(count, 1)]
    slice x17 -> x1, local copies, waits for them, and re-layouts: 2.72 us -> 0.08 us  [with_halo(): noise[:, :, :HALO]]
    sub x9 -> x0, other arithmetic: 2.15 us -> none  [the longest x3 0.78 us: advance(): 0.5 * (flux[:, 1:, :] + flux[:, :-1, :])]
    ppermute x1, waiting for transfers between devices: 4.76 us -> 3.06 us  [with_halo(): south = lax.ppermute(wide[:, :HALO, :], 'row', shift_pairs(rows, -1))]
    select_n x7 -> x0, other arithmetic: 1.44 us -> none  [the longest x3 0.68 us: apply_walls(): bottom = jnp.where(at_bottom, mirror, padded[:, low, :])]
    ppermute x1, waiting for transfers between devices: 7.97 us -> 6.65 us  [with_halo(): lax.ppermute(noise[:, :, :HALO], across, shift_pairs(strips, -1, strip_pl...]
  transfers between devices with their start and end apart: 4 -> 4, of which waited for: 3 -> 2; matrix products, arithmetic and copies ran while one was open for 3% -> 9% of each run, Pallas kernels for 0% -> 0%
where the time goes in v1:
time: 36 us; the launch traced here: 35.8 us
  starting transfers between devices  16.2 us (45%)
  waiting for transfers between devices  9.72 us (27%)
  Pallas kernels  3.52 us (10%)
  other arithmetic  3.15 us (9%)
  local copies, waits for them, and re-layouts  2.44 us (7%)
  between operations  0.71 us (2%)
    ppermute x1, starting transfers between devices, with_halo(): lax.ppermute(noise[:, :, -HALO:], across, shift_pairs(strips, 1, strip_pl...  9.03 us
    ppermute x1, waiting for transfers between devices, with_halo(): lax.ppermute(noise[:, :, :HALO], across, shift_pairs(strips, -1, strip_pl...  6.65 us
    pallas_call x1, Pallas kernels, body(): pl.pallas_call(level_kernel, out_shape=(out, out), in_specs=[pl.BlockSpec...  3.52 us
    ppermute x1, waiting for transfers between devices, with_halo(): south = lax.ppermute(wide[:, :HALO, :], 'row', shift_pairs(rows, -1))  3.06 us
    ppermute x1, starting transfers between devices, with_halo(): south = lax.ppermute(wide[:, :HALO, :], 'row', shift_pairs(rows, -1))  2.66 us
    ppermute x1, starting transfers between devices, with_halo(): north = lax.ppermute(wide[:, -HALO:, :], 'row', shift_pairs(rows, 1))  2.62 us
    ppermute x1, starting transfers between devices, with_halo(): lax.ppermute(noise[:, :, :HALO], across, shift_pairs(strips, -1, strip_pl...  1.92 us
    unnamed x5, local copies, waits for them, and re-layouts  1.56 us
  transfers between devices with their start and end apart: 4, of which 2 were waited for; matrix products, arithmetic and copies ran while one was open for 9% of the time, Pallas kernels for 0%

profile of v1, /device:TPU:31, one launch (start us, length us, event | category | flops | bytes accessed | tf_op | source)
XLA Modules:
  0.0 35.8 jit_solution(1912875399175474945)
XLA Ops:
  0.6 0.0 copy-start
  0.6 0.9 %constant_dynamic-update-slice_fusion.1 = f32[2,64,256]{2,1,0:T(8,128)S(1)} fusion(f32[1,64,256]{2,1,0:T(8,128)} %param.3), kind=kLoop, calls=%fused_computation.12 | loop fusion | bytes 131072
  1.5 0.0 copy-done
  1.5 0.1 fusion.2
  1.6 9.0 %collective-permute-start.1 = (f32[2,64,2]{2,1,0:T(8,128)S(1)}, f32[2,64,2]{2,1,0:T(8,128)S(1)}, u32[]{:S(2)}, u32[]{:S(2)}) collective-permute-start(f32[2,64,2]{2,1,0:T(8,128)S(1)} %get-tuple-element.9), channel_id=1, source_target_pairs={{0,128},{128,1},{1,129},{129,2},{2,130},{130,3},{3,131},{131,4},{4... | collective-permute-start | bytes 3080 | tf_op jit(solution)/shard_map/ppermute | solution.py:35
  10.6 1.9 %collective-permute-start = (f32[2,64,2]{2,1,0:T(8,128)S(1)}, f32[2,64,2]{2,1,0:T(8,128)S(1)}, u32[]{:S(2)}, u32[]{:S(2)}) collective-permute-start(f32[2,64,2]{2,1,0:T(8,128)S(1)} %get-tuple-element.8), channel_id=1, source_target_pairs={{128,0},{1,128},{129,1},{2,129},{130,2},{3,130},{131,3},{4,131},{1... | collective-permute-start | bytes 3080 | tf_op jit(solution)/shard_map/ppermute | solution.py:36
  12.6 0.0 copy-start.1
  12.6 0.7 %copy-done.1 = f32[1024]{0:T(1024)S(1)} copy-done((f32[1024]{0:T(1024)S(1)}, f32[1024]{0:T(1024)}, u32[]{:S(2)}) %copy-start.1) | copy-done | bytes 4120
  13.3 0.1 pad_dynamic-slice_fusion
  13.4 0.1 slice_bitcast_fusion.3
  13.4 0.2 reshape.70
  13.6 0.2 fusion.1
  13.9 0.1 pad_dynamic-slice_fusion.1
  14.0 0.1 slice_bitcast_fusion.1
  14.0 0.1 pad_maximum_fusion.5
  14.1 0.1 copy.15
  14.2 0.6 %broadcast_add_fusion.fine_inflow_ref = f32[72,1]{1,0:T(8,128)} fusion(f32[72,1]{1,0:T(8,128)S(1)} %copy.15), kind=kLoop, calls=%fused_computation.4 | loop fusion | flops 72 | bytes 576 | tf_op jit(solution)/shard_map/add | solution.py:52
  14.8 0.1 pad_maximum_fusion.6
  14.9 0.1 copy.17
  15.0 0.6 %broadcast_add_fusion.1.coarse_inflow_ref = f32[40,1]{1,0:T(8,128)} fusion(f32[40,1]{1,0:T(8,128)S(1)} %copy.17), kind=kLoop, calls=%fused_computation.5 | loop fusion | flops 40 | bytes 320 | tf_op jit(solution)/shard_map/add | solution.py:52
  15.6 0.0 collective-permute-done.1
  15.6 6.7 %collective-permute-done = f32[2,64,2]{2,1,0:T(8,128)S(1)} collective-permute-done((f32[2,64,2]{2,1,0:T(8,128)S(1)}, f32[2,64,2]{2,1,0:T(8,128)S(1)}, u32[]{:S(2)}, u32[]{:S(2)}) %collective-permute-start) | collective-permute-done | bytes 1056 | tf_op jit(solution)/shard_map/ppermute | solution.py:36
  22.3 0.1 pad_maximum_fusion.4
  22.3 2.6 %collective-permute-start.3 = (f32[2,2,384]{2,1,0:T(2,128)S(1)}, f32[2,2,384]{2,1,0:T(2,128)S(1)}, u32[]{:S(2)}, u32[]{:S(2)}) collective-permute-start(f32[2,2,384]{2,1,0:T(2,128)S(1)} %get-tuple-element.7), channel_id=1, source_target_pairs={{0,8},{8,16},{16,24},{24,32},{32,40},{40,48},{48,56},{56,64},{64,7... | collective-permute-start | bytes 18440 | tf_op jit(solution)/shard_map/ppermute | solution.py:41
  25.0 2.7 %collective-permute-start.2 = (f32[2,2,384]{2,1,0:T(2,128)S(1)}, f32[2,2,384]{2,1,0:T(2,128)S(1)}, u32[]{:S(2)}, u32[]{:S(2)}) collective-permute-start(f32[2,2,384]{2,1,0:T(2,128)S(1)} %get-tuple-element.6), channel_id=1, source_target_pairs={{8,0},{16,8},{24,16},{32,24},{40,32},{48,40},{56,48},{64,56},{72,6... | collective-permute-start | bytes 18440 | tf_op jit(solution)/shard_map/ppermute | solution.py:42
  27.6 0.7 %add_convert_fusion.flags_ref = s32[4]{0:T(128)} fusion(pred[1]{0:T(512)(128)(4,1)} %bitcast.3, pred[1]{0:T(512)(128)(4,1)} %bitcast.2, pred[1]{0:T(512)(128)(4,1)} %bitcast.1, pred[1]{0:T(512)(128)(4,1)} %bitcast), kind=kLoop, calls=%fused_computation.14 | loop fusion | flops 16 | bytes 20 | tf_op jit(solution)/shard_map/convert_element_type | solution.py:172
  28.3 0.1 pad.19.clone
  28.4 0.0 collective-permute-done.3
  28.4 3.1 %collective-permute-done.2 = f32[2,2,384]{2,1,0:T(2,128)S(1)} collective-permute-done((f32[2,2,384]{2,1,0:T(2,128)S(1)}, f32[2,2,384]{2,1,0:T(2,128)S(1)}, u32[]{:S(2)}, u32[]{:S(2)}) %collective-permute-start.2) | collective-permute-done | bytes 6176 | tf_op jit(solution)/shard_map/ppermute | solution.py:42
  31.4 0.8 %pad_maximum_fusion.noise_ref = f32[2,72,384]{2,1,0:T(8,128)} fusion(f32[2,2,384]{2,1,0:T(2,128)S(1)} %collective-permute-done.3, f32[2,2,384]{2,1,0:T(2,128)S(1)} %collective-permute-done.2, f32[2,64,2]{2,1,0:T(8,128)S(1)} %collective-permute-done.1, f32[2,64,124]{2,1,0:T(8,128)S(1)} %broadcast_in_dim.12, f32[2,64,2]{2,1,0:T(8,128)S(1)} %collective-permute-done, ...), kind=kLoop, calls=%fused_computation.3 | loop fusion | flops 331776 | bytes 430368 | tf_op jit(solution)/shard_map/concatenate | solution.py:44
  32.2 3.5 %shard_map.50 = (f32[3,32,128]{2,1,0:T(8,128)}, f32[3,32,128]{2,1,0:T(8,128)}) custom-call(s32[4]{0:T(128)} %add_convert_fusion.flags_ref, f32[2,72,384]{2,1,0:T(8,128)} %pad_maximum_fusion.noise_ref, f32[72,1]{1,0:T(8,128)} %broadcast_add_fusion.fine_inflow_ref, f32[40,1]{1,0:T(8,128)} %broadcast_add_fusion.1.coarse_inflow_ref), custom_call_target="tpu_custom_call" | custom-call | tf_op jit(solution)/shard_map/pallas_call | solution.py:184
  (5 shorter events, 0.0 us)
Async XLA Ops:
  0.6 0.9 %copy-start = (f32[1,64,256]{2,1,0:T(8,128)S(1)}, f32[1,64,256]{2,1,0:T(8,128)}, u32[]{:S(2)}) copy-start(f32[1,64,256]{2,1,0:T(8,128)} %param.4) | copy-start | bytes 196612
  1.6 14.0 %collective-permute-start.1 = (f32[2,64,2]{2,1,0:T(8,128)S(1)}, f32[2,64,2]{2,1,0:T(8,128)S(1)}, u32[]{:S(2)}, u32[]{:S(2)}) collective-permute-start(f32[2,64,2]{2,1,0:T(8,128)S(1)} %get-tuple-element.9), channel_id=1, source_target_pairs={{0,128},{128,1},{1,129},{129,2},{2,130},{130,3},{3,131},{131,4},{4... | collective-permute-start | bytes 3080 | tf_op jit(solution)/shard_map/ppermute | solution.py:35
  10.6 11.6 %collective-permute-start = (f32[2,64,2]{2,1,0:T(8,128)S(1)}, f32[2,64,2]{2,1,0:T(8,128)S(1)}, u32[]{:S(2)}, u32[]{:S(2)}) collective-permute-start(f32[2,64,2]{2,1,0:T(8,128)S(1)} %get-tuple-element.8), channel_id=1, source_target_pairs={{128,0},{1,128},{129,1},{2,129},{130,2},{3,130},{131,3},{4,131},{1... | collective-permute-start | bytes 3080 | tf_op jit(solution)/shard_map/ppermute | solution.py:36
  12.6 0.7 %copy-start.1 = (f32[1024]{0:T(1024)S(1)}, f32[1024]{0:T(1024)}, u32[]{:S(2)}) copy-start(f32[1024]{0:T(1024)} %param.5) | copy-start | bytes 12292
  22.3 6.0 %collective-permute-start.3 = (f32[2,2,384]{2,1,0:T(2,128)S(1)}, f32[2,2,384]{2,1,0:T(2,128)S(1)}, u32[]{:S(2)}, u32[]{:S(2)}) collective-permute-start(f32[2,2,384]{2,1,0:T(2,128)S(1)} %get-tuple-element.7), channel_id=1, source_target_pairs={{0,8},{8,16},{16,24},{24,32},{32,40},{40,48},{48,56},{56,64},{64,7... | collective-permute-start | bytes 18440 | tf_op jit(solution)/shard_map/ppermute | solution.py:41
  25.0 6.5 %collective-permute-start.2 = (f32[2,2,384]{2,1,0:T(2,128)S(1)}, f32[2,2,384]{2,1,0:T(2,128)S(1)}, u32[]{:S(2)}, u32[]{:S(2)}) collective-permute-start(f32[2,2,384]{2,1,0:T(2,128)S(1)} %get-tuple-element.6), channel_id=1, source_target_pairs={{8,0},{16,8},{24,16},{32,24},{40,32},{48,40},{56,48},{64,56},{72,6... | collective-permute-start | bytes 18440 | tf_op jit(solution)/shard_map/ppermute | solution.py:42

commit v2 on v1

--- a/solution.py
+++ b/solution.py
@@ -13,15 +13,6 @@
 COARSE_SHAPE = (40, 256)
 
 
-def shift_pairs(count, delta, place=lambda i: i):
-    return [(place(i), place(i + delta)) for i in range(count) if 0 <= i + delta < count]
-
-
-def strip_place(strip):
-    levels = lax.axis_size("level")
-    return (strip % levels) * lax.axis_size("col") + strip // levels
-
-
 def pair_mean(values):
     paired = values.reshape(-1, 2)
     return (paired[:, 0] + paired[:, 1]) * 0.5
@@ -29,20 +20,45 @@
 
 def with_halo(noise):
     fields, count_rows, count_cols = noise.shape
-    strips = lax.axis_size("col") * lax.axis_size("level")
-    rows = lax.axis_size("row")
-    across = ("level", "col")
-    west = lax.ppermute(noise[:, :, -HALO:], across, shift_pairs(strips, 1, strip_place))
-    east = lax.ppermute(noise[:, :, :HALO], across, shift_pairs(strips, -1, strip_place))
+    levels, cols, rows = lax.axis_size("level"), lax.axis_size("col"), lax.axis_size("row")
+    strips = levels * cols
+
+    def place(row, strip):
+        return ((strip % levels) * rows + row) * cols + strip // levels
+
+    def sent(block, down, right):
+        pairs = [
+            (place(r, s), place(r + down, s + right))
+            for r in range(rows) for s in range(strips)
+            if 0 <= r + down < rows and 0 <= s + right < strips
+        ]
+        return lax.ppermute(block, ("level", "row", "col"), pairs)
+
+    top, low = slice(0, HALO), slice(count_rows - HALO, count_rows)
+    first, last = slice(0, HALO), slice(count_cols - HALO, count_cols)
+    west = sent(noise[:, :, last], 0, 1)
+    east = sent(noise[:, :, first], 0, -1)
+    north = sent(noise[:, low, :], 1, 0)
+    south = sent(noise[:, top, :], -1, 0)
+    north_west = sent(noise[:, low, last], 1, 1)
+    north_east = sent(noise[:, low, first], 1, -1)
+    south_west = sent(noise[:, top, last], -1, 1)
+    south_east = sent(noise[:, top, first], -1, -1)
     gap_cols = FINE_SHAPE[1] - count_cols - 2 * HALO
-    wide = jnp.concatenate(
-        [noise, east, jnp.zeros((fields, count_rows, gap_cols), noise.dtype), west], axis=2
-    )
-    north = lax.ppermute(wide[:, -HALO:, :], "row", shift_pairs(rows, 1))
-    south = lax.ppermute(wide[:, :HALO, :], "row", shift_pairs(rows, -1))
+
+    def band(middle, after, before):
+        gap = jnp.zeros(middle.shape[:2] + (gap_cols,), noise.dtype)
+        return jnp.concatenate([middle, after, gap, before], axis=2)
+
     gap_rows = FINE_SHAPE[0] - count_rows - 2 * HALO
     return jnp.concatenate(
-        [wide, south, jnp.zeros((fields, gap_rows, FINE_SHAPE[1]), noise.dtype), north], axis=1
+        [
+            band(noise, east, west),
+            band(south, south_east, south_west),
+            jnp.zeros((fields, gap_rows, FINE_SHAPE[1]), noise.dtype),
+            band(north, north_east, north_west),
+        ],
+        axis=1,
     )
 
 

time: 36 us -> 61.2 us (1.70)
  starting transfers between devices: 16.2 us -> 29.3 us
  waiting for transfers between devices: 9.72 us -> 21.6 us
    ppermute x4 -> x8, starting transfers between devices: 16.2 us -> 29.3 us  [sent(): return lax.ppermute(block, ('level', 'row', 'col'), pairs)]
    ppermute x4 -> x8, waiting for transfers between devices: 9.72 us -> 21.6 us  [sent(): return lax.ppermute(block, ('level', 'row', 'col'), pairs)]
  transfers between devices with their start and end apart: 4 -> 8, of which waited for: 2 -> 3; matrix products, arithmetic and copies ran while one was open for 9% -> 5% of each run, Pallas kernels for 0% -> 0%
where the time goes in v2:
time: 61.2 us; the launch traced here: 60.8 us
  starting transfers between devices  29.3 us (48%)
  waiting for transfers between devices  21.6 us (35%)
  Pallas kernels  3.52 us (6%)
  other arithmetic  3.02 us (5%)
  local copies, waits for them, and re-layouts  2.6 us (4%)
  between operations  0.78 us (1%)
    ppermute x8, starting transfers between devices, sent(): return lax.ppermute(block, ('level', 'row', 'col'), pairs)  29.3 us
    ppermute x8, waiting for transfers between devices, sent(): return lax.ppermute(block, ('level', 'row', 'col'), pairs)  21.6 us
    pallas_call x1, Pallas kernels, body(): pl.pallas_call(level_kernel, out_shape=(out, out), in_specs=[pl.BlockSpec...  3.52 us
    unnamed x5, local copies, waits for them, and re-layouts  1.56 us
  transfers between devices with their start and end apart: 8, of which 3 were waited for; matrix products, arithmetic and copies ran while one was open for 5% of the time, Pallas kernels for 0%

profile of v2, /device:TPU:31, one launch (start us, length us, event | category | flops | bytes accessed | tf_op | source)
XLA Modules:
  0.0 60.8 jit_solution(7135691493004556204)
XLA Ops:
  0.6 0.9 %constant_dynamic-update-slice_fusion.1 = f32[2,64,256]{2,1,0:T(8,128)S(1)} fusion(f32[1,64,256]{2,1,0:T(8,128)} %param.3), kind=kLoop, calls=%fused_computation.8 | loop fusion | bytes 131072
  1.5 0.1 fusion.4
  1.6 8.5 %collective-permute-start.7 = (f32[2,2,2]{2,1,0:T(2,128)S(1)}, f32[2,2,2]{2,1,0:T(2,128)S(1)}, u32[]{:S(2)}, u32[]{:S(2)}) collective-permute-start(f32[2,2,2]{2,1,0:T(2,128)S(1)} %get-tuple-element.11), channel_id=1, source_target_pairs={{0,136},{128,9},{1,137},{129,10},{2,138},{130,11},{3,139},{131,12}... | collective-permute-start | bytes 104 | tf_op jit(solution)/shard_map/ppermute | solution.py:35
  10.1 4.0 %collective-permute-start.5 = (f32[2,2,256]{2,1,0:T(2,128)S(1)}, f32[2,2,256]{2,1,0:T(2,128)S(1)}, u32[]{:S(2)}, u32[]{:S(2)}) collective-permute-start(f32[2,2,256]{2,1,0:T(2,128)S(1)} %get-tuple-element.9), channel_id=1, source_target_pairs={{0,8},{128,136},{1,9},{129,137},{2,10},{130,138},{3,11},{131,139},... | collective-permute-start | bytes 12296 | tf_op jit(solution)/shard_map/ppermute | solution.py:35
  14.1 1.9 %collective-permute-start.2 = (f32[2,2,256]{2,1,0:T(2,128)S(1)}, f32[2,2,256]{2,1,0:T(2,128)S(1)}, u32[]{:S(2)}, u32[]{:S(2)}) collective-permute-start(f32[2,2,256]{2,1,0:T(2,128)S(1)} %get-tuple-element.8), channel_id=1, source_target_pairs={{8,0},{136,128},{9,1},{137,129},{10,2},{138,130},{11,3},{139,131},... | collective-permute-start | bytes 12296 | tf_op jit(solution)/shard_map/ppermute | solution.py:35
  16.1 0.1 fusion.2
  16.2 2.7 %collective-permute-start.1 = (f32[2,64,2]{2,1,0:T(8,128)S(1)}, f32[2,64,2]{2,1,0:T(8,128)S(1)}, u32[]{:S(2)}, u32[]{:S(2)}) collective-permute-start(f32[2,64,2]{2,1,0:T(8,128)S(1)} %get-tuple-element.7), channel_id=1, source_target_pairs={{0,128},{128,1},{1,129},{129,2},{2,130},{130,3},{3,131},{131,4},{4... | collective-permute-start | bytes 3080 | tf_op jit(solution)/shard_map/ppermute | solution.py:35
  18.9 1.9 %collective-permute-start = (f32[2,64,2]{2,1,0:T(8,128)S(1)}, f32[2,64,2]{2,1,0:T(8,128)S(1)}, u32[]{:S(2)}, u32[]{:S(2)}) collective-permute-start(f32[2,64,2]{2,1,0:T(8,128)S(1)} %get-tuple-element.6), channel_id=1, source_target_pairs={{128,0},{1,128},{129,1},{2,129},{130,2},{3,130},{131,3},{4,131},{1... | collective-permute-start | bytes 3080 | tf_op jit(solution)/shard_map/ppermute | solution.py:35
  20.8 0.7 %copy-done.1 = f32[1024]{0:T(1024)S(1)} copy-done((f32[1024]{0:T(1024)S(1)}, f32[1024]{0:T(1024)}, u32[]{:S(2)}) %copy-start.1) | copy-done | bytes 4120
  21.5 0.1 pad_dynamic-slice_fusion
  21.6 0.1 slice_bitcast_fusion.3
  21.7 0.2 reshape.70
  21.9 0.2 fusion.1
  22.1 0.1 pad_dynamic-slice_fusion.1
  22.2 0.1 slice_bitcast_fusion.1
  22.3 0.1 pad_maximum_fusion
  22.3 0.1 copy.15
  22.4 0.6 broadcast_add_fusion.fine_inflow_ref
  23.1 0.1 pad_maximum_fusion.1
  23.1 0.1 copy.17
  23.2 0.6 %broadcast_add_fusion.1.coarse_inflow_ref = f32[40,1]{1,0:T(8,128)} fusion(f32[40,1]{1,0:T(8,128)S(1)} %copy.17), kind=kLoop, calls=%fused_computation.5 | loop fusion | flops 40 | bytes 320 | tf_op jit(solution)/shard_map/add | solution.py:68
  23.8 0.6 %add_convert_fusion.flags_ref = s32[4]{0:T(128)} fusion(pred[1]{0:T(512)(128)(4,1)} %bitcast.3, pred[1]{0:T(512)(128)(4,1)} %bitcast.2, pred[1]{0:T(512)(128)(4,1)} %bitcast.1, pred[1]{0:T(512)(128)(4,1)} %bitcast), kind=kLoop, calls=%fused_computation.10 | loop fusion | flops 16 | bytes 20 | tf_op jit(solution)/shard_map/convert_element_type | solution.py:188
  24.5 0.1 pad.22.clone
  24.5 0.1 pad.16.clone
  24.6 5.1 %collective-permute-start.6 = (f32[2,2,2]{2,1,0:T(2,128)S(1)}, f32[2,2,2]{2,1,0:T(2,128)S(1)}, u32[]{:S(2)}, u32[]{:S(2)}) collective-permute-start(f32[2,2,2]{2,1,0:T(2,128)S(1)} %get-tuple-element.12), channel_id=1, source_target_pairs={{128,8},{1,136},{129,9},{2,137},{130,10},{3,138},{131,11},{4,139},... | collective-permute-start | bytes 104 | tf_op jit(solution)/shard_map/ppermute | solution.py:35
  29.7 6.8 %collective-permute-done.6 = f32[2,2,2]{2,1,0:T(2,128)S(1)} collective-permute-done((f32[2,2,2]{2,1,0:T(2,128)S(1)}, f32[2,2,2]{2,1,0:T(2,128)S(1)}, u32[]{:S(2)}, u32[]{:S(2)}) %collective-permute-start.6) | collective-permute-done | bytes 64 | tf_op jit(solution)/shard_map/ppermute | solution.py:35
  36.4 3.3 %collective-permute-start.4 = (f32[2,2,2]{2,1,0:T(2,128)S(1)}, f32[2,2,2]{2,1,0:T(2,128)S(1)}, u32[]{:S(2)}, u32[]{:S(2)}) collective-permute-start(f32[2,2,2]{2,1,0:T(2,128)S(1)} %get-tuple-element.13), channel_id=1, source_target_pairs={{8,128},{136,1},{9,129},{137,2},{10,130},{138,3},{11,131},{139,4},... | collective-permute-start | bytes 104 | tf_op jit(solution)/shard_map/ppermute | solution.py:35
  39.7 3.7 %collective-permute-done.4 = f32[2,2,2]{2,1,0:T(2,128)S(1)} collective-permute-done((f32[2,2,2]{2,1,0:T(2,128)S(1)}, f32[2,2,2]{2,1,0:T(2,128)S(1)}, u32[]{:S(2)}, u32[]{:S(2)}) %collective-permute-start.4) | collective-permute-done | bytes 64 | tf_op jit(solution)/shard_map/ppermute | solution.py:35
  43.4 1.9 %collective-permute-start.3 = (f32[2,2,2]{2,1,0:T(2,128)S(1)}, f32[2,2,2]{2,1,0:T(2,128)S(1)}, u32[]{:S(2)}, u32[]{:S(2)}) collective-permute-start(f32[2,2,2]{2,1,0:T(2,128)S(1)} %get-tuple-element.10), channel_id=1, source_target_pairs={{136,0},{9,128},{137,1},{10,129},{138,2},{11,130},{139,3},{12,131}... | collective-permute-start | bytes 104 | tf_op jit(solution)/shard_map/ppermute | solution.py:35
  45.3 11.1 %collective-permute-done.3 = f32[2,2,2]{2,1,0:T(2,128)S(1)} collective-permute-done((f32[2,2,2]{2,1,0:T(2,128)S(1)}, f32[2,2,2]{2,1,0:T(2,128)S(1)}, u32[]{:S(2)}, u32[]{:S(2)}) %collective-permute-start.3) | collective-permute-done | bytes 64 | tf_op jit(solution)/shard_map/ppermute | solution.py:35
  56.5 0.8 %maximum_maximum_fusion.noise_ref = f32[2,72,384]{2,1,0:T(8,128)} fusion(f32[2,2,2]{2,1,0:T(2,128)S(1)} %collective-permute-done.7, f32[2,2,124]{2,1,0:T(2,128)S(1)} %broadcast.23, f32[2,2,2]{2,1,0:T(2,128)S(1)} %collective-permute-done.6, f32[2,2,256]{2,1,0:T(2,128)S(1)} %collective-permute-done.5, f32[2,2,2]{2,1,0:T(2,128)S(1)} %collective-permute-done.4, ...), kind=kLoop, calls=%fused_computation.3 | loop fusion | flops 663552 | bytes 475488 | tf_op jit(solution)/shard_map/concatenate | solution.py:54
  57.3 3.5 %shard_map.50 = (f32[3,32,128]{2,1,0:T(8,128)}, f32[3,32,128]{2,1,0:T(8,128)}) custom-call(s32[4]{0:T(128)} %add_convert_fusion.flags_ref, f32[2,72,384]{2,1,0:T(8,128)} %maximum_maximum_fusion.noise_ref, f32[72,1]{1,0:T(8,128)} %broadcast_add_fusion.fine_inflow_ref, f32[40,1]{1,0:T(8,128)} %broadcast_add_fusion.1.coarse_inflow_ref), custom_call_target="tpu_custom_call" | custom-call | tf_op jit(solution)/shard_map/pallas_call | solution.py:200
  (15 shorter events, 0.1 us)
Async XLA Ops:
  0.6 0.9 %copy-start = (f32[1,64,256]{2,1,0:T(8,128)S(1)}, f32[1,64,256]{2,1,0:T(8,128)}, u32[]{:S(2)}) copy-start(f32[1,64,256]{2,1,0:T(8,128)} %param.4) | copy-start | bytes 196612
  1.6 23.0 %collective-permute-start.7 = (f32[2,2,2]{2,1,0:T(2,128)S(1)}, f32[2,2,2]{2,1,0:T(2,128)S(1)}, u32[]{:S(2)}, u32[]{:S(2)}) collective-permute-start(f32[2,2,2]{2,1,0:T(2,128)S(1)} %get-tuple-element.11), channel_id=1, source_target_pairs={{0,136},{128,9},{1,137},{129,10},{2,138},{130,11},{3,139},{131,12}... | collective-permute-start | bytes 104 | tf_op jit(solution)/shard_map/ppermute | solution.py:35
  10.1 46.4 %collective-permute-start.5 = (f32[2,2,256]{2,1,0:T(2,128)S(1)}, f32[2,2,256]{2,1,0:T(2,128)S(1)}, u32[]{:S(2)}, u32[]{:S(2)}) collective-permute-start(f32[2,2,256]{2,1,0:T(2,128)S(1)} %get-tuple-element.9), channel_id=1, source_target_pairs={{0,8},{128,136},{1,9},{129,137},{2,10},{130,138},{3,11},{131,139},... | collective-permute-start | bytes 12296 | tf_op jit(solution)/shard_map/ppermute | solution.py:35
  14.1 42.3 %collective-permute-start.2 = (f32[2,2,256]{2,1,0:T(2,128)S(1)}, f32[2,2,256]{2,1,0:T(2,128)S(1)}, u32[]{:S(2)}, u32[]{:S(2)}) collective-permute-start(f32[2,2,256]{2,1,0:T(2,128)S(1)} %get-tuple-element.8), channel_id=1, source_target_pairs={{8,0},{136,128},{9,1},{137,129},{10,2},{138,130},{11,3},{139,131},... | collective-permute-start | bytes 12296 | tf_op jit(solution)/shard_map/ppermute | solution.py:35
  16.2 40.3 %collective-permute-start.1 = (f32[2,64,2]{2,1,0:T(8,128)S(1)}, f32[2,64,2]{2,1,0:T(8,128)S(1)}, u32[]{:S(2)}, u32[]{:S(2)}) collective-permute-start(f32[2,64,2]{2,1,0:T(8,128)S(1)} %get-tuple-element.7), channel_id=1, source_target_pairs={{0,128},{128,1},{1,129},{129,2},{2,130},{130,3},{3,131},{131,4},{4... | collective-permute-start | bytes 3080 | tf_op jit(solution)/shard_map/ppermute | solution.py:35
  18.9 37.6 %collective-permute-start = (f32[2,64,2]{2,1,0:T(8,128)S(1)}, f32[2,64,2]{2,1,0:T(8,128)S(1)}, u32[]{:S(2)}, u32[]{:S(2)}) collective-permute-start(f32[2,64,2]{2,1,0:T(8,128)S(1)} %get-tuple-element.6), channel_id=1, source_target_pairs={{128,0},{1,128},{129,1},{2,129},{130,2},{3,130},{131,3},{4,131},{1... | collective-permute-start | bytes 3080 | tf_op jit(solution)/shard_map/ppermute | solution.py:35
  20.8 0.7 %copy-start.1 = (f32[1024]{0:T(1024)S(1)}, f32[1024]{0:T(1024)}, u32[]{:S(2)}) copy-start(f32[1024]{0:T(1024)} %param.5) | copy-start | bytes 12292
  24.6 11.8 %collective-permute-start.6 = (f32[2,2,2]{2,1,0:T(2,128)S(1)}, f32[2,2,2]{2,1,0:T(2,128)S(1)}, u32[]{:S(2)}, u32[]{:S(2)}) collective-permute-start(f32[2,2,2]{2,1,0:T(2,128)S(1)} %get-tuple-element.12), channel_id=1, source_target_pairs={{128,8},{1,136},{129,9},{2,137},{130,10},{3,138},{131,11},{4,139},... | collective-permute-start | bytes 104 | tf_op jit(solution)/shard_map/ppermute | solution.py:35
  36.4 7.0 %collective-permute-start.4 = (f32[2,2,2]{2,1,0:T(2,128)S(1)}, f32[2,2,2]{2,1,0:T(2,128)S(1)}, u32[]{:S(2)}, u32[]{:S(2)}) collective-permute-start(f32[2,2,2]{2,1,0:T(2,128)S(1)} %get-tuple-element.13), channel_id=1, source_target_pairs={{8,128},{136,1},{9,129},{137,2},{10,130},{138,3},{11,131},{139,4},... | collective-permute-start | bytes 104 | tf_op jit(solution)/shard_map/ppermute | solution.py:35
  43.4 13.0 %collective-permute-start.3 = (f32[2,2,2]{2,1,0:T(2,128)S(1)}, f32[2,2,2]{2,1,0:T(2,128)S(1)}, u32[]{:S(2)}, u32[]{:S(2)}) collective-permute-start(f32[2,2,2]{2,1,0:T(2,128)S(1)} %get-tuple-element.10), channel_id=1, source_target_pairs={{136,0},{9,128},{137,1},{10,129},{138,2},{11,130},{139,3},{12,131}... | collective-permute-start | bytes 104 | tf_op jit(solution)/shard_map/ppermute | solution.py:35

commit v3 on v1

--- a/solution.py
+++ b/solution.py
@@ -13,8 +13,16 @@
 COARSE_SHAPE = (40, 256)
 
 
-def shift_pairs(count, delta, place=lambda i: i):
-    return [(place(i), place(i + delta)) for i in range(count) if 0 <= i + delta < count]
+def pair_mean(values):
+    paired = values.reshape(-1, 2)
+    return (paired[:, 0] + paired[:, 1]) * 0.5
+
+
+def swap_pairs(count, parity, place=lambda i: i):
+    pairs = []
+    for i in range(parity, count - 1, 2):
+        pairs += [(place(i), place(i + 1)), (place(i + 1), place(i))]
+    return pairs
 
 
 def strip_place(strip):
@@ -22,24 +30,31 @@
     return (strip % levels) * lax.axis_size("col") + strip // levels
 
 
-def pair_mean(values):
-    paired = values.reshape(-1, 2)
-    return (paired[:, 0] + paired[:, 1]) * 0.5
+def swapped(first, last, index, count, axis, place=lambda i: i):
+    odd = index % 2 == 1
+    got = []
+    for parity in range(2):
+        sends_last = odd if parity else jnp.logical_not(odd)
+        block = jnp.where(sends_last, last, first)
+        got.append(lax.ppermute(block, axis, swap_pairs(count, parity, place)))
+    before = jnp.where(odd, got[0], got[1])
+    after = jnp.where(odd, got[1], got[0])
+    return before, after
 
 
 def with_halo(noise):
     fields, count_rows, count_cols = noise.shape
     strips = lax.axis_size("col") * lax.axis_size("level")
+    strip = lax.axis_index("col") * lax.axis_size("level") + lax.axis_index("level")
     rows = lax.axis_size("row")
-    across = ("level", "col")
-    west = lax.ppermute(noise[:, :, -HALO:], across, shift_pairs(strips, 1, strip_place))
-    east = lax.ppermute(noise[:, :, :HALO], across, shift_pairs(strips, -1, strip_place))
+    west, east = swapped(
+        noise[:, :, :HALO], noise[:, :, -HALO:], strip, strips, ("level", "col"), strip_place
+    )
     gap_cols = FINE_SHAPE[1] - count_cols - 2 * HALO
     wide = jnp.concatenate(
         [noise, east, jnp.zeros((fields, count_rows, gap_cols), noise.dtype), west], axis=2
     )
-    north = lax.ppermute(wide[:, -HALO:, :], "row", shift_pairs(rows, 1))
-    south = lax.ppermute(wide[:, :HALO, :], "row", shift_pairs(rows, -1))
+    north, south = swapped(wide[:, :HALO], wide[:, -HALO:], lax.axis_index("row"), rows, "row")
     gap_rows = FINE_SHAPE[0] - count_rows - 2 * HALO
     return jnp.concatenate(
         [wide, south, jnp.zeros((fields, gap_rows, FINE_SHAPE[1]), noise.dtype), north], axis=1

time: 36 us -> 27.1 us (0.75)
  the two profiles are of different devices: /device:TPU:31 before, /device:TPU:192 now
where the time goes in v3:
time: 27.1 us; the launch traced here: 26.9 us
  starting transfers between devices  10.4 us (38%)
  waiting for transfers between devices  6.58 us (24%)
  Pallas kernels  3.52 us (13%)
  other arithmetic  3.25 us (12%)
  local copies, waits for them, and re-layouts  2.36 us (9%)
  between operations  0.74 us (3%)
    ppermute x4, starting transfers between devices, swapped(): got.append(lax.ppermute(block, axis, swap_pairs(count, parity, place)))  10.4 us
    ppermute x4, waiting for transfers between devices, swapped(): got.append(lax.ppermute(block, axis, swap_pairs(count, parity, place)))  6.58 us
    pallas_call x1, Pallas kernels, body(): pl.pallas_call(level_kernel, out_shape=(out, out), in_specs=[pl.BlockSpec...  3.52 us
    unnamed x5, local copies, waits for them, and re-layouts  1.56 us
    add x2, other arithmetic, wrapped_rows(): return (0.5 + jnp.roll(window, -lead)).reshape(count, 1)  1.22 us
    concatenate x1, other arithmetic, with_halo(): jnp.concatenate([wide, south, jnp.zeros((fields, gap_rows, FINE_SHAPE[1])...  0.8 us
    convert_element_type x1, other arithmetic, body(): flags = jnp.stack([row_index == 0, row_index == lax.axis_size('row') - 1,...  0.65 us
  transfers between devices with their start and end apart: 4, of which 2 were waited for; matrix products, arithmetic and copies ran while one was open for 11% of the time, Pallas kernels for 0%

profile of v3, /device:TPU:192, one launch (start us, length us, event | category | flops | bytes accessed | tf_op | source)
XLA Modules:
  0.0 26.9 jit_solution(12740976539533517234)
XLA Ops:
  0.6 0.0 copy-start
  0.7 0.9 %constant_dynamic-update-slice_fusion.1 = f32[2,64,256]{2,1,0:T(8,128)S(1)} fusion(f32[1,64,256]{2,1,0:T(8,128)} %param.3), kind=kLoop, calls=%fused_computation.16 | loop fusion | bytes 131072
  1.5 0.0 copy-done
  1.5 0.1 slice_select_fusion.1
  1.6 4.3 %collective-permute-start = (f32[2,64,2]{2,1,0:T(8,128)S(1)}, f32[2,64,2]{2,1,0:T(8,128)S(1)}, u32[]{:S(2)}, u32[]{:S(2)}) collective-permute-start(f32[2,64,2]{2,1,0:T(8,128)S(1)} %get-tuple-element.11), channel_id=1, source_target_pairs={{128,1},{1,128},{129,2},{2,129},{130,3},{3,130},{131,4},{4,131},{1... | collective-permute-start | bytes 3080 | tf_op jit(solution)/shard_map/ppermute | solution.py:39
  6.0 0.1 collective-permute-start.1
  6.1 0.0 copy-start.1
  6.1 0.7 %copy-done.1 = f32[1024]{0:T(1024)S(1)} copy-done((f32[1024]{0:T(1024)S(1)}, f32[1024]{0:T(1024)}, u32[]{:S(2)}) %copy-start.1) | copy-done | bytes 4120
  6.8 0.2 reshape.70
  7.0 0.2 fusion.1
  7.2 0.1 pad_dynamic-slice_fusion.1
  7.3 0.1 slice_bitcast_fusion.1
  7.4 0.1 pad_dynamic-slice_fusion
  7.5 0.1 slice_bitcast_fusion.3
  7.5 0.1 pad_maximum_fusion.6
  7.6 0.1 copy.17
  7.7 0.1 pad_maximum_fusion.5
  7.8 0.1 copy.15
  7.9 0.6 %broadcast_add_fusion.fine_inflow_ref = f32[72,1]{1,0:T(8,128)} fusion(f32[72,1]{1,0:T(8,128)S(1)} %copy.15), kind=kLoop, calls=%fused_computation.8 | loop fusion | flops 72 | bytes 576 | tf_op jit(solution)/shard_map/add | solution.py:67
  8.5 0.6 %broadcast_add_fusion.1.coarse_inflow_ref = f32[40,1]{1,0:T(8,128)} fusion(f32[40,1]{1,0:T(8,128)S(1)} %copy.17), kind=kLoop, calls=%fused_computation.9 | loop fusion | flops 40 | bytes 320 | tf_op jit(solution)/shard_map/add | solution.py:67
  9.1 4.1 %collective-permute-done = f32[2,64,2]{2,1,0:T(8,128)S(1)} collective-permute-done((f32[2,64,2]{2,1,0:T(8,128)S(1)}, f32[2,64,2]{2,1,0:T(8,128)S(1)}, u32[]{:S(2)}, u32[]{:S(2)}) %collective-permute-start) | collective-permute-done | bytes 1056 | tf_op jit(solution)/shard_map/ppermute | solution.py:39
  13.2 0.0 collective-permute-done.1
  13.3 0.1 broadcast_select_fusion.5
  13.4 1.6 %collective-permute-start.3 = (f32[2,2,384]{2,1,0:T(2,128)S(1)}, f32[2,2,384]{2,1,0:T(2,128)S(1)}, u32[]{:S(2)}, u32[]{:S(2)}) collective-permute-start(f32[2,2,384]{2,1,0:T(2,128)S(1)} %broadcast_select_fusion.2), channel_id=1, source_target_pairs={{0,8},{8,0},{16,24},{24,16},{32,40},{40,32},{48,56},{56,48},{64,72... | collective-permute-start | bytes 18440 | tf_op jit(solution)/shard_map/ppermute | solution.py:39
  14.9 4.4 %collective-permute-start.2 = (f32[2,2,384]{2,1,0:T(2,128)S(1)}, f32[2,2,384]{2,1,0:T(2,128)S(1)}, u32[]{:S(2)}, u32[]{:S(2)}) collective-permute-start(f32[2,2,384]{2,1,0:T(2,128)S(1)} %get-tuple-element.6), channel_id=1, source_target_pairs={{8,16},{16,8},{24,32},{32,24},{40,48},{48,40},{56,64},{64,56},{72,... | collective-permute-start | bytes 18440 | tf_op jit(solution)/shard_map/ppermute | solution.py:39
  19.4 0.7 %add_convert_fusion.flags_ref = s32[4]{0:T(128)} fusion(pred[1]{0:T(512)(128)(4,1)} %bitcast.3, pred[1]{0:T(512)(128)(4,1)} %bitcast.2, pred[1]{0:T(512)(128)(4,1)} %bitcast.1, pred[1]{0:T(512)(128)(4,1)} %bitcast), kind=kLoop, calls=%fused_computation.22 | loop fusion | flops 16 | bytes 20 | tf_op jit(solution)/shard_map/convert_element_type | solution.py:187
  20.0 0.1 pad.19.clone
  20.1 0.0 collective-permute-done.3
  20.1 2.4 %collective-permute-done.2 = f32[2,2,384]{2,1,0:T(2,128)S(1)} collective-permute-done((f32[2,2,384]{2,1,0:T(2,128)S(1)}, f32[2,2,384]{2,1,0:T(2,128)S(1)}, u32[]{:S(2)}, u32[]{:S(2)}) %collective-permute-start.2) | collective-permute-done | bytes 6176 | tf_op jit(solution)/shard_map/ppermute | solution.py:39
  22.6 0.8 %pad_maximum_fusion.noise_ref = f32[2,72,384]{2,1,0:T(8,128)} fusion(f32[2,2,384]{2,1,0:T(2,128)S(1)} %get-tuple-element.14, f32[2,2,384]{2,1,0:T(2,128)S(1)} %get-tuple-element.13, f32[2,64,2]{2,1,0:T(8,128)S(1)} %get-tuple-element.10, f32[2,64,124]{2,1,0:T(8,128)S(1)} %broadcast_in_dim.12, f32[2,64,2]{2,1,0:T(8,128)S(1)} %get-tuple-element.9, ...), kind=kLoop, calls=%fused_computation.3 | loop fusion | flops 331776 | bytes 430368 | tf_op jit(solution)/shard_map/concatenate | solution.py:59
  23.4 3.5 %shard_map.50 = (f32[3,32,128]{2,1,0:T(8,128)}, f32[3,32,128]{2,1,0:T(8,128)}) custom-call(s32[4]{0:T(128)} %add_convert_fusion.flags_ref, f32[2,72,384]{2,1,0:T(8,128)} %pad_maximum_fusion.noise_ref, f32[72,1]{1,0:T(8,128)} %broadcast_add_fusion.fine_inflow_ref, f32[40,1]{1,0:T(8,128)} %broadcast_add_fusion.1.coarse_inflow_ref), custom_call_target="tpu_custom_call" | custom-call | tf_op jit(solution)/shard_map/pallas_call | solution.py:199
  (8 shorter events, 0.0 us)
Async XLA Ops:
  0.6 0.9 %copy-start = (f32[1,64,256]{2,1,0:T(8,128)S(1)}, f32[1,64,256]{2,1,0:T(8,128)}, u32[]{:S(2)}) copy-start(f32[1,64,256]{2,1,0:T(8,128)} %param.4) | copy-start | bytes 196612
  1.6 11.6 %collective-permute-start = (f32[2,64,2]{2,1,0:T(8,128)S(1)}, f32[2,64,2]{2,1,0:T(8,128)S(1)}, u32[]{:S(2)}, u32[]{:S(2)}) collective-permute-start(f32[2,64,2]{2,1,0:T(8,128)S(1)} %get-tuple-element.11), channel_id=1, source_target_pairs={{128,1},{1,128},{129,2},{2,129},{130,3},{3,130},{131,4},{4,131},{1... | collective-permute-start | bytes 3080 | tf_op jit(solution)/shard_map/ppermute | solution.py:39
  6.0 7.3 %collective-permute-start.1 = (f32[2,64,2]{2,1,0:T(8,128)S(1)}, f32[2,64,2]{2,1,0:T(8,128)S(1)}, u32[]{:S(2)}, u32[]{:S(2)}) collective-permute-start(f32[2,64,2]{2,1,0:T(8,128)S(1)} %get-tuple-element.12), channel_id=1, source_target_pairs={{0,128},{128,0},{1,129},{129,1},{2,130},{130,2},{3,131},{131,3},{4... | collective-permute-start | bytes 3080 | tf_op jit(solution)/shard_map/ppermute | solution.py:39
  6.1 0.7 %copy-start.1 = (f32[1024]{0:T(1024)S(1)}, f32[1024]{0:T(1024)}, u32[]{:S(2)}) copy-start(f32[1024]{0:T(1024)} %param.5) | copy-start | bytes 12292
  13.4 6.8 %collective-permute-start.3 = (f32[2,2,384]{2,1,0:T(2,128)S(1)}, f32[2,2,384]{2,1,0:T(2,128)S(1)}, u32[]{:S(2)}, u32[]{:S(2)}) collective-permute-start(f32[2,2,384]{2,1,0:T(2,128)S(1)} %broadcast_select_fusion.2), channel_id=1, source_target_pairs={{0,8},{8,0},{16,24},{24,16},{32,40},{40,32},{48,56},{56,48},{64,72... | collective-permute-start | bytes 18440 | tf_op jit(solution)/shard_map/ppermute | solution.py:39
  14.9 7.6 %collective-permute-start.2 = (f32[2,2,384]{2,1,0:T(2,128)S(1)}, f32[2,2,384]{2,1,0:T(2,128)S(1)}, u32[]{:S(2)}, u32[]{:S(2)}) collective-permute-start(f32[2,2,384]{2,1,0:T(2,128)S(1)} %get-tuple-element.6), channel_id=1, source_target_pairs={{8,16},{16,8},{24,32},{32,24},{40,48},{48,40},{56,64},{64,56},{72,... | collective-permute-start | bytes 18440 | tf_op jit(solution)/shard_map/ppermute | solution.py:39

commit v4 on v3

--- a/solution.py
+++ b/solution.py
@@ -47,17 +47,19 @@
     strips = lax.axis_size("col") * lax.axis_size("level")
     strip = lax.axis_index("col") * lax.axis_size("level") + lax.axis_index("level")
     rows = lax.axis_size("row")
+    north, south = swapped(
+        noise[:, :HALO], noise[:, -HALO:], lax.axis_index("row"), rows, "row"
+    )
+    gap_rows = FINE_SHAPE[0] - count_rows - 2 * HALO
+    tall = jnp.concatenate(
+        [noise, south, jnp.zeros((fields, gap_rows, count_cols), noise.dtype), north], axis=1
+    )
     west, east = swapped(
-        noise[:, :, :HALO], noise[:, :, -HALO:], strip, strips, ("level", "col"), strip_place
+        tall[:, :, :HALO], tall[:, :, -HALO:], strip, strips, ("level", "col"), strip_place
     )
     gap_cols = FINE_SHAPE[1] - count_cols - 2 * HALO
-    wide = jnp.concatenate(
-        [noise, east, jnp.zeros((fields, count_rows, gap_cols), noise.dtype), west], axis=2
-    )
-    north, south = swapped(wide[:, :HALO], wide[:, -HALO:], lax.axis_index("row"), rows, "row")
-    gap_rows = FINE_SHAPE[0] - count_rows - 2 * HALO
     return jnp.concatenate(
-        [wide, south, jnp.zeros((fields, gap_rows, FINE_SHAPE[1]), noise.dtype), north], axis=1
+        [tall, east, jnp.zeros((fields, FINE_SHAPE[0], gap_cols), noise.dtype), west], axis=2
     )
 
 

time: 27.1 us -> 26.9 us (level)
  waiting for transfers between devices: 6.58 us -> 8.72 us
  starting transfers between devices: 10.4 us -> 8.89 us
  local copies, waits for them, and re-layouts: 2.36 us -> 1.68 us
    ppermute x4, waiting for transfers between devices: 6.58 us -> 8.72 us  [swapped(): got.append(lax.ppermute(block, axis, swap_pairs(count, parity, place)))]
    ppermute x4, starting transfers between devices: 10.4 us -> 8.89 us  [swapped(): got.append(lax.ppermute(block, axis, swap_pairs(count, parity, place)))]
    unnamed x5, local copies, waits for them, and re-layouts: 1.56 us -> 0.89 us
    concatenate x1 -> x2, other arithmetic: 0.8 us -> 0.8 us  [the longest x1 0.78 us: with_halo(): jnp.concatenate([tall, east, jnp.zeros((fields, FINE_SHAPE[0], gap_cols),...]
  transfers between devices with their start and end apart: 4 -> 4, of which waited for: 2 -> 3; matrix products, arithmetic and copies ran while one was open for 11% -> 11% of each run, Pallas kernels for 0% -> 0%
where the time goes in v4:
time: 26.9 us; the launch traced here: 26.7 us
  starting transfers between devices  8.89 us (33%)
  waiting for transfers between devices  8.72 us (32%)
  Pallas kernels  3.52 us (13%)
  other arithmetic  3.17 us (12%)
  local copies, waits for them, and re-layouts  1.68 us (6%)
  between operations  0.75 us (3%)
    ppermute x4, starting transfers between devices, swapped(): got.append(lax.ppermute(block, axis, swap_pairs(count, parity, place)))  8.89 us
    ppermute x4, waiting for transfers between devices, swapped(): got.append(lax.ppermute(block, axis, swap_pairs(count, parity, place)))  8.72 us
    pallas_call x1, Pallas kernels, body(): pl.pallas_call(level_kernel, out_shape=(out, out), in_specs=[pl.BlockSpec...  3.52 us
    add x2, other arithmetic, wrapped_rows(): return (0.5 + jnp.roll(window, -lead)).reshape(count, 1)  1.22 us
    unnamed x5, local copies, waits for them, and re-layouts  0.89 us
    concatenate x1, other arithmetic, with_halo(): jnp.concatenate([tall, east, jnp.zeros((fields, FINE_SHAPE[0], gap_cols),...  0.78 us
    convert_element_type x1, other arithmetic, body(): flags = jnp.stack([row_index == 0, row_index == lax.axis_size('row') - 1,...  0.65 us
  transfers between devices with their start and end apart: 4, of which 3 were waited for; matrix products, arithmetic and copies ran while one was open for 11% of the time, Pallas kernels for 0%

profile of v4, /device:TPU:192, one launch (start us, length us, event | category | flops | bytes accessed | tf_op | source)
XLA Modules:
  0.0 26.7 jit_solution(2621115242913511501)
XLA Ops:
  0.6 0.0 copy-start
  0.7 0.9 %constant_dynamic-update-slice_fusion.1 = f32[2,64,256]{2,1,0:T(8,128)S(1)} fusion(f32[1,64,256]{2,1,0:T(8,128)} %param.3), kind=kLoop, calls=%fused_computation.13 | loop fusion | bytes 131072
  1.5 0.0 copy-done
  1.6 0.0 copy-start.1
  1.6 5.1 %collective-permute-start = (f32[2,2,256]{2,1,0:T(2,128)S(1)}, f32[2,2,256]{2,1,0:T(2,128)S(1)}, u32[]{:S(2)}, u32[]{:S(2)}) collective-permute-start(f32[2,2,256]{2,1,0:T(2,128)S(1)} %get-tuple-element.10), channel_id=1, source_target_pairs={{8,16},{16,8},{24,32},{32,24},{40,48},{48,40},{56,64},{64,56},{72,... | collective-permute-start | bytes 12296 | tf_op jit(solution)/shard_map/ppermute | solution.py:39
  6.7 0.1 collective-permute-start.1
  6.8 0.0 copy-done.1
  6.8 0.2 reshape.70
  7.0 0.2 fusion.1
  7.2 0.1 pad_dynamic-slice_fusion.1
  7.3 0.1 slice_bitcast_fusion.1
  7.4 0.1 pad_dynamic-slice_fusion
  7.5 0.1 slice_bitcast_fusion.3
  7.6 0.1 pad_maximum_fusion.3
  7.6 0.1 copy.17
  7.7 0.1 pad_maximum_fusion.2
  7.8 0.1 copy.15
  7.9 0.6 %broadcast_add_fusion.fine_inflow_ref = f32[72,1]{1,0:T(8,128)} fusion(f32[72,1]{1,0:T(8,128)S(1)} %copy.15), kind=kLoop, calls=%fused_computation.9 | loop fusion | flops 72 | bytes 576 | tf_op jit(solution)/shard_map/add | solution.py:69
  8.5 0.6 %broadcast_add_fusion.1.coarse_inflow_ref = f32[40,1]{1,0:T(8,128)} fusion(f32[40,1]{1,0:T(8,128)S(1)} %copy.17), kind=kLoop, calls=%fused_computation.10 | loop fusion | flops 40 | bytes 320 | tf_op jit(solution)/shard_map/add | solution.py:69
  9.1 0.1 collective-permute-done
  9.2 1.2 %collective-permute-done.1 = f32[2,2,256]{2,1,0:T(2,128)S(1)} collective-permute-done((f32[2,2,256]{2,1,0:T(2,128)S(1)}, f32[2,2,256]{2,1,0:T(2,128)S(1)}, u32[]{:S(2)}, u32[]{:S(2)}) %collective-permute-start.1) | collective-permute-done | bytes 4128 | tf_op jit(solution)/shard_map/ppermute | solution.py:39
  10.4 0.1 slice_select_fusion.1
  10.5 2.3 %collective-permute-start.2 = (f32[2,72,2]{2,1,0:T(8,128)S(1)}, f32[2,72,2]{2,1,0:T(8,128)S(1)}, u32[]{:S(2)}, u32[]{:S(2)}) collective-permute-start(f32[2,72,2]{2,1,0:T(8,128)S(1)} %get-tuple-element.8), channel_id=1, source_target_pairs={{128,1},{1,128},{129,2},{2,129},{130,3},{3,130},{131,4},{4,131},{1... | collective-permute-start | bytes 3464 | tf_op jit(solution)/shard_map/ppermute | solution.py:39
  12.8 1.4 %collective-permute-start.3 = (f32[2,72,2]{2,1,0:T(8,128)S(1)}, f32[2,72,2]{2,1,0:T(8,128)S(1)}, u32[]{:S(2)}, u32[]{:S(2)}) collective-permute-start(f32[2,72,2]{2,1,0:T(8,128)S(1)} %get-tuple-element.9), channel_id=1, source_target_pairs={{0,128},{128,0},{1,129},{129,1},{2,130},{130,2},{3,131},{131,3},{4... | collective-permute-start | bytes 3464 | tf_op jit(solution)/shard_map/ppermute | solution.py:39
  14.2 0.7 %add_convert_fusion.flags_ref = s32[4]{0:T(128)} fusion(pred[1]{0:T(512)(128)(4,1)} %bitcast.3, pred[1]{0:T(512)(128)(4,1)} %bitcast.2, pred[1]{0:T(512)(128)(4,1)} %bitcast.1, pred[1]{0:T(512)(128)(4,1)} %bitcast), kind=kLoop, calls=%fused_computation.19 | loop fusion | flops 16 | bytes 20 | tf_op jit(solution)/shard_map/convert_element_type | solution.py:189
  14.9 0.1 pad.19.clone
  14.9 7.5 %collective-permute-done.2 = f32[2,72,2]{2,1,0:T(8,128)S(1)} collective-permute-done((f32[2,72,2]{2,1,0:T(8,128)S(1)}, f32[2,72,2]{2,1,0:T(8,128)S(1)}, u32[]{:S(2)}, u32[]{:S(2)}) %collective-permute-start.2) | collective-permute-done | bytes 1184 | tf_op jit(solution)/shard_map/ppermute | solution.py:39
  22.4 0.0 collective-permute-done.3
  22.4 0.8 %pad_maximum_fusion.noise_ref = f32[2,72,384]{2,1,0:T(8,128)} fusion(f32[2,72,2]{2,1,0:T(8,128)S(1)} %get-tuple-element.7, f32[2,72,2]{2,1,0:T(8,128)S(1)} %get-tuple-element.6, f32[2,2,256]{2,1,0:T(2,128)S(1)} %get-tuple-element.13, f32[2,4,256]{2,1,0:T(4,128)S(1)} %broadcast_in_dim.12, f32[2,2,256]{2,1,0:T(2,128)S(1)} %get-tuple-element.12, ...), kind=kLoop, calls=%fused_computation.3 | loop fusion | flops 331776 | bytes 372480 | tf_op jit(solution)/shard_map/concatenate | solution.py:61
  23.2 3.5 %shard_map.50 = (f32[3,32,128]{2,1,0:T(8,128)}, f32[3,32,128]{2,1,0:T(8,128)}) custom-call(s32[4]{0:T(128)} %add_convert_fusion.flags_ref, f32[2,72,384]{2,1,0:T(8,128)} %pad_maximum_fusion.noise_ref, f32[72,1]{1,0:T(8,128)} %broadcast_add_fusion.fine_inflow_ref, f32[40,1]{1,0:T(8,128)} %broadcast_add_fusion.1.coarse_inflow_ref), custom_call_target="tpu_custom_call" | custom-call | tf_op jit(solution)/shard_map/pallas_call | solution.py:201
  (9 shorter events, 0.1 us)
Async XLA Ops:
  0.6 0.9 %copy-start = (f32[1,64,256]{2,1,0:T(8,128)S(1)}, f32[1,64,256]{2,1,0:T(8,128)}, u32[]{:S(2)}) copy-start(f32[1,64,256]{2,1,0:T(8,128)} %param.4) | copy-start | bytes 196612
  1.6 5.2 %copy-start.1 = (f32[1024]{0:T(1024)S(1)}, f32[1024]{0:T(1024)}, u32[]{:S(2)}) copy-start(f32[1024]{0:T(1024)} %param.5) | copy-start | bytes 12292
  1.6 7.6 %collective-permute-start = (f32[2,2,256]{2,1,0:T(2,128)S(1)}, f32[2,2,256]{2,1,0:T(2,128)S(1)}, u32[]{:S(2)}, u32[]{:S(2)}) collective-permute-start(f32[2,2,256]{2,1,0:T(2,128)S(1)} %get-tuple-element.10), channel_id=1, source_target_pairs={{8,16},{16,8},{24,32},{32,24},{40,48},{48,40},{56,64},{64,56},{72,... | collective-permute-start | bytes 12296 | tf_op jit(solution)/shard_map/ppermute | solution.py:39
  6.7 3.7 %collective-permute-start.1 = (f32[2,2,256]{2,1,0:T(2,128)S(1)}, f32[2,2,256]{2,1,0:T(2,128)S(1)}, u32[]{:S(2)}, u32[]{:S(2)}) collective-permute-start(f32[2,2,256]{2,1,0:T(2,128)S(1)} %get-tuple-element.11), channel_id=1, source_target_pairs={{0,8},{8,0},{16,24},{24,16},{32,40},{40,32},{48,56},{56,48},{64,72... | collective-permute-start | bytes 12296 | tf_op jit(solution)/shard_map/ppermute | solution.py:39
  10.5 11.9 %collective-permute-start.2 = (f32[2,72,2]{2,1,0:T(8,128)S(1)}, f32[2,72,2]{2,1,0:T(8,128)S(1)}, u32[]{:S(2)}, u32[]{:S(2)}) collective-permute-start(f32[2,72,2]{2,1,0:T(8,128)S(1)} %get-tuple-element.8), channel_id=1, source_target_pairs={{128,1},{1,128},{129,2},{2,129},{130,3},{3,130},{131,4},{4,131},{1... | collective-permute-start | bytes 3464 | tf_op jit(solution)/shard_map/ppermute | solution.py:39
  12.8 9.6 %collective-permute-start.3 = (f32[2,72,2]{2,1,0:T(8,128)S(1)}, f32[2,72,2]{2,1,0:T(8,128)S(1)}, u32[]{:S(2)}, u32[]{:S(2)}) collective-permute-start(f32[2,72,2]{2,1,0:T(8,128)S(1)} %get-tuple-element.9), channel_id=1, source_target_pairs={{0,128},{128,0},{1,129},{129,1},{2,130},{130,2},{3,131},{131,3},{4... | collective-permute-start | bytes 3464 | tf_op jit(solution)/shard_map/ppermute | solution.py:39

commit v5 on v4

--- a/solution.py
+++ b/solution.py
@@ -42,25 +42,36 @@
     return before, after
 
 
-def with_halo(noise):
-    fields, count_rows, count_cols = noise.shape
+def halo_frames(friction, height):
+    count_rows, count_cols = friction.shape
+    fields = 2
     strips = lax.axis_size("col") * lax.axis_size("level")
     strip = lax.axis_index("col") * lax.axis_size("level") + lax.axis_index("level")
     rows = lax.axis_size("row")
+
+    def both(part):
+        return jnp.stack([friction[part], height[part]])
+
     north, south = swapped(
-        noise[:, :HALO], noise[:, -HALO:], lax.axis_index("row"), rows, "row"
+        both(slice(0, HALO)), both(slice(count_rows - HALO, count_rows)),
+        lax.axis_index("row"), rows, "row",
     )
     gap_rows = FINE_SHAPE[0] - count_rows - 2 * HALO
-    tall = jnp.concatenate(
-        [noise, south, jnp.zeros((fields, gap_rows, count_cols), noise.dtype), north], axis=1
-    )
+    row_frame = jnp.concatenate(
+        [south, jnp.zeros((fields, gap_rows, count_cols), friction.dtype), north], axis=1
+    )
+    first = (slice(None), slice(0, HALO))
+    last = (slice(None), slice(count_cols - HALO, count_cols))
     west, east = swapped(
-        tall[:, :, :HALO], tall[:, :, -HALO:], strip, strips, ("level", "col"), strip_place
+        jnp.concatenate([both(first), row_frame[:, :, :HALO]], axis=1),
+        jnp.concatenate([both(last), row_frame[:, :, -HALO:]], axis=1),
+        strip, strips, ("level", "col"), strip_place,
     )
     gap_cols = FINE_SHAPE[1] - count_cols - 2 * HALO
-    return jnp.concatenate(
-        [tall, east, jnp.zeros((fields, FINE_SHAPE[0], gap_cols), noise.dtype), west], axis=2
-    )
+    col_frame = jnp.concatenate(
+        [east, jnp.zeros((fields, FINE_SHAPE[0], gap_cols), friction.dtype), west], axis=2
+    )
+    return row_frame, col_frame
 
 
 def wrapped_rows(values, start, count, lead):
@@ -146,15 +157,23 @@
     return jnp.dot(a, b, precision=lax.Precision.HIGHEST, preferred_element_type=jnp.float32)
 
 
-def level_kernel(flags_ref, noise_ref, fine_inflow_ref, coarse_inflow_ref, mean_ref, corr_ref):
+def level_kernel(
+    flags_ref, friction_ref, height_ref, row_frame_ref, col_frame_ref, fine_inflow_ref,
+    coarse_inflow_ref, mean_ref, corr_ref,
+):
     flags = [flags_ref[i] for i in range(4)]
+
+    def framed(center_ref, field):
+        tall = jnp.concatenate([center_ref[0], row_frame_ref[field]], axis=0)
+        return jnp.concatenate([tall, col_frame_ref[field]], axis=1)
+
     fine_rows, fine_cols = FINE_SHAPE
     coarse_rows, coarse_cols = COARSE_SHAPE
     out_rows, out_cols = mean_ref.shape[1], mean_ref.shape[2]
     tile_rows, tile_cols = 2 * out_rows, 2 * out_cols
 
-    fine_coef = noise_ref[0]
-    noise_height = noise_ref[1]
+    fine_coef = framed(friction_ref, 0)
+    noise_height = framed(height_ref, 1)
     depth = 1.0 + 0.1 * noise_height
     state = (depth, 0.5 * depth, jnp.zeros_like(depth))
     fine_inflow = jnp.broadcast_to(fine_inflow_ref[...], FINE_SHAPE)
@@ -190,7 +209,7 @@
     tile_rows, tile_cols = friction.shape[1], friction.shape[2]
     out_rows, out_cols = tile_rows // 2, tile_cols // 2
 
-    noise = with_halo(jnp.concatenate([friction, height], axis=0))
+    row_frame, col_frame = halo_frames(friction[0], height[0])
     lead = FINE_SHAPE[0] - tile_rows - HALO
     fine_inflow = wrapped_rows(inflow, row_index * tile_rows, FINE_SHAPE[0], lead)
     lead = COARSE_SHAPE[0] - out_rows - 1
@@ -201,9 +220,9 @@
     mean, corr = pl.pallas_call(
         level_kernel,
         out_shape=(out, out),
-        in_specs=[pl.BlockSpec(memory_space=pltpu.SMEM), vmem, vmem, vmem],
+        in_specs=[pl.BlockSpec(memory_space=pltpu.SMEM)] + [vmem] * 6,
         out_specs=(vmem, vmem),
-    )(flags, noise, fine_inflow, coarse_inflow)
+    )(flags, friction, height, row_frame, col_frame, fine_inflow, coarse_inflow)
     return (mean[None], corr[None])
 
 

time: 26.9 us -> 28.5 us (1.059)
  local copies, waits for them, and re-layouts: 1.68 us -> 3.83 us
  waiting for transfers between devices: 8.72 us -> 8.04 us
    slice x0 -> x8, local copies, waits for them, and re-layouts: none -> 1.26 us  [the longest x7 1.19 us: both(): return jnp.stack([friction[part], height[part]])]
    ppermute x4, waiting for transfers between devices: 8.72 us -> 8.04 us  [swapped(): got.append(lax.ppermute(block, axis, swap_pairs(count, parity, place)))]
    unnamed x5 -> x8, local copies, waits for them, and re-layouts: 0.89 us -> 1.5 us
  transfers between devices with their start and end apart: 4 -> 4, of which waited for: 3 -> 1; matrix products, arithmetic and copies ran while one was open for 11% -> 14% of each run, Pallas kernels for 0% -> 0%
where the time goes in v5:
time: 28.5 us; the launch traced here: 28.2 us
  starting transfers between devices  8.89 us (31%)
  waiting for transfers between devices  8.04 us (28%)
  local copies, waits for them, and re-layouts  3.83 us (13%)
  Pallas kernels  3.48 us (12%)
  other arithmetic  3.14 us (11%)
  between operations  0.79 us (3%)
    ppermute x4, starting transfers between devices, swapped(): got.append(lax.ppermute(block, axis, swap_pairs(count, parity, place)))  8.89 us
    ppermute x4, waiting for transfers between devices, swapped(): got.append(lax.ppermute(block, axis, swap_pairs(count, parity, place)))  8.04 us
    pallas_call x1, Pallas kernels, body(): pl.pallas_call(level_kernel, out_shape=(out, out), in_specs=[pl.BlockSpec...  3.48 us
    unnamed x8, local copies, waits for them, and re-layouts  1.5 us
    add x2, other arithmetic, wrapped_rows(): return (0.5 + jnp.roll(window, -lead)).reshape(count, 1)  1.25 us
    slice x7, local copies, waits for them, and re-layouts, both(): return jnp.stack([friction[part], height[part]])  1.19 us
    concatenate x1, other arithmetic, halo_frames(): jnp.concatenate([east, jnp.zeros((fields, FINE_SHAPE[0], gap_cols), frict...  0.71 us
    convert_element_type x1, other arithmetic, body(): flags = jnp.stack([row_index == 0, row_index == lax.axis_size('row') - 1,...  0.67 us
  transfers between devices with their start and end apart: 4, of which 1 were waited for; matrix products, arithmetic and copies ran while one was open for 14% of the time, Pallas kernels for 0%

profile of v5, /device:TPU:192, one launch (start us, length us, event | category | flops | bytes accessed | tf_op | source)
XLA Modules:
  0.0 28.2 jit_solution(11366866366627425409)
XLA Ops:
  0.6 0.8 %fusion.6 = (f32[1,2,256]{2,1,0:T(2,128)S(1)}, f32[1,2,256]{2,1,0:T(2,128)S(1)}, f32[1,2,256]{2,1,0:T(2,128)S(1)}, f32[1,2,256]{2,1,0:T(2,128)S(1)}) fusion(f32[1,64,256]{2,1,0:T(8,128)} %friction_ref.1, f32[1,64,256]{2,1,0:T(8,128)} %height_ref.1), kind=kLoop, calls=%fused_computation.32 | loop fusion | bytes 16384 | tf_op jit(solution)/shard_map/slice | solution.py:53
  1.4 5.1 %collective-permute-start = (f32[2,2,256]{2,1,0:T(2,128)S(1)}, f32[2,2,256]{2,1,0:T(2,128)S(1)}, u32[]{:S(2)}, u32[]{:S(2)}) collective-permute-start(f32[2,2,256]{2,1,0:T(2,128)S(1)} %get-tuple-element.22), channel_id=1, source_target_pairs={{8,16},{16,8},{24,32},{32,24},{40,48},{48,40},{56,64},{64,56},{72,... | collective-permute-start | bytes 12296 | tf_op jit(solution)/shard_map/ppermute | solution.py:39
  6.5 0.1 collective-permute-start.1
  6.7 0.2 reshape.78
  6.9 0.2 fusion.1
  7.1 0.1 pad_dynamic-slice_fusion.1
  7.3 0.1 pad_dynamic-slice_fusion
  7.4 0.3 copy-done
  7.7 0.1 fusion.4
  7.8 0.1 copy.49
  7.9 0.7 %copy-done.1 = f32[1,64,256]{2,1,0:T(8,128)S(1)} copy-done((f32[1,64,256]{2,1,0:T(8,128)S(1)}, f32[1,64,256]{2,1,0:T(8,128)}, u32[]{:S(2)}) %copy-start.1) | copy-done | bytes 65560
  8.5 0.1 fusion.5
  8.6 0.1 copy.50
  8.8 0.1 pad_maximum_fusion.9
  8.9 0.1 copy.57
  9.0 0.6 %broadcast_add_fusion.1.coarse_inflow_ref = f32[40,1]{1,0:T(8,128)} fusion(f32[40,1]{1,0:T(8,128)S(1)} %copy.57), kind=kLoop, calls=%fused_computation.12 | loop fusion | flops 40 | bytes 320 | tf_op jit(solution)/shard_map/add | solution.py:80
  9.6 0.1 pad_maximum_fusion.8
  9.7 0.1 copy.55
  9.8 0.6 %broadcast_add_fusion.fine_inflow_ref = f32[72,1]{1,0:T(8,128)} fusion(f32[72,1]{1,0:T(8,128)S(1)} %copy.55), kind=kLoop, calls=%fused_computation.10 | loop fusion | flops 72 | bytes 576 | tf_op jit(solution)/shard_map/add | solution.py:80
  10.5 0.1 copy.51
  10.6 0.1 copy.54
  10.7 0.1 pad.26.clone
  10.8 0.1 pad_maximum_fusion.3.row_frame_ref
  10.9 0.1 fusion.8
  10.9 0.5 %copy-done.2 = f32[2,8,256]{2,1,0:T(8,128)} copy-done((f32[2,8,256]{2,1,0:T(8,128)}, f32[2,8,256]{2,1,0:T(8,128)S(1)}, u32[]{:S(2)}) %copy-start.2) | copy-done | bytes 16408
  11.5 3.5 %collective-permute-start.2 = (f32[2,72,2]{2,1,0:T(8,128)S(1)}, f32[2,72,2]{2,1,0:T(8,128)S(1)}, u32[]{:S(2)}, u32[]{:S(2)}) collective-permute-start(f32[2,72,2]{2,1,0:T(8,128)S(1)} %get-tuple-element.8), channel_id=1, source_target_pairs={{128,1},{1,128},{129,2},{2,129},{130,3},{3,130},{131,4},{4,131},{1... | collective-permute-start | bytes 3464 | tf_op jit(solution)/shard_map/ppermute | solution.py:39
  15.0 0.1 collective-permute-start.3
  15.2 0.7 %add_convert_fusion.flags_ref = s32[4]{0:T(128)} fusion(pred[1]{0:T(512)(128)(4,1)} %bitcast.3, pred[1]{0:T(512)(128)(4,1)} %bitcast.2, pred[1]{0:T(512)(128)(4,1)} %bitcast.1, pred[1]{0:T(512)(128)(4,1)} %bitcast), kind=kLoop, calls=%fused_computation.23 | loop fusion | flops 16 | bytes 20 | tf_op jit(solution)/shard_map/convert_element_type | solution.py:208
  15.8 0.1 pad.15.clone
  15.9 8.0 %collective-permute-done.2 = f32[2,72,2]{2,1,0:T(8,128)S(1)} collective-permute-done((f32[2,72,2]{2,1,0:T(8,128)S(1)}, f32[2,72,2]{2,1,0:T(8,128)S(1)}, u32[]{:S(2)}, u32[]{:S(2)}) %collective-permute-start.2) | collective-permute-done | bytes 1184 | tf_op jit(solution)/shard_map/ppermute | solution.py:39
  24.0 0.7 %pad_maximum_fusion.2.col_frame_ref = f32[2,72,128]{2,1,0:T(8,128)} fusion(f32[2,72,2]{2,1,0:T(8,128)S(1)} %get-tuple-element.7, f32[2,72,2]{2,1,0:T(8,128)S(1)} %get-tuple-element.6, f32[128]{0:T(128)S(1)} %pad.15.clone), kind=kLoop, calls=%fused_computation.5 | loop fusion | flops 36864 | bytes 76544 | tf_op jit(solution)/shard_map/concatenate | solution.py:71
  24.7 3.5 %shard_map.50 = (f32[3,32,128]{2,1,0:T(8,128)}, f32[3,32,128]{2,1,0:T(8,128)}) custom-call(s32[4]{0:T(128)} %add_convert_fusion.flags_ref, f32[1,64,256]{2,1,0:T(8,128)} %friction_ref.1, f32[1,64,256]{2,1,0:T(8,128)} %height_ref.1, f32[2,8,256]{2,1,0:T(8,128)} %copy-done.2, f32[2,72,128]{2,1,0:T(8,128)} %pad_maximum_fusion.2.col_frame_ref, ...), custom_call_target="tpu_custom_call" | custom-call | tf_op jit(solution)/shard_map/pallas_call | solution.py:220
  (22 shorter events, 0.4 us)
Async XLA Ops:
  1.4 5.2 %copy-start.3 = (f32[1024]{0:T(1024)S(1)}, f32[1024]{0:T(1024)}, u32[]{:S(2)}) copy-start(f32[1024]{0:T(1024)} %param.5) | copy-start | bytes 12292
  1.4 9.4 %collective-permute-start = (f32[2,2,256]{2,1,0:T(2,128)S(1)}, f32[2,2,256]{2,1,0:T(2,128)S(1)}, u32[]{:S(2)}, u32[]{:S(2)}) collective-permute-start(f32[2,2,256]{2,1,0:T(2,128)S(1)} %get-tuple-element.22), channel_id=1, source_target_pairs={{8,16},{16,8},{24,32},{32,24},{40,48},{48,40},{56,64},{64,56},{72,... | collective-permute-start | bytes 12296 | tf_op jit(solution)/shard_map/ppermute | solution.py:39
  6.5 4.2 %collective-permute-start.1 = (f32[2,2,256]{2,1,0:T(2,128)S(1)}, f32[2,2,256]{2,1,0:T(2,128)S(1)}, u32[]{:S(2)}, u32[]{:S(2)}) collective-permute-start(f32[2,2,256]{2,1,0:T(2,128)S(1)} %get-tuple-element.23), channel_id=1, source_target_pairs={{0,8},{8,0},{16,24},{24,16},{32,40},{40,32},{48,56},{56,48},{64,72... | collective-permute-start | bytes 12296 | tf_op jit(solution)/shard_map/ppermute | solution.py:39
  6.9 0.8 %copy-start = (f32[1,64,256]{2,1,0:T(8,128)S(1)}, f32[1,64,256]{2,1,0:T(8,128)}, u32[]{:S(2)}) copy-start(f32[1,64,256]{2,1,0:T(8,128)} %friction_ref.1) | copy-start | bytes 196612
  7.7 0.8 %copy-start.1 = (f32[1,64,256]{2,1,0:T(8,128)S(1)}, f32[1,64,256]{2,1,0:T(8,128)}, u32[]{:S(2)}) copy-start(f32[1,64,256]{2,1,0:T(8,128)} %height_ref.1) | copy-start | bytes 196612
  10.9 0.6 %copy-start.2 = (f32[2,8,256]{2,1,0:T(8,128)}, f32[2,8,256]{2,1,0:T(8,128)S(1)}, u32[]{:S(2)}) copy-start(f32[2,8,256]{2,1,0:T(8,128)S(1)} %pad_maximum_fusion.3.row_frame_ref) | copy-start | bytes 49156
  11.5 12.5 %collective-permute-start.2 = (f32[2,72,2]{2,1,0:T(8,128)S(1)}, f32[2,72,2]{2,1,0:T(8,128)S(1)}, u32[]{:S(2)}, u32[]{:S(2)}) collective-permute-start(f32[2,72,2]{2,1,0:T(8,128)S(1)} %get-tuple-element.8), channel_id=1, source_target_pairs={{128,1},{1,128},{129,2},{2,129},{130,3},{3,130},{131,4},{4,131},{1... | collective-permute-start | bytes 3464 | tf_op jit(solution)/shard_map/ppermute | solution.py:39
  15.0 8.9 %collective-permute-start.3 = (f32[2,72,2]{2,1,0:T(8,128)S(1)}, f32[2,72,2]{2,1,0:T(8,128)S(1)}, u32[]{:S(2)}, u32[]{:S(2)}) collective-permute-start(f32[2,72,2]{2,1,0:T(8,128)S(1)} %get-tuple-element.9), channel_id=1, source_target_pairs={{0,128},{128,0},{1,129},{129,1},{2,130},{130,2},{3,131},{131,3},{4... | collective-permute-start | bytes 3464 | tf_op jit(solution)/shard_map/ppermute | solution.py:39

commit v6 on v3

--- a/solution.py
+++ b/solution.py
@@ -37,28 +37,39 @@
         sends_last = odd if parity else jnp.logical_not(odd)
         block = jnp.where(sends_last, last, first)
         got.append(lax.ppermute(block, axis, swap_pairs(count, parity, place)))
+    return got
+
+
+def by_parity(got, odd):
     before = jnp.where(odd, got[0], got[1])
     after = jnp.where(odd, got[1], got[0])
     return before, after
 
 
-def with_halo(noise):
-    fields, count_rows, count_cols = noise.shape
+def halo_tiles(friction, height):
+    count_rows, count_cols = friction.shape
+    fields = 2
     strips = lax.axis_size("col") * lax.axis_size("level")
     strip = lax.axis_index("col") * lax.axis_size("level") + lax.axis_index("level")
-    rows = lax.axis_size("row")
-    west, east = swapped(
-        noise[:, :, :HALO], noise[:, :, -HALO:], strip, strips, ("level", "col"), strip_place
+    row_index = lax.axis_index("row")
+    tile_rows, tile_cols = 8, 128
+
+    def both(rows):
+        return jnp.stack([friction[rows], height[rows]])
+
+    row_got = swapped(
+        both(slice(0, tile_rows)), both(slice(count_rows - tile_rows, count_rows)),
+        row_index, lax.axis_size("row"), "row",
     )
-    gap_cols = FINE_SHAPE[1] - count_cols - 2 * HALO
-    wide = jnp.concatenate(
-        [noise, east, jnp.zeros((fields, count_rows, gap_cols), noise.dtype), west], axis=2
+    north, south = by_parity(row_got, row_index % 2 == 1)
+    sub_at = lax.broadcasted_iota(jnp.int32, (fields, tile_rows, count_cols), 1)
+    row_frame = jnp.where(sub_at < tile_rows // 2, south, north)
+    tall = jnp.concatenate([jnp.stack([friction, height]), row_frame], axis=1)
+    col_got = swapped(
+        tall[:, :, :tile_cols], tall[:, :, count_cols - tile_cols:],
+        strip, strips, ("level", "col"), strip_place,
     )
-    north, south = swapped(wide[:, :HALO], wide[:, -HALO:], lax.axis_index("row"), rows, "row")
-    gap_rows = FINE_SHAPE[0] - count_rows - 2 * HALO
-    return jnp.concatenate(
-        [wide, south, jnp.zeros((fields, gap_rows, FINE_SHAPE[1]), noise.dtype), north], axis=1
-    )
+    return row_got, col_got
 
 
 def wrapped_rows(values, start, count, lead):
@@ -144,15 +155,31 @@
     return jnp.dot(a, b, precision=lax.Precision.HIGHEST, preferred_element_type=jnp.float32)
 
 
-def level_kernel(flags_ref, noise_ref, fine_inflow_ref, coarse_inflow_ref, mean_ref, corr_ref):
+def level_kernel(
+    flags_ref, friction_ref, height_ref, row_first_ref, row_second_ref, col_first_ref,
+    col_second_ref, fine_inflow_ref, coarse_inflow_ref, mean_ref, corr_ref,
+):
     flags = [flags_ref[i] for i in range(4)]
+    odd_row = flags_ref[4] == 1
+    odd_strip = flags_ref[5] == 1
+
+    def framed(center_ref, field):
+        north, south = by_parity((row_first_ref[field], row_second_ref[field]), odd_row)
+        sub_at = lax.broadcasted_iota(jnp.int32, north.shape, 0)
+        tall = jnp.concatenate(
+            [center_ref[0], jnp.where(sub_at < north.shape[0] // 2, south, north)], axis=0
+        )
+        west, east = by_parity((col_first_ref[field], col_second_ref[field]), odd_strip)
+        lane_at = lax.broadcasted_iota(jnp.int32, east.shape, 1)
+        return jnp.concatenate([tall, jnp.where(lane_at < east.shape[1] // 2, east, west)], axis=1)
+
     fine_rows, fine_cols = FINE_SHAPE
     coarse_rows, coarse_cols = COARSE_SHAPE
     out_rows, out_cols = mean_ref.shape[1], mean_ref.shape[2]
     tile_rows, tile_cols = 2 * out_rows, 2 * out_cols
 
-    fine_coef = noise_ref[0]
-    noise_height = noise_ref[1]
+    fine_coef = framed(friction_ref, 0)
+    noise_height = framed(height_ref, 1)
     depth = 1.0 + 0.1 * noise_height
     state = (depth, 0.5 * depth, jnp.zeros_like(depth))
     fine_inflow = jnp.broadcast_to(fine_inflow_ref[...], FINE_SHAPE)
@@ -183,12 +210,13 @@
     strips = lax.axis_size("col") * lax.axis_size("level")
     row_index = lax.axis_index("row")
     flags = jnp.stack(
-        [row_index == 0, row_index == lax.axis_size("row") - 1, strip == 0, strip == strips - 1]
+        [row_index == 0, row_index == lax.axis_size("row") - 1, strip == 0, strip == strips - 1,
+         row_index % 2 == 1, strip % 2 == 1]
     ).astype(jnp.int32)
     tile_rows, tile_cols = friction.shape[1], friction.shape[2]
     out_rows, out_cols = tile_rows // 2, tile_cols // 2
 
-    noise = with_halo(jnp.concatenate([friction, height], axis=0))
+    row_got, col_got = halo_tiles(friction[0], height[0])
     lead = FINE_SHAPE[0] - tile_rows - HALO
     fine_inflow = wrapped_rows(inflow, row_index * tile_rows, FINE_SHAPE[0], lead)
     lead = COARSE_SHAPE[0] - out_rows - 1
@@ -199,9 +227,9 @@
     mean, corr = pl.pallas_call(
         level_kernel,
         out_shape=(out, out),
-        in_specs=[pl.BlockSpec(memory_space=pltpu.SMEM), vmem, vmem, vmem],
+        in_specs=[pl.BlockSpec(memory_space=pltpu.SMEM)] + [vmem] * 8,
         out_specs=(vmem, vmem),
-    )(flags, noise, fine_inflow, coarse_inflow)
+    )(flags, friction, height, *row_got, *col_got, fine_inflow, coarse_inflow)
     return (mean[None], corr[None])
 
 

time: 27.1 us -> 28.5 us (1.052)
  the two profiles are of different devices: /device:TPU:192 before, /device:TPU:57 now
where the time goes in v6:
time: 28.5 us; the launch traced here: 28.2 us
  starting transfers between devices  14.4 us (51%)
  waiting for transfers between devices  4.51 us (16%)
  Pallas kernels  3.6 us (13%)
  local copies, waits for them, and re-layouts  2.74 us (10%)
  other arithmetic  2.25 us (8%)
  between operations  0.72 us (3%)
    ppermute x4, starting transfers between devices, swapped(): got.append(lax.ppermute(block, axis, swap_pairs(count, parity, place)))  14.4 us
    ppermute x4, waiting for transfers between devices, swapped(): got.append(lax.ppermute(block, axis, swap_pairs(count, parity, place)))  4.51 us
    pallas_call x1, Pallas kernels, body(): pl.pallas_call(level_kernel, out_shape=(out, out), in_specs=[pl.BlockSpec...  3.6 us
    add x2, other arithmetic, wrapped_rows(): return (0.5 + jnp.roll(window, -lead)).reshape(count, 1)  1.21 us
    unnamed x14, local copies, waits for them, and re-layouts  1.17 us
    slice x1, local copies, waits for them, and re-layouts, both(): return jnp.stack([friction[rows], height[rows]])  0.75 us
  transfers between devices with their start and end apart: 4, of which 2 were waited for; matrix products, arithmetic and copies ran while one was open for 10% of the time, Pallas kernels for 0%

profile of v6, /device:TPU:57, one launch (start us, length us, event | category | flops | bytes accessed | tf_op | source)
XLA Modules:
  0.0 28.2 jit_solution(11263189393243574855)
XLA Ops:
  0.6 0.8 %fusion.4 = (f32[1,8,256]{2,1,0:T(8,128)S(1)}, f32[1,8,256]{2,1,0:T(8,128)S(1)}, f32[1,8,256]{2,1,0:T(8,128)S(1)}, f32[1,8,256]{2,1,0:T(8,128)S(1)}) fusion(f32[1,64,256]{2,1,0:T(8,128)} %friction_ref.1, f32[1,64,256]{2,1,0:T(8,128)} %height_ref.1), kind=kLoop, calls=%fused_computation.22 | loop fusion | bytes 65536 | tf_op jit(solution)/shard_map/slice | solution.py:58
  1.4 1.3 %collective-permute-start = (f32[2,8,256]{2,1,0:T(8,128)S(1)}, f32[2,8,256]{2,1,0:T(8,128)S(1)}, u32[]{:S(2)}, u32[]{:S(2)}) collective-permute-start(f32[2,8,256]{2,1,0:T(8,128)S(1)} %get-tuple-element.13), channel_id=1, source_target_pairs={{0,8},{8,0},{16,24},{24,16},{32,40},{40,32},{48,56},{56,48},{64,72... | collective-permute-start | bytes 49160 | tf_op jit(solution)/shard_map/ppermute | solution.py:39
  2.7 3.4 %collective-permute-start.1 = (f32[2,8,256]{2,1,0:T(8,128)S(1)}, f32[2,8,256]{2,1,0:T(8,128)S(1)}, u32[]{:S(2)}, u32[]{:S(2)}) collective-permute-start(f32[2,8,256]{2,1,0:T(8,128)S(1)} %get-tuple-element.12), channel_id=1, source_target_pairs={{8,16},{16,8},{24,32},{32,24},{40,48},{48,40},{56,64},{64,56},{72,... | collective-permute-start | bytes 49160 | tf_op jit(solution)/shard_map/ppermute | solution.py:39
  6.1 0.0 copy-done.6
  6.1 0.2 reshape.78
  6.3 0.2 fusion.1
  6.6 0.1 pad_dynamic-slice_fusion.1
  6.7 0.1 slice_bitcast_fusion.1
  6.7 0.1 pad_dynamic-slice_fusion
  6.8 0.1 slice_bitcast_fusion.3
  6.9 0.1 pad_maximum_fusion.3
  7.0 0.1 copy.15
  7.1 0.6 %broadcast_add_fusion.fine_inflow_ref = f32[72,1]{1,0:T(8,128)} fusion(f32[72,1]{1,0:T(8,128)S(1)} %copy.15), kind=kLoop, calls=%fused_computation.6 | loop fusion | flops 72 | bytes 576 | tf_op jit(solution)/shard_map/add | solution.py:78
  7.7 0.1 pad_maximum_fusion.4
  7.8 0.1 copy.17
  7.8 0.0 collective-permute-done.row_first_ref
  7.9 1.6 %collective-permute-done.1.row_second_ref = f32[2,8,256]{2,1,0:T(8,128)S(1)} collective-permute-done((f32[2,8,256]{2,1,0:T(8,128)S(1)}, f32[2,8,256]{2,1,0:T(8,128)S(1)}, u32[]{:S(2)}, u32[]{:S(2)}) %collective-permute-start.1) | collective-permute-done | bytes 16416 | tf_op jit(solution)/shard_map/ppermute | solution.py:39
  9.4 0.1 select_select_fusion
  9.5 0.0 copy-done.4
  9.5 0.5 %copy-done.5 = f32[2,8,256]{2,1,0:T(8,128)} copy-done((f32[2,8,256]{2,1,0:T(8,128)}, f32[2,8,256]{2,1,0:T(8,128)S(1)}, u32[]{:S(2)}) %copy-start.5) | copy-done | bytes 16408
  10.0 0.0 copy-done.1
  10.0 0.0 copy-done
  10.1 2.2 %collective-permute-start.2 = (f32[2,72,128]{2,1,0:T(8,128)S(1)}, f32[2,72,128]{2,1,0:T(8,128)S(1)}, u32[]{:S(2)}, u32[]{:S(2)}) collective-permute-start(f32[2,72,128]{2,1,0:T(8,128)S(1)} %get-tuple-element.7), channel_id=1, source_target_pairs={{0,128},{128,0},{1,129},{129,1},{2,130},{130,2},{3,131},{131,3},{4... | collective-permute-start | bytes 221192 | tf_op jit(solution)/shard_map/ppermute | solution.py:39
  12.3 7.5 %collective-permute-start.3 = (f32[2,72,128]{2,1,0:T(8,128)S(1)}, f32[2,72,128]{2,1,0:T(8,128)S(1)}, u32[]{:S(2)}, u32[]{:S(2)}) collective-permute-start(f32[2,72,128]{2,1,0:T(8,128)S(1)} %get-tuple-element.6), channel_id=1, source_target_pairs={{128,1},{1,128},{129,2},{2,129},{130,3},{3,130},{131,4},{4,131},{1... | collective-permute-start | bytes 221192 | tf_op jit(solution)/shard_map/ppermute | solution.py:39
  19.7 0.6 %broadcast_add_fusion.1.coarse_inflow_ref = f32[40,1]{1,0:T(8,128)} fusion(f32[40,1]{1,0:T(8,128)S(1)} %copy.17), kind=kLoop, calls=%fused_computation.12 | loop fusion | flops 40 | bytes 320 | tf_op jit(solution)/shard_map/add | solution.py:78
  20.3 0.1 stack.40
  20.4 0.5 %convert_element_type.7.flags_ref = s32[6]{0:T(128)} convert(pred[6]{0:T(512)(128)(4,1)S(1)} %stack.40) | non-fusion elementwise | flops 6 | bytes 30 | tf_op jit(solution)/shard_map/convert_element_type | solution.py:215
  21.0 0.0 collective-permute-done.2.col_first_ref
  21.0 2.9 %collective-permute-done.3.col_second_ref = f32[2,72,128]{2,1,0:T(8,128)S(1)} collective-permute-done((f32[2,72,128]{2,1,0:T(8,128)S(1)}, f32[2,72,128]{2,1,0:T(8,128)S(1)}, u32[]{:S(2)}, u32[]{:S(2)}) %collective-permute-start.3) | collective-permute-done | bytes 73760 | tf_op jit(solution)/shard_map/ppermute | solution.py:39
  23.9 0.0 copy-done.2
  23.9 0.6 %copy-done.3 = f32[2,72,128]{2,1,0:T(8,128)} copy-done((f32[2,72,128]{2,1,0:T(8,128)}, f32[2,72,128]{2,1,0:T(8,128)S(1)}, u32[]{:S(2)}) %copy-start.3) | copy-done | bytes 73752
  24.6 3.6 %shard_map.50 = (f32[3,32,128]{2,1,0:T(8,128)}, f32[3,32,128]{2,1,0:T(8,128)}) custom-call(s32[6]{0:T(128)} %convert_element_type.7.flags_ref, f32[1,64,256]{2,1,0:T(8,128)} %friction_ref.1, f32[1,64,256]{2,1,0:T(8,128)} %height_ref.1, f32[2,8,256]{2,1,0:T(8,128)} %copy-done.4, f32[2,8,256]{2,1,0:T(8,128)} %copy-done.5, f32[2,72,128]{2,1,0:T(8,128)} %copy-done.2, ...), custom_call_target="tpu_custom_call" | custom-call | tf_op jit(solution)/shard_map/pallas_call | solution.py:227
  (13 shorter events, 0.1 us)
Async XLA Ops:
  1.4 6.4 %collective-permute-start = (f32[2,8,256]{2,1,0:T(8,128)S(1)}, f32[2,8,256]{2,1,0:T(8,128)S(1)}, u32[]{:S(2)}, u32[]{:S(2)}) collective-permute-start(f32[2,8,256]{2,1,0:T(8,128)S(1)} %get-tuple-element.13), channel_id=1, source_target_pairs={{0,8},{8,0},{16,24},{24,16},{32,40},{40,32},{48,56},{56,48},{64,72... | collective-permute-start | bytes 49160 | tf_op jit(solution)/shard_map/ppermute | solution.py:39
  2.7 3.4 %copy-start.6 = (f32[1024]{0:T(1024)S(1)}, f32[1024]{0:T(1024)}, u32[]{:S(2)}) copy-start(f32[1024]{0:T(1024)} %param.5) | copy-start | bytes 12292
  2.7 6.7 %collective-permute-start.1 = (f32[2,8,256]{2,1,0:T(8,128)S(1)}, f32[2,8,256]{2,1,0:T(8,128)S(1)}, u32[]{:S(2)}, u32[]{:S(2)}) collective-permute-start(f32[2,8,256]{2,1,0:T(8,128)S(1)} %get-tuple-element.12), channel_id=1, source_target_pairs={{8,16},{16,8},{24,32},{32,24},{40,48},{48,40},{56,64},{64,56},{72,... | collective-permute-start | bytes 49160 | tf_op jit(solution)/shard_map/ppermute | solution.py:39
  7.1 3.0 %copy-start.1 = (f32[1,64,256]{2,1,0:T(8,128)S(1)}, f32[1,64,256]{2,1,0:T(8,128)}, u32[]{:S(2)}) copy-start(f32[1,64,256]{2,1,0:T(8,128)} %height_ref.1) | copy-start | bytes 196612
  7.7 2.3 %copy-start = (f32[1,64,256]{2,1,0:T(8,128)S(1)}, f32[1,64,256]{2,1,0:T(8,128)}, u32[]{:S(2)}) copy-start(f32[1,64,256]{2,1,0:T(8,128)} %friction_ref.1) | copy-start | bytes 196612
  7.8 1.6 %copy-start.4 = (f32[2,8,256]{2,1,0:T(8,128)}, f32[2,8,256]{2,1,0:T(8,128)S(1)}, u32[]{:S(2)}) copy-start(f32[2,8,256]{2,1,0:T(8,128)S(1)} %collective-permute-done.row_first_ref) | copy-start | bytes 49156
  9.4 0.6 %copy-start.5 = (f32[2,8,256]{2,1,0:T(8,128)}, f32[2,8,256]{2,1,0:T(8,128)S(1)}, u32[]{:S(2)}) copy-start(f32[2,8,256]{2,1,0:T(8,128)S(1)} %collective-permute-done.1.row_second_ref) | copy-start | bytes 49156
  10.1 10.9 %collective-permute-start.2 = (f32[2,72,128]{2,1,0:T(8,128)S(1)}, f32[2,72,128]{2,1,0:T(8,128)S(1)}, u32[]{:S(2)}, u32[]{:S(2)}) collective-permute-start(f32[2,72,128]{2,1,0:T(8,128)S(1)} %get-tuple-element.7), channel_id=1, source_target_pairs={{0,128},{128,0},{1,129},{129,1},{2,130},{130,2},{3,131},{131,3},{4... | collective-permute-start | bytes 221192 | tf_op jit(solution)/shard_map/ppermute | solution.py:39
  12.3 11.7 %collective-permute-start.3 = (f32[2,72,128]{2,1,0:T(8,128)S(1)}, f32[2,72,128]{2,1,0:T(8,128)S(1)}, u32[]{:S(2)}, u32[]{:S(2)}) collective-permute-start(f32[2,72,128]{2,1,0:T(8,128)S(1)} %get-tuple-element.6), channel_id=1, source_target_pairs={{128,1},{1,128},{129,2},{2,129},{130,3},{3,130},{131,4},{4,131},{1... | collective-permute-start | bytes 221192 | tf_op jit(solution)/shard_map/ppermute | solution.py:39
  21.0 2.9 %copy-start.2 = (f32[2,72,128]{2,1,0:T(8,128)}, f32[2,72,128]{2,1,0:T(8,128)S(1)}, u32[]{:S(2)}) copy-start(f32[2,72,128]{2,1,0:T(8,128)S(1)} %collective-permute-done.2.col_first_ref) | copy-start | bytes 221188
  23.9 0.6 %copy-start.3 = (f32[2,72,128]{2,1,0:T(8,128)}, f32[2,72,128]{2,1,0:T(8,128)S(1)}, u32[]{:S(2)}) copy-start(f32[2,72,128]{2,1,0:T(8,128)S(1)} %collective-permute-done.3.col_second_ref) | copy-start | bytes 221188

commit v7 on v4

--- a/solution.py
+++ b/solution.py
@@ -132,6 +132,35 @@
     return (depth, moved[1] * damping, moved[2] * damping)
 
 
+def walls_at_rest(state, flags, inflow_speed, bottom_row, right_col):
+    depth, along_cols, _ = state
+    depth, along_cols, _ = apply_walls(
+        (depth, along_cols, depth), flags, inflow_speed, bottom_row, right_col
+    )
+    return (depth, along_cols, jnp.zeros_like(depth))
+
+
+def advance_at_rest(state, friction_coef, step):
+    depth, along_cols, _ = state
+    velocity = along_cols / depth
+    root = jnp.sqrt(depth)
+    flux = (along_cols, along_cols * velocity + 0.5 * depth * depth)
+    face_x = face_flux((depth, along_cols), flux, jnp.abs(velocity) + root, 1)
+    reach = 0.5 * jnp.maximum(next_of(root, 0), root)
+    face_y = [0.0 - reach * (next_of(u, 0) - u) for u in (depth, along_cols)]
+    pressure = 0.5 * depth * depth
+    pressure_face = 0.5 * (next_of(pressure, 0) + pressure)
+    moved = [
+        u - step_ratio * (fx - prev_of(fx, 1) + (fy - prev_of(fy, 0)))
+        for u, fx, fy in zip((depth, along_cols), face_x, face_y)
+    ]
+    moved.append(0.0 - step_ratio * (pressure_face - prev_of(pressure_face, 0)))
+    depth = moved[0]
+    speed = jnp.sqrt(moved[1] * moved[1] + moved[2] * moved[2]) / depth
+    damping = 1.0 / (1.0 + step * friction_coef * speed / depth)
+    return (depth, moved[1] * damping, moved[2] * damping)
+
+
 def pair_matrix(shape, out_axis, last_from):
     out_at = lax.broadcasted_iota(jnp.int32, shape, out_axis)
     in_at = lax.broadcasted_iota(jnp.int32, shape, 1 - out_axis)
@@ -158,9 +187,10 @@
     depth = 1.0 + 0.1 * noise_height
     state = (depth, 0.5 * depth, jnp.zeros_like(depth))
     fine_inflow = jnp.broadcast_to(fine_inflow_ref[...], FINE_SHAPE)
-    for _ in range(2):
-        state = apply_walls(state, flags, fine_inflow, tile_rows, tile_cols)
-        state = advance(state, fine_coef, fine_step)
+    state = walls_at_rest(state, flags, fine_inflow, tile_rows, tile_cols)
+    state = advance_at_rest(state, fine_coef, fine_step)
+    state = apply_walls(state, flags, fine_inflow, tile_rows, tile_cols)
+    state = advance(state, fine_coef, fine_step)
 
     rows_sum = pair_matrix((coarse_rows, fine_rows), 0, fine_rows - 2)
     cols_sum = pair_matrix((fine_cols, coarse_cols), 1, fine_cols - 2)
@@ -168,8 +198,8 @@
     depth = 1.0 + 0.1 * (matmul(matmul(rows_sum, noise_height), cols_sum) * 0.25)
     coarse = (depth, 0.5 * depth, jnp.zeros_like(depth))
     coarse_inflow = jnp.broadcast_to(coarse_inflow_ref[...], COARSE_SHAPE)
-    coarse = apply_walls(coarse, flags, coarse_inflow, out_rows, out_cols)
-    coarse = advance(coarse, coarse_coef, coarse_step)
+    coarse = walls_at_rest(coarse, flags, coarse_inflow, out_rows, out_cols)
+    coarse = advance_at_rest(coarse, coarse_coef, coarse_step)
 
     rows_out = pair_matrix((out_rows, tile_rows), 0, None)
     cols_out = pair_matrix((tile_cols, out_cols), 1, None)

time: 26.9 us -> 26.8 us (level)
  no operation moved by 1% of the time
where the time goes in v7:
time: 26.8 us; the launch traced here: 26.6 us
  starting transfers between devices  8.89 us (33%)
  waiting for transfers between devices  8.72 us (33%)
  Pallas kernels  3.38 us (13%)
  other arithmetic  3.17 us (12%)
  local copies, waits for them, and re-layouts  1.68 us (6%)
  between operations  0.75 us (3%)
    ppermute x4, starting transfers between devices, swapped(): got.append(lax.ppermute(block, axis, swap_pairs(count, parity, place)))  8.89 us
    ppermute x4, waiting for transfers between devices, swapped(): got.append(lax.ppermute(block, axis, swap_pairs(count, parity, place)))  8.72 us
    pallas_call x1, Pallas kernels, body(): pl.pallas_call(level_kernel, out_shape=(out, out), in_specs=[pl.BlockSpec...  3.38 us
    add x2, other arithmetic, wrapped_rows(): return (0.5 + jnp.roll(window, -lead)).reshape(count, 1)  1.22 us
    unnamed x5, local copies, waits for them, and re-layouts  0.89 us
    concatenate x1, other arithmetic, with_halo(): jnp.concatenate([tall, east, jnp.zeros((fields, FINE_SHAPE[0], gap_cols),...  0.78 us
    convert_element_type x1, other arithmetic, body(): flags = jnp.stack([row_index == 0, row_index == lax.axis_size('row') - 1,...  0.65 us
  transfers between devices with their start and end apart: 4, of which 3 were waited for; matrix products, arithmetic and copies ran while one was open for 11% of the time, Pallas kernels for 0%

profile of v7, /device:TPU:192, one launch (start us, length us, event | category | flops | bytes accessed | tf_op | source)
XLA Modules:
  0.0 26.6 jit_solution(7847345292613999381)
XLA Ops:
  0.6 0.0 copy-start
  0.7 0.9 %constant_dynamic-update-slice_fusion.1 = f32[2,64,256]{2,1,0:T(8,128)S(1)} fusion(f32[1,64,256]{2,1,0:T(8,128)} %param.3), kind=kLoop, calls=%fused_computation.13 | loop fusion | bytes 131072
  1.5 0.0 copy-done
  1.6 0.0 copy-start.1
  1.6 5.1 %collective-permute-start = (f32[2,2,256]{2,1,0:T(2,128)S(1)}, f32[2,2,256]{2,1,0:T(2,128)S(1)}, u32[]{:S(2)}, u32[]{:S(2)}) collective-permute-start(f32[2,2,256]{2,1,0:T(2,128)S(1)} %get-tuple-element.10), channel_id=1, source_target_pairs={{8,16},{16,8},{24,32},{32,24},{40,48},{48,40},{56,64},{64,56},{72,... | collective-permute-start | bytes 12296 | tf_op jit(solution)/shard_map/ppermute | solution.py:39
  6.7 0.1 collective-permute-start.1
  6.8 0.0 copy-done.1
  6.8 0.2 reshape.70
  7.0 0.2 fusion.1
  7.2 0.1 pad_dynamic-slice_fusion.1
  7.3 0.1 slice_bitcast_fusion.1
  7.4 0.1 pad_dynamic-slice_fusion
  7.5 0.1 slice_bitcast_fusion.3
  7.6 0.1 pad_maximum_fusion.3
  7.6 0.1 copy.17
  7.7 0.1 pad_maximum_fusion.2
  7.8 0.1 copy.15
  7.9 0.6 %broadcast_add_fusion.fine_inflow_ref = f32[72,1]{1,0:T(8,128)} fusion(f32[72,1]{1,0:T(8,128)S(1)} %copy.15), kind=kLoop, calls=%fused_computation.9 | loop fusion | flops 72 | bytes 576 | tf_op jit(solution)/shard_map/add | solution.py:69
  8.5 0.6 %broadcast_add_fusion.1.coarse_inflow_ref = f32[40,1]{1,0:T(8,128)} fusion(f32[40,1]{1,0:T(8,128)S(1)} %copy.17), kind=kLoop, calls=%fused_computation.10 | loop fusion | flops 40 | bytes 320 | tf_op jit(solution)/shard_map/add | solution.py:69
  9.1 0.1 collective-permute-done
  9.2 1.2 %collective-permute-done.1 = f32[2,2,256]{2,1,0:T(2,128)S(1)} collective-permute-done((f32[2,2,256]{2,1,0:T(2,128)S(1)}, f32[2,2,256]{2,1,0:T(2,128)S(1)}, u32[]{:S(2)}, u32[]{:S(2)}) %collective-permute-start.1) | collective-permute-done | bytes 4128 | tf_op jit(solution)/shard_map/ppermute | solution.py:39
  10.4 0.1 slice_select_fusion.1
  10.5 2.3 %collective-permute-start.2 = (f32[2,72,2]{2,1,0:T(8,128)S(1)}, f32[2,72,2]{2,1,0:T(8,128)S(1)}, u32[]{:S(2)}, u32[]{:S(2)}) collective-permute-start(f32[2,72,2]{2,1,0:T(8,128)S(1)} %get-tuple-element.8), channel_id=1, source_target_pairs={{128,1},{1,128},{129,2},{2,129},{130,3},{3,130},{131,4},{4,131},{1... | collective-permute-start | bytes 3464 | tf_op jit(solution)/shard_map/ppermute | solution.py:39
  12.8 1.4 %collective-permute-start.3 = (f32[2,72,2]{2,1,0:T(8,128)S(1)}, f32[2,72,2]{2,1,0:T(8,128)S(1)}, u32[]{:S(2)}, u32[]{:S(2)}) collective-permute-start(f32[2,72,2]{2,1,0:T(8,128)S(1)} %get-tuple-element.9), channel_id=1, source_target_pairs={{0,128},{128,0},{1,129},{129,1},{2,130},{130,2},{3,131},{131,3},{4... | collective-permute-start | bytes 3464 | tf_op jit(solution)/shard_map/ppermute | solution.py:39
  14.2 0.7 %add_convert_fusion.flags_ref = s32[4]{0:T(128)} fusion(pred[1]{0:T(512)(128)(4,1)} %bitcast.3, pred[1]{0:T(512)(128)(4,1)} %bitcast.2, pred[1]{0:T(512)(128)(4,1)} %bitcast.1, pred[1]{0:T(512)(128)(4,1)} %bitcast), kind=kLoop, calls=%fused_computation.19 | loop fusion | flops 16 | bytes 20 | tf_op jit(solution)/shard_map/convert_element_type | solution.py:219
  14.9 0.1 pad.19.clone
  14.9 7.5 %collective-permute-done.2 = f32[2,72,2]{2,1,0:T(8,128)S(1)} collective-permute-done((f32[2,72,2]{2,1,0:T(8,128)S(1)}, f32[2,72,2]{2,1,0:T(8,128)S(1)}, u32[]{:S(2)}, u32[]{:S(2)}) %collective-permute-start.2) | collective-permute-done | bytes 1184 | tf_op jit(solution)/shard_map/ppermute | solution.py:39
  22.4 0.0 collective-permute-done.3
  22.4 0.8 %pad_maximum_fusion.noise_ref = f32[2,72,384]{2,1,0:T(8,128)} fusion(f32[2,72,2]{2,1,0:T(8,128)S(1)} %get-tuple-element.7, f32[2,72,2]{2,1,0:T(8,128)S(1)} %get-tuple-element.6, f32[2,2,256]{2,1,0:T(2,128)S(1)} %get-tuple-element.13, f32[2,4,256]{2,1,0:T(4,128)S(1)} %broadcast_in_dim.12, f32[2,2,256]{2,1,0:T(2,128)S(1)} %get-tuple-element.12, ...), kind=kLoop, calls=%fused_computation.3 | loop fusion | flops 331776 | bytes 372480 | tf_op jit(solution)/shard_map/concatenate | solution.py:61
  23.2 3.4 %shard_map.50 = (f32[3,32,128]{2,1,0:T(8,128)}, f32[3,32,128]{2,1,0:T(8,128)}) custom-call(s32[4]{0:T(128)} %add_convert_fusion.flags_ref, f32[2,72,384]{2,1,0:T(8,128)} %pad_maximum_fusion.noise_ref, f32[72,1]{1,0:T(8,128)} %broadcast_add_fusion.fine_inflow_ref, f32[40,1]{1,0:T(8,128)} %broadcast_add_fusion.1.coarse_inflow_ref), custom_call_target="tpu_custom_call" | custom-call | tf_op jit(solution)/shard_map/pallas_call | solution.py:231
  (9 shorter events, 0.1 us)
Async XLA Ops:
  0.6 0.9 %copy-start = (f32[1,64,256]{2,1,0:T(8,128)S(1)}, f32[1,64,256]{2,1,0:T(8,128)}, u32[]{:S(2)}) copy-start(f32[1,64,256]{2,1,0:T(8,128)} %param.4) | copy-start | bytes 196612
  1.6 5.2 %copy-start.1 = (f32[1024]{0:T(1024)S(1)}, f32[1024]{0:T(1024)}, u32[]{:S(2)}) copy-start(f32[1024]{0:T(1024)} %param.5) | copy-start | bytes 12292
  1.6 7.6 %collective-permute-start = (f32[2,2,256]{2,1,0:T(2,128)S(1)}, f32[2,2,256]{2,1,0:T(2,128)S(1)}, u32[]{:S(2)}, u32[]{:S(2)}) collective-permute-start(f32[2,2,256]{2,1,0:T(2,128)S(1)} %get-tuple-element.10), channel_id=1, source_target_pairs={{8,16},{16,8},{24,32},{32,24},{40,48},{48,40},{56,64},{64,56},{72,... | collective-permute-start | bytes 12296 | tf_op jit(solution)/shard_map/ppermute | solution.py:39
  6.7 3.7 %collective-permute-start.1 = (f32[2,2,256]{2,1,0:T(2,128)S(1)}, f32[2,2,256]{2,1,0:T(2,128)S(1)}, u32[]{:S(2)}, u32[]{:S(2)}) collective-permute-start(f32[2,2,256]{2,1,0:T(2,128)S(1)} %get-tuple-element.11), channel_id=1, source_target_pairs={{0,8},{8,0},{16,24},{24,16},{32,40},{40,32},{48,56},{56,48},{64,72... | collective-permute-start | bytes 12296 | tf_op jit(solution)/shard_map/ppermute | solution.py:39
  10.5 11.9 %collective-permute-start.2 = (f32[2,72,2]{2,1,0:T(8,128)S(1)}, f32[2,72,2]{2,1,0:T(8,128)S(1)}, u32[]{:S(2)}, u32[]{:S(2)}) collective-permute-start(f32[2,72,2]{2,1,0:T(8,128)S(1)} %get-tuple-element.8), channel_id=1, source_target_pairs={{128,1},{1,128},{129,2},{2,129},{130,3},{3,130},{131,4},{4,131},{1... | collective-permute-start | bytes 3464 | tf_op jit(solution)/shard_map/ppermute | solution.py:39
  12.8 9.6 %collective-permute-start.3 = (f32[2,72,2]{2,1,0:T(8,128)S(1)}, f32[2,72,2]{2,1,0:T(8,128)S(1)}, u32[]{:S(2)}, u32[]{:S(2)}) collective-permute-start(f32[2,72,2]{2,1,0:T(8,128)S(1)} %get-tuple-element.9), channel_id=1, source_target_pairs={{0,128},{128,0},{1,129},{129,1},{2,130},{130,2},{3,131},{131,3},{4... | collective-permute-start | bytes 3464 | tf_op jit(solution)/shard_map/ppermute | solution.py:39

commit v8 on v7

--- a/solution.py
+++ b/solution.py
@@ -194,8 +194,10 @@
 
     rows_sum = pair_matrix((coarse_rows, fine_rows), 0, fine_rows - 2)
     cols_sum = pair_matrix((fine_cols, coarse_cols), 1, fine_cols - 2)
-    coarse_coef = matmul(matmul(rows_sum, fine_coef), cols_sum) * 0.25
-    depth = 1.0 + 0.1 * (matmul(matmul(rows_sum, noise_height), cols_sum) * 0.25)
+    paired = matmul(rows_sum, jnp.concatenate([fine_coef, noise_height], axis=1))
+    small = matmul(jnp.concatenate([paired[:, :fine_cols], paired[:, fine_cols:]], axis=0), cols_sum)
+    coarse_coef = small[:coarse_rows] * 0.25
+    depth = 1.0 + 0.1 * (small[coarse_rows:] * 0.25)
     coarse = (depth, 0.5 * depth, jnp.zeros_like(depth))
     coarse_inflow = jnp.broadcast_to(coarse_inflow_ref[...], COARSE_SHAPE)
     coarse = walls_at_rest(coarse, flags, coarse_inflow, out_rows, out_cols)
@@ -203,9 +205,15 @@
 
     rows_out = pair_matrix((out_rows, tile_rows), 0, None)
     cols_out = pair_matrix((tile_cols, out_cols), 1, None)
+    paired = matmul(
+        rows_out, jnp.concatenate([values[:tile_rows, :tile_cols] for values in state], axis=1)
+    )
+    stacked = jnp.concatenate(
+        [paired[:, field * tile_cols: (field + 1) * tile_cols] for field in range(3)], axis=0
+    )
+    means = matmul(stacked, cols_out)
     for field in range(3):
-        fine_part = state[field][:tile_rows, :tile_cols]
-        mean = matmul(matmul(rows_out, fine_part), cols_out) * 0.25
+        mean = means[field * out_rows: (field + 1) * out_rows] * 0.25
         mean_ref[field] = mean
         corr_ref[field] = mean - coarse[field][:out_rows, :out_cols]
 

time: 26.8 us -> 26.5 us (0.989)
  transfers between devices with their start and end apart: 4 -> 4, of which waited for: 3 -> 3; matrix products, arithmetic and copies ran while one was open for 11% -> 12% of each run, Pallas kernels for 0% -> 0%
where the time goes in v8:
time: 26.5 us; the launch traced here: 26.3 us
  starting transfers between devices  8.89 us (34%)
  waiting for transfers between devices  8.72 us (33%)
  other arithmetic  3.17 us (12%)
  Pallas kernels  3.12 us (12%)
  local copies, waits for them, and re-layouts  1.68 us (6%)
  between operations  0.75 us (3%)
    ppermute x4, starting transfers between devices, swapped(): got.append(lax.ppermute(block, axis, swap_pairs(count, parity, place)))  8.89 us
    ppermute x4, waiting for transfers between devices, swapped(): got.append(lax.ppermute(block, axis, swap_pairs(count, parity, place)))  8.72 us
    pallas_call x1, Pallas kernels, body(): pl.pallas_call(level_kernel, out_shape=(out, out), in_specs=[pl.BlockSpec...  3.12 us
    add x2, other arithmetic, wrapped_rows(): return (0.5 + jnp.roll(window, -lead)).reshape(count, 1)  1.22 us
    unnamed x5, local copies, waits for them, and re-layouts  0.89 us
    concatenate x1, other arithmetic, with_halo(): jnp.concatenate([tall, east, jnp.zeros((fields, FINE_SHAPE[0], gap_cols),...  0.78 us
    convert_element_type x1, other arithmetic, body(): flags = jnp.stack([row_index == 0, row_index == lax.axis_size('row') - 1,...  0.65 us
  transfers between devices with their start and end apart: 4, of which 3 were waited for; matrix products, arithmetic and copies ran while one was open for 12% of the time, Pallas kernels for 0%

profile of v8, /device:TPU:192, one launch (start us, length us, event | category | flops | bytes accessed | tf_op | source)
XLA Modules:
  0.0 26.3 jit_solution(15479642748101281850)
XLA Ops:
  0.6 0.0 copy-start
  0.7 0.9 %constant_dynamic-update-slice_fusion.1 = f32[2,64,256]{2,1,0:T(8,128)S(1)} fusion(f32[1,64,256]{2,1,0:T(8,128)} %param.3), kind=kLoop, calls=%fused_computation.13 | loop fusion | bytes 131072
  1.5 0.0 copy-done
  1.6 0.0 copy-start.1
  1.6 5.1 %collective-permute-start = (f32[2,2,256]{2,1,0:T(2,128)S(1)}, f32[2,2,256]{2,1,0:T(2,128)S(1)}, u32[]{:S(2)}, u32[]{:S(2)}) collective-permute-start(f32[2,2,256]{2,1,0:T(2,128)S(1)} %get-tuple-element.10), channel_id=1, source_target_pairs={{8,16},{16,8},{24,32},{32,24},{40,48},{48,40},{56,64},{64,56},{72,... | collective-permute-start | bytes 12296 | tf_op jit(solution)/shard_map/ppermute | solution.py:39
  6.7 0.1 collective-permute-start.1
  6.8 0.0 copy-done.1
  6.8 0.2 reshape.70
  7.0 0.2 fusion.1
  7.2 0.1 pad_dynamic-slice_fusion.1
  7.3 0.1 slice_bitcast_fusion.1
  7.4 0.1 pad_dynamic-slice_fusion
  7.5 0.1 slice_bitcast_fusion.3
  7.6 0.1 pad_maximum_fusion.3
  7.6 0.1 copy.17
  7.7 0.1 pad_maximum_fusion.2
  7.8 0.1 copy.15
  7.9 0.6 %broadcast_add_fusion.fine_inflow_ref = f32[72,1]{1,0:T(8,128)} fusion(f32[72,1]{1,0:T(8,128)S(1)} %copy.15), kind=kLoop, calls=%fused_computation.9 | loop fusion | flops 72 | bytes 576 | tf_op jit(solution)/shard_map/add | solution.py:69
  8.5 0.6 %broadcast_add_fusion.1.coarse_inflow_ref = f32[40,1]{1,0:T(8,128)} fusion(f32[40,1]{1,0:T(8,128)S(1)} %copy.17), kind=kLoop, calls=%fused_computation.10 | loop fusion | flops 40 | bytes 320 | tf_op jit(solution)/shard_map/add | solution.py:69
  9.1 0.1 collective-permute-done
  9.2 1.2 %collective-permute-done.1 = f32[2,2,256]{2,1,0:T(2,128)S(1)} collective-permute-done((f32[2,2,256]{2,1,0:T(2,128)S(1)}, f32[2,2,256]{2,1,0:T(2,128)S(1)}, u32[]{:S(2)}, u32[]{:S(2)}) %collective-permute-start.1) | collective-permute-done | bytes 4128 | tf_op jit(solution)/shard_map/ppermute | solution.py:39
  10.4 0.1 slice_select_fusion.1
  10.5 2.3 %collective-permute-start.2 = (f32[2,72,2]{2,1,0:T(8,128)S(1)}, f32[2,72,2]{2,1,0:T(8,128)S(1)}, u32[]{:S(2)}, u32[]{:S(2)}) collective-permute-start(f32[2,72,2]{2,1,0:T(8,128)S(1)} %get-tuple-element.8), channel_id=1, source_target_pairs={{128,1},{1,128},{129,2},{2,129},{130,3},{3,130},{131,4},{4,131},{1... | collective-permute-start | bytes 3464 | tf_op jit(solution)/shard_map/ppermute | solution.py:39
  12.8 1.4 %collective-permute-start.3 = (f32[2,72,2]{2,1,0:T(8,128)S(1)}, f32[2,72,2]{2,1,0:T(8,128)S(1)}, u32[]{:S(2)}, u32[]{:S(2)}) collective-permute-start(f32[2,72,2]{2,1,0:T(8,128)S(1)} %get-tuple-element.9), channel_id=1, source_target_pairs={{0,128},{128,0},{1,129},{129,1},{2,130},{130,2},{3,131},{131,3},{4... | collective-permute-start | bytes 3464 | tf_op jit(solution)/shard_map/ppermute | solution.py:39
  14.2 0.7 %add_convert_fusion.flags_ref = s32[4]{0:T(128)} fusion(pred[1]{0:T(512)(128)(4,1)} %bitcast.3, pred[1]{0:T(512)(128)(4,1)} %bitcast.2, pred[1]{0:T(512)(128)(4,1)} %bitcast.1, pred[1]{0:T(512)(128)(4,1)} %bitcast), kind=kLoop, calls=%fused_computation.19 | loop fusion | flops 16 | bytes 20 | tf_op jit(solution)/shard_map/convert_element_type | solution.py:227
  14.9 0.1 pad.19.clone
  14.9 7.5 %collective-permute-done.2 = f32[2,72,2]{2,1,0:T(8,128)S(1)} collective-permute-done((f32[2,72,2]{2,1,0:T(8,128)S(1)}, f32[2,72,2]{2,1,0:T(8,128)S(1)}, u32[]{:S(2)}, u32[]{:S(2)}) %collective-permute-start.2) | collective-permute-done | bytes 1184 | tf_op jit(solution)/shard_map/ppermute | solution.py:39
  22.4 0.0 collective-permute-done.3
  22.4 0.8 %pad_maximum_fusion.noise_ref = f32[2,72,384]{2,1,0:T(8,128)} fusion(f32[2,72,2]{2,1,0:T(8,128)S(1)} %get-tuple-element.7, f32[2,72,2]{2,1,0:T(8,128)S(1)} %get-tuple-element.6, f32[2,2,256]{2,1,0:T(2,128)S(1)} %get-tuple-element.13, f32[2,4,256]{2,1,0:T(4,128)S(1)} %broadcast_in_dim.12, f32[2,2,256]{2,1,0:T(2,128)S(1)} %get-tuple-element.12, ...), kind=kLoop, calls=%fused_computation.3 | loop fusion | flops 331776 | bytes 372480 | tf_op jit(solution)/shard_map/concatenate | solution.py:61
  23.2 3.1 %shard_map.50 = (f32[3,32,128]{2,1,0:T(8,128)}, f32[3,32,128]{2,1,0:T(8,128)}) custom-call(s32[4]{0:T(128)} %add_convert_fusion.flags_ref, f32[2,72,384]{2,1,0:T(8,128)} %pad_maximum_fusion.noise_ref, f32[72,1]{1,0:T(8,128)} %broadcast_add_fusion.fine_inflow_ref, f32[40,1]{1,0:T(8,128)} %broadcast_add_fusion.1.coarse_inflow_ref), custom_call_target="tpu_custom_call" | custom-call | tf_op jit(solution)/shard_map/pallas_call | solution.py:239
  (9 shorter events, 0.1 us)
Async XLA Ops:
  0.6 0.9 %copy-start = (f32[1,64,256]{2,1,0:T(8,128)S(1)}, f32[1,64,256]{2,1,0:T(8,128)}, u32[]{:S(2)}) copy-start(f32[1,64,256]{2,1,0:T(8,128)} %param.4) | copy-start | bytes 196612
  1.6 5.2 %copy-start.1 = (f32[1024]{0:T(1024)S(1)}, f32[1024]{0:T(1024)}, u32[]{:S(2)}) copy-start(f32[1024]{0:T(1024)} %param.5) | copy-start | bytes 12292
  1.6 7.6 %collective-permute-start = (f32[2,2,256]{2,1,0:T(2,128)S(1)}, f32[2,2,256]{2,1,0:T(2,128)S(1)}, u32[]{:S(2)}, u32[]{:S(2)}) collective-permute-start(f32[2,2,256]{2,1,0:T(2,128)S(1)} %get-tuple-element.10), channel_id=1, source_target_pairs={{8,16},{16,8},{24,32},{32,24},{40,48},{48,40},{56,64},{64,56},{72,... | collective-permute-start | bytes 12296 | tf_op jit(solution)/shard_map/ppermute | solution.py:39
  6.7 3.7 %collective-permute-start.1 = (f32[2,2,256]{2,1,0:T(2,128)S(1)}, f32[2,2,256]{2,1,0:T(2,128)S(1)}, u32[]{:S(2)}, u32[]{:S(2)}) collective-permute-start(f32[2,2,256]{2,1,0:T(2,128)S(1)} %get-tuple-element.11), channel_id=1, source_target_pairs={{0,8},{8,0},{16,24},{24,16},{32,40},{40,32},{48,56},{56,48},{64,72... | collective-permute-start | bytes 12296 | tf_op jit(solution)/shard_map/ppermute | solution.py:39
  10.5 11.9 %collective-permute-start.2 = (f32[2,72,2]{2,1,0:T(8,128)S(1)}, f32[2,72,2]{2,1,0:T(8,128)S(1)}, u32[]{:S(2)}, u32[]{:S(2)}) collective-permute-start(f32[2,72,2]{2,1,0:T(8,128)S(1)} %get-tuple-element.8), channel_id=1, source_target_pairs={{128,1},{1,128},{129,2},{2,129},{130,3},{3,130},{131,4},{4,131},{1... | collective-permute-start | bytes 3464 | tf_op jit(solution)/shard_map/ppermute | solution.py:39
  12.8 9.6 %collective-permute-start.3 = (f32[2,72,2]{2,1,0:T(8,128)S(1)}, f32[2,72,2]{2,1,0:T(8,128)S(1)}, u32[]{:S(2)}, u32[]{:S(2)}) collective-permute-start(f32[2,72,2]{2,1,0:T(8,128)S(1)} %get-tuple-element.9), channel_id=1, source_target_pairs={{0,128},{128,0},{1,129},{129,1},{2,130},{130,2},{3,131},{131,3},{4... | collective-permute-start | bytes 3464 | tf_op jit(solution)/shard_map/ppermute | solution.py:39

commit v9 on v8

--- a/solution.py
+++ b/solution.py
@@ -46,20 +46,29 @@
     fields, count_rows, count_cols = noise.shape
     strips = lax.axis_size("col") * lax.axis_size("level")
     strip = lax.axis_index("col") * lax.axis_size("level") + lax.axis_index("level")
+    row_index = lax.axis_index("row")
     rows = lax.axis_size("row")
-    north, south = swapped(
-        noise[:, :HALO], noise[:, -HALO:], lax.axis_index("row"), rows, "row"
-    )
+    north, south = swapped(noise[:, :HALO], noise[:, -HALO:], row_index, rows, "row")
+    west, east = swapped(
+        noise[:, :, :HALO], noise[:, :, -HALO:], strip, strips, ("level", "col"), strip_place
+    )
+    sides = jnp.concatenate([west, east], axis=2)
+    above, below = swapped(sides[:, :HALO], sides[:, -HALO:], row_index, rows, "row")
+    gap_cols = FINE_SHAPE[1] - count_cols - 2 * HALO
+
+    def band(middle, corners):
+        gap = jnp.zeros(middle.shape[:2] + (gap_cols,), noise.dtype)
+        return jnp.concatenate([middle, corners[:, :, HALO:], gap, corners[:, :, :HALO]], axis=2)
+
     gap_rows = FINE_SHAPE[0] - count_rows - 2 * HALO
-    tall = jnp.concatenate(
-        [noise, south, jnp.zeros((fields, gap_rows, count_cols), noise.dtype), north], axis=1
-    )
-    west, east = swapped(
-        tall[:, :, :HALO], tall[:, :, -HALO:], strip, strips, ("level", "col"), strip_place
-    )
-    gap_cols = FINE_SHAPE[1] - count_cols - 2 * HALO
     return jnp.concatenate(
-        [tall, east, jnp.zeros((fields, FINE_SHAPE[0], gap_cols), noise.dtype), west], axis=2
+        [
+            band(noise, sides),
+            band(south, below),
+            jnp.zeros((fields, gap_rows, FINE_SHAPE[1]), noise.dtype),
+            band(north, above),
+        ],
+        axis=1,
     )
 
 

time: 26.5 us -> 32 us (1.21)
  the two profiles are of different devices: /device:TPU:192 before, /device:TPU:56 now
where the time goes in v9:
time: 32 us; the launch traced here: 31.8 us
  starting transfers between devices  18.1 us (57%)
  waiting for transfers between devices  4.74 us (15%)
  other arithmetic  3.2 us (10%)
  Pallas kernels  3.12 us (10%)
  local copies, waits for them, and re-layouts  1.83 us (6%)
  between operations  0.76 us (2%)
    ppermute x6, starting transfers between devices, swapped(): got.append(lax.ppermute(block, axis, swap_pairs(count, parity, place)))  18.1 us
    ppermute x6, waiting for transfers between devices, swapped(): got.append(lax.ppermute(block, axis, swap_pairs(count, parity, place)))  4.74 us
    pallas_call x1, Pallas kernels, body(): pl.pallas_call(level_kernel, out_shape=(out, out), in_specs=[pl.BlockSpec...  3.12 us
    add x2, other arithmetic, wrapped_rows(): return (0.5 + jnp.roll(window, -lead)).reshape(count, 1)  1.22 us
    unnamed x5, local copies, waits for them, and re-layouts  0.88 us
    concatenate x1, other arithmetic, with_halo(): jnp.concatenate([band(noise, sides), band(south, below), jnp.zeros((field...  0.81 us
  transfers between devices with their start and end apart: 6, of which 1 were waited for; matrix products, arithmetic and copies ran while one was open for 10% of the time, Pallas kernels for 0%

profile of v9, /device:TPU:56, one launch (start us, length us, event | category | flops | bytes accessed | tf_op | source)
XLA Modules:
  0.0 31.8 jit_solution(15191751107035704128)
XLA Ops:
  0.7 0.9 %constant_dynamic-update-slice_fusion.1 = f32[2,64,256]{2,1,0:T(8,128)S(1)} fusion(f32[1,64,256]{2,1,0:T(8,128)} %param.3), kind=kLoop, calls=%fused_computation.12 | loop fusion | bytes 131072
  1.5 0.1 slice_select_fusion
  1.6 2.1 %collective-permute-start = (f32[2,64,2]{2,1,0:T(8,128)S(1)}, f32[2,64,2]{2,1,0:T(8,128)S(1)}, u32[]{:S(2)}, u32[]{:S(2)}) collective-permute-start(f32[2,64,2]{2,1,0:T(8,128)S(1)} %get-tuple-element.14), channel_id=1, source_target_pairs={{128,1},{1,128},{129,2},{2,129},{130,3},{3,130},{131,4},{4,131},{1... | collective-permute-start | bytes 3080 | tf_op jit(solution)/shard_map/ppermute | solution.py:39
  3.7 6.0 %collective-permute-start.1 = (f32[2,64,2]{2,1,0:T(8,128)S(1)}, f32[2,64,2]{2,1,0:T(8,128)S(1)}, u32[]{:S(2)}, u32[]{:S(2)}) collective-permute-start(f32[2,64,2]{2,1,0:T(8,128)S(1)} %get-tuple-element.13), channel_id=1, source_target_pairs={{0,128},{128,0},{1,129},{129,1},{2,130},{130,2},{3,131},{131,3},{4... | collective-permute-start | bytes 3080 | tf_op jit(solution)/shard_map/ppermute | solution.py:39
  9.7 5.1 %collective-permute-start.2 = (f32[2,2,256]{2,1,0:T(2,128)S(1)}, f32[2,2,256]{2,1,0:T(2,128)S(1)}, u32[]{:S(2)}, u32[]{:S(2)}) collective-permute-start(f32[2,2,256]{2,1,0:T(2,128)S(1)} %get-tuple-element.9), channel_id=1, source_target_pairs={{8,16},{16,8},{24,32},{32,24},{40,48},{48,40},{56,64},{64,56},{72,... | collective-permute-start | bytes 12296 | tf_op jit(solution)/shard_map/ppermute | solution.py:39
  14.8 0.1 collective-permute-start.3
  14.9 0.2 reshape.70
  15.2 0.2 fusion.1
  15.4 0.1 pad_dynamic-slice_fusion.1
  15.5 0.1 slice_bitcast_fusion.1
  15.6 0.1 pad_dynamic-slice_fusion
  15.6 0.1 slice_bitcast_fusion.3
  15.7 0.1 pad_maximum_fusion.3
  15.8 0.1 copy.23
  15.9 0.6 %broadcast_add_fusion.1.coarse_inflow_ref = f32[40,1]{1,0:T(8,128)} fusion(f32[40,1]{1,0:T(8,128)S(1)} %copy.23), kind=kLoop, calls=%fused_computation.9 | loop fusion | flops 40 | bytes 320 | tf_op jit(solution)/shard_map/add | solution.py:78
  16.5 0.1 pad_maximum_fusion.2
  16.6 0.1 copy.21
  16.7 0.6 %broadcast_add_fusion.fine_inflow_ref = f32[72,1]{1,0:T(8,128)} fusion(f32[72,1]{1,0:T(8,128)S(1)} %copy.21), kind=kLoop, calls=%fused_computation.8 | loop fusion | flops 72 | bytes 576 | tf_op jit(solution)/shard_map/add | solution.py:78
  17.3 0.6 %add_convert_fusion.flags_ref = s32[4]{0:T(128)} fusion(pred[1]{0:T(512)(128)(4,1)} %bitcast.3, pred[1]{0:T(512)(128)(4,1)} %bitcast.2, pred[1]{0:T(512)(128)(4,1)} %bitcast.1, pred[1]{0:T(512)(128)(4,1)} %bitcast), kind=kLoop, calls=%fused_computation.20 | loop fusion | flops 16 | bytes 20 | tf_op jit(solution)/shard_map/convert_element_type | solution.py:236
  17.9 0.1 pad.16.clone
  17.9 0.1 pad.22.clone
  18.0 0.0 collective-permute-done
  18.0 0.0 collective-permute-done.1
  18.0 0.1 broadcast_select_fusion.9
  18.1 2.0 %collective-permute-start.5 = (f32[2,2,4]{2,1,0:T(2,128)S(1)}, f32[2,2,4]{2,1,0:T(2,128)S(1)}, u32[]{:S(2)}, u32[]{:S(2)}) collective-permute-start(f32[2,2,4]{2,1,0:T(2,128)S(1)} %broadcast_select_fusion.6), channel_id=1, source_target_pairs={{0,8},{8,0},{16,24},{24,16},{32,40},{40,32},{48,56},{56,48},{64,72... | collective-permute-start | bytes 200 | tf_op jit(solution)/shard_map/ppermute | solution.py:39
  20.2 2.8 %collective-permute-start.4 = (f32[2,2,4]{2,1,0:T(2,128)S(1)}, f32[2,2,4]{2,1,0:T(2,128)S(1)}, u32[]{:S(2)}, u32[]{:S(2)}) collective-permute-start(f32[2,2,4]{2,1,0:T(2,128)S(1)} %get-tuple-element.6), channel_id=1, source_target_pairs={{8,16},{16,8},{24,32},{32,24},{40,48},{48,40},{56,64},{64,56},{72,... | collective-permute-start | bytes 200 | tf_op jit(solution)/shard_map/ppermute | solution.py:39
  23.0 0.0 collective-permute-done.5
  23.0 4.7 %collective-permute-done.4 = f32[2,2,4]{2,1,0:T(2,128)S(1)} collective-permute-done((f32[2,2,4]{2,1,0:T(2,128)S(1)}, f32[2,2,4]{2,1,0:T(2,128)S(1)}, u32[]{:S(2)}, u32[]{:S(2)}) %collective-permute-start.4) | collective-permute-done | bytes 96 | tf_op jit(solution)/shard_map/ppermute | solution.py:39
  27.8 0.1 fusion.2
  27.8 0.0 collective-permute-done.2
  27.9 0.8 %maximum_maximum_fusion.noise_ref = f32[2,72,384]{2,1,0:T(8,128)} fusion(f32[2,2,2]{2,1,0:T(2,128)S(1)} %get-tuple-element.23, f32[2,2,124]{2,1,0:T(2,128)S(1)} %broadcast.25, f32[2,2,2]{2,1,0:T(2,128)S(1)} %get-tuple-element.24, f32[2,2,256]{2,1,0:T(2,128)S(1)} %get-tuple-element.16, f32[2,2,2]{2,1,0:T(2,128)S(1)} %get-tuple-element.20, ...), kind=kLoop, calls=%fused_computation.3 | loop fusion | flops 663552 | bytes 475488 | tf_op jit(solution)/shard_map/concatenate | solution.py:64
  28.7 3.1 %shard_map.50 = (f32[3,32,128]{2,1,0:T(8,128)}, f32[3,32,128]{2,1,0:T(8,128)}) custom-call(s32[4]{0:T(128)} %add_convert_fusion.flags_ref, f32[2,72,384]{2,1,0:T(8,128)} %maximum_maximum_fusion.noise_ref, f32[72,1]{1,0:T(8,128)} %broadcast_add_fusion.fine_inflow_ref, f32[40,1]{1,0:T(8,128)} %broadcast_add_fusion.1.coarse_inflow_ref), custom_call_target="tpu_custom_call" | custom-call | tf_op jit(solution)/shard_map/pallas_call | solution.py:248
  (16 shorter events, 0.1 us)
Async XLA Ops:
  0.6 0.9 %copy-start = (f32[1,64,256]{2,1,0:T(8,128)S(1)}, f32[1,64,256]{2,1,0:T(8,128)}, u32[]{:S(2)}) copy-start(f32[1,64,256]{2,1,0:T(8,128)} %param.4) | copy-start | bytes 196612
  1.6 16.4 %collective-permute-start = (f32[2,64,2]{2,1,0:T(8,128)S(1)}, f32[2,64,2]{2,1,0:T(8,128)S(1)}, u32[]{:S(2)}, u32[]{:S(2)}) collective-permute-start(f32[2,64,2]{2,1,0:T(8,128)S(1)} %get-tuple-element.14), channel_id=1, source_target_pairs={{128,1},{1,128},{129,2},{2,129},{130,3},{3,130},{131,4},{4,131},{1... | collective-permute-start | bytes 3080 | tf_op jit(solution)/shard_map/ppermute | solution.py:39
  3.7 14.3 %collective-permute-start.1 = (f32[2,64,2]{2,1,0:T(8,128)S(1)}, f32[2,64,2]{2,1,0:T(8,128)S(1)}, u32[]{:S(2)}, u32[]{:S(2)}) collective-permute-start(f32[2,64,2]{2,1,0:T(8,128)S(1)} %get-tuple-element.13), channel_id=1, source_target_pairs={{0,128},{128,0},{1,129},{129,1},{2,130},{130,2},{3,131},{131,3},{4... | collective-permute-start | bytes 3080 | tf_op jit(solution)/shard_map/ppermute | solution.py:39
  9.7 5.2 %copy-start.1 = (f32[1024]{0:T(1024)S(1)}, f32[1024]{0:T(1024)}, u32[]{:S(2)}) copy-start(f32[1024]{0:T(1024)} %param.5) | copy-start | bytes 12292
  9.7 18.1 %collective-permute-start.2 = (f32[2,2,256]{2,1,0:T(2,128)S(1)}, f32[2,2,256]{2,1,0:T(2,128)S(1)}, u32[]{:S(2)}, u32[]{:S(2)}) collective-permute-start(f32[2,2,256]{2,1,0:T(2,128)S(1)} %get-tuple-element.9), channel_id=1, source_target_pairs={{8,16},{16,8},{24,32},{32,24},{40,48},{48,40},{56,64},{64,56},{72,... | collective-permute-start | bytes 12296 | tf_op jit(solution)/shard_map/ppermute | solution.py:39
  14.8 13.0 %collective-permute-start.3 = (f32[2,2,256]{2,1,0:T(2,128)S(1)}, f32[2,2,256]{2,1,0:T(2,128)S(1)}, u32[]{:S(2)}, u32[]{:S(2)}) collective-permute-start(f32[2,2,256]{2,1,0:T(2,128)S(1)} %get-tuple-element.10), channel_id=1, source_target_pairs={{0,8},{8,0},{16,24},{24,16},{32,40},{40,32},{48,56},{56,48},{64,72... | collective-permute-start | bytes 12296 | tf_op jit(solution)/shard_map/ppermute | solution.py:39
  18.1 4.9 %collective-permute-start.5 = (f32[2,2,4]{2,1,0:T(2,128)S(1)}, f32[2,2,4]{2,1,0:T(2,128)S(1)}, u32[]{:S(2)}, u32[]{:S(2)}) collective-permute-start(f32[2,2,4]{2,1,0:T(2,128)S(1)} %broadcast_select_fusion.6), channel_id=1, source_target_pairs={{0,8},{8,0},{16,24},{24,16},{32,40},{40,32},{48,56},{56,48},{64,72... | collective-permute-start | bytes 200 | tf_op jit(solution)/shard_map/ppermute | solution.py:39
  20.2 7.6 %collective-permute-start.4 = (f32[2,2,4]{2,1,0:T(2,128)S(1)}, f32[2,2,4]{2,1,0:T(2,128)S(1)}, u32[]{:S(2)}, u32[]{:S(2)}) collective-permute-start(f32[2,2,4]{2,1,0:T(2,128)S(1)} %get-tuple-element.6), channel_id=1, source_target_pairs={{8,16},{16,8},{24,32},{32,24},{40,48},{48,40},{56,64},{64,56},{72,... | collective-permute-start | bytes 200 | tf_op jit(solution)/shard_map/ppermute | solution.py:39

commit v10 on v8

--- a/solution.py
+++ b/solution.py
@@ -42,24 +42,49 @@
     return before, after
 
 
+def swap_once(first, last, index, count, axis, parity, place=lambda i: i):
+    gets_after = (index % 2 == 1) if parity else (index % 2 == 0)
+    block = jnp.where(gets_after, last, first)
+    return gets_after, lax.ppermute(block, axis, swap_pairs(count, parity, place))
+
+
 def with_halo(noise):
     fields, count_rows, count_cols = noise.shape
     strips = lax.axis_size("col") * lax.axis_size("level")
     strip = lax.axis_index("col") * lax.axis_size("level") + lax.axis_index("level")
-    rows = lax.axis_size("row")
+    across = ("level", "col")
+    gap_cols = FINE_SHAPE[1] - count_cols - 2 * HALO
+
+    def sides(width, after, before):
+        gap = jnp.zeros((fields, width, gap_cols), noise.dtype)
+        return [after, gap, before]
+
+    gets_after, got = swap_once(
+        noise[:, :, :HALO], noise[:, :, -HALO:], strip, strips, across, 1, strip_place
+    )
+    none = jnp.zeros_like(got)
+    wide = jnp.concatenate(
+        [noise] + sides(count_rows, jnp.where(gets_after, got, none),
+                        jnp.where(gets_after, none, got)),
+        axis=2,
+    )
     north, south = swapped(
-        noise[:, :HALO], noise[:, -HALO:], lax.axis_index("row"), rows, "row"
+        wide[:, :HALO], wide[:, -HALO:], lax.axis_index("row"), lax.axis_size("row"), "row"
     )
     gap_rows = FINE_SHAPE[0] - count_rows - 2 * HALO
     tall = jnp.concatenate(
-        [noise, south, jnp.zeros((fields, gap_rows, count_cols), noise.dtype), north], axis=1
-    )
-    west, east = swapped(
-        tall[:, :, :HALO], tall[:, :, -HALO:], strip, strips, ("level", "col"), strip_place
-    )
-    gap_cols = FINE_SHAPE[1] - count_cols - 2 * HALO
+        [wide, south, jnp.zeros((fields, gap_rows, FINE_SHAPE[1]), noise.dtype), north], axis=1
+    )
+    gets_after, got = swap_once(
+        tall[:, :, :HALO], tall[:, :, count_cols - HALO: count_cols], strip, strips, across, 0,
+        strip_place,
+    )
+    east = tall[:, :, count_cols: count_cols + HALO]
+    west = tall[:, :, FINE_SHAPE[1] - HALO:]
     return jnp.concatenate(
-        [tall, east, jnp.zeros((fields, FINE_SHAPE[0], gap_cols), noise.dtype), west], axis=2
+        [tall[:, :, :count_cols]]
+        + sides(FINE_SHAPE[0], jnp.where(gets_after, got, east), jnp.where(gets_after, west, got)),
+        axis=2,
     )
 
 

time: 26.5 us -> 28.7 us (1.083); the launches traced: 26.3 us -> 28.1 us
  starting transfers between devices: 8.89 us -> 10.4 us
  waiting for transfers between devices: 8.72 us -> 7.84 us
  local copies, waits for them, and re-layouts: 1.68 us -> 2.45 us
  other arithmetic: 3.17 us -> 3.5 us
    ppermute x4 -> x2, waiting for transfers between devices: 8.72 us -> 2.49 us  [swapped(): got.append(lax.ppermute(block, axis, swap_pairs(count, parity, place)))]
    ppermute x0 -> x2, waiting for transfers between devices: none -> 5.35 us  [swap_once(): lax.ppermute(block, axis, swap_pairs(count, parity, place))]
    ppermute x0 -> x2, starting transfers between devices: none -> 4.43 us  [swap_once(): lax.ppermute(block, axis, swap_pairs(count, parity, place))]
    ppermute x4 -> x2, starting transfers between devices: 8.89 us -> 6.01 us  [swapped(): got.append(lax.ppermute(block, axis, swap_pairs(count, parity, place)))]
    unnamed x5, local copies, waits for them, and re-layouts: 0.89 us -> 1.56 us
  transfers between devices with their start and end apart: 4 -> 4, of which waited for: 3 -> 3; matrix products, arithmetic and copies ran while one was open for 12% -> 11% of each run, Pallas kernels for 0% -> 0%
where the time goes in v10:
time: 28.7 us; the launch traced here: 28.1 us
  starting transfers between devices  10.4 us (36%)
  waiting for transfers between devices  7.84 us (27%)
  other arithmetic  3.5 us (12%)
  Pallas kernels  3.12 us (11%)
  local copies, waits for them, and re-layouts  2.45 us (9%)
  between operations  0.76 us (3%)
    ppermute x2, starting transfers between devices, swapped(): got.append(lax.ppermute(block, axis, swap_pairs(count, parity, place)))  6.01 us
    ppermute x2, waiting for transfers between devices, swap_once(): lax.ppermute(block, axis, swap_pairs(count, parity, place))  5.35 us
    ppermute x2, starting transfers between devices, swap_once(): lax.ppermute(block, axis, swap_pairs(count, parity, place))  4.43 us
    pallas_call x1, Pallas kernels, body(): pl.pallas_call(level_kernel, out_shape=(out, out), in_specs=[pl.BlockSpec...  3.12 us
    ppermute x2, waiting for transfers between devices, swapped(): got.append(lax.ppermute(block, axis, swap_pairs(count, parity, place)))  2.49 us
    unnamed x5, local copies, waits for them, and re-layouts  1.56 us
    add x2, other arithmetic, wrapped_rows(): return (0.5 + jnp.roll(window, -lead)).reshape(count, 1)  1.22 us
    concatenate x1, other arithmetic, with_halo(): jnp.concatenate([tall[:, :, :count_cols]] + sides(FINE_SHAPE[0], jnp.wher...  0.78 us
  transfers between devices with their start and end apart: 4, of which 3 were waited for; matrix products, arithmetic and copies ran while one was open for 11% of the time, Pallas kernels for 0%

profile of v10, /device:TPU:192, one launch (start us, length us, event | category | flops | bytes accessed | tf_op | source)
XLA Modules:
  0.0 28.1 jit_solution(12858921140091699591)
XLA Ops:
  0.7 0.9 %constant_dynamic-update-slice_fusion.1 = f32[2,64,256]{2,1,0:T(8,128)S(1)} fusion(f32[1,64,256]{2,1,0:T(8,128)} %param.3), kind=kLoop, calls=%fused_computation.19 | loop fusion | bytes 131072
  1.5 0.1 slice_select_fusion.3
  1.6 4.3 %collective-permute-start = (f32[2,64,2]{2,1,0:T(8,128)S(1)}, f32[2,64,2]{2,1,0:T(8,128)S(1)}, u32[]{:S(2)}, u32[]{:S(2)}) collective-permute-start(f32[2,64,2]{2,1,0:T(8,128)S(1)} %slice_select_fusion.3), channel_id=1, source_target_pairs={{128,1},{1,128},{129,2},{2,129},{130,3},{3,130},{131,4},{4,131},{1... | collective-permute-start | bytes 3080 | tf_op jit(solution)/shard_map/ppermute | solution.py:48
  6.0 0.0 copy-start.1
  6.0 0.7 %copy-done.1 = f32[1024]{0:T(1024)S(1)} copy-done((f32[1024]{0:T(1024)S(1)}, f32[1024]{0:T(1024)}, u32[]{:S(2)}) %copy-start.1) | copy-done | bytes 4120
  6.7 0.2 reshape.70
  6.9 0.2 fusion.1
  7.1 0.1 pad_dynamic-slice_fusion.1
  7.2 0.1 slice_bitcast_fusion.1
  7.3 0.1 pad_dynamic-slice_fusion
  7.4 0.1 slice_bitcast_fusion.3
  7.4 0.1 pad_maximum_fusion.6
  7.5 0.1 copy.15
  7.6 0.6 %broadcast_add_fusion.fine_inflow_ref = f32[72,1]{1,0:T(8,128)} fusion(f32[72,1]{1,0:T(8,128)S(1)} %copy.15), kind=kLoop, calls=%fused_computation.11 | loop fusion | flops 72 | bytes 576 | tf_op jit(solution)/shard_map/add | solution.py:94
  8.2 0.1 pad_maximum_fusion.7
  8.3 0.1 copy.17
  8.4 4.8 %collective-permute-done = f32[2,64,2]{2,1,0:T(8,128)S(1)} collective-permute-done((f32[2,64,2]{2,1,0:T(8,128)S(1)}, f32[2,64,2]{2,1,0:T(8,128)S(1)}, u32[]{:S(2)}, u32[]{:S(2)}) %collective-permute-start) | collective-permute-done | bytes 1056 | tf_op jit(solution)/shard_map/ppermute | solution.py:48
  13.3 0.1 broadcast_select_fusion.5
  13.4 1.6 %collective-permute-start.2 = (f32[2,2,384]{2,1,0:T(2,128)S(1)}, f32[2,2,384]{2,1,0:T(2,128)S(1)}, u32[]{:S(2)}, u32[]{:S(2)}) collective-permute-start(f32[2,2,384]{2,1,0:T(2,128)S(1)} %broadcast_select_fusion.2), channel_id=1, source_target_pairs={{0,8},{8,0},{16,24},{24,16},{32,40},{40,32},{48,56},{56,48},{64,72... | collective-permute-start | bytes 18440 | tf_op jit(solution)/shard_map/ppermute | solution.py:39
  14.9 4.4 %collective-permute-start.1 = (f32[2,2,384]{2,1,0:T(2,128)S(1)}, f32[2,2,384]{2,1,0:T(2,128)S(1)}, u32[]{:S(2)}, u32[]{:S(2)}) collective-permute-start(f32[2,2,384]{2,1,0:T(2,128)S(1)} %get-tuple-element.6), channel_id=1, source_target_pairs={{8,16},{16,8},{24,32},{32,24},{40,48},{48,40},{56,64},{64,56},{72,... | collective-permute-start | bytes 18440 | tf_op jit(solution)/shard_map/ppermute | solution.py:39
  19.4 0.6 %broadcast_add_fusion.1.coarse_inflow_ref = f32[40,1]{1,0:T(8,128)} fusion(f32[40,1]{1,0:T(8,128)S(1)} %copy.17), kind=kLoop, calls=%fused_computation.12 | loop fusion | flops 40 | bytes 320 | tf_op jit(solution)/shard_map/add | solution.py:94
  20.0 0.1 pad.23.clone
  20.1 2.5 %collective-permute-done.1 = f32[2,2,384]{2,1,0:T(2,128)S(1)} collective-permute-done((f32[2,2,384]{2,1,0:T(2,128)S(1)}, f32[2,2,384]{2,1,0:T(2,128)S(1)}, u32[]{:S(2)}, u32[]{:S(2)}) %collective-permute-start.1) | collective-permute-done | bytes 6176 | tf_op jit(solution)/shard_map/ppermute | solution.py:39
  22.6 0.1 pad_maximum_fusion
  22.7 0.1 slice_select_fusion.2
  22.8 0.1 collective-permute-start.3
  22.9 0.7 %add_convert_fusion.flags_ref = s32[4]{0:T(128)} fusion(pred[1]{0:T(512)(128)(4,1)} %bitcast.3, pred[1]{0:T(512)(128)(4,1)} %bitcast.2, pred[1]{0:T(512)(128)(4,1)} %bitcast.1, pred[1]{0:T(512)(128)(4,1)} %bitcast), kind=kLoop, calls=%fused_computation.25 | loop fusion | flops 16 | bytes 20 | tf_op jit(solution)/shard_map/convert_element_type | solution.py:252
  23.5 0.1 pad.16.clone
  23.6 0.5 %collective-permute-done.3 = f32[2,72,2]{2,1,0:T(8,128)S(1)} collective-permute-done((f32[2,72,2]{2,1,0:T(8,128)S(1)}, f32[2,72,2]{2,1,0:T(8,128)S(1)}, u32[]{:S(2)}, u32[]{:S(2)}) %collective-permute-start.3) | collective-permute-done | bytes 1184 | tf_op jit(solution)/shard_map/ppermute | solution.py:48
  24.1 0.1 slice_select_fusion.1
  24.2 0.8 %pad_maximum_fusion.1.noise_ref = f32[2,72,384]{2,1,0:T(8,128)} fusion(f32[2,72,2]{2,1,0:T(8,128)S(1)} %get-tuple-element.10, f32[2,72,2]{2,1,0:T(8,128)S(1)} %get-tuple-element.9, f32[2,72,256]{2,1,0:T(8,128)S(1)} %slice.66, f32[384]{0:T(512)S(1)} %pad.16.clone), kind=kLoop, calls=%fused_computation.4 | loop fusion | flops 165888 | bytes 372480 | tf_op jit(solution)/shard_map/concatenate | solution.py:84
  25.0 3.1 %shard_map.50 = (f32[3,32,128]{2,1,0:T(8,128)}, f32[3,32,128]{2,1,0:T(8,128)}) custom-call(s32[4]{0:T(128)} %add_convert_fusion.flags_ref, f32[2,72,384]{2,1,0:T(8,128)} %pad_maximum_fusion.1.noise_ref, f32[72,1]{1,0:T(8,128)} %broadcast_add_fusion.fine_inflow_ref, f32[40,1]{1,0:T(8,128)} %broadcast_add_fusion.1.coarse_inflow_ref), custom_call_target="tpu_custom_call" | custom-call | tf_op jit(solution)/shard_map/pallas_call | solution.py:264
  (13 shorter events, 0.1 us)
Async XLA Ops:
  0.6 0.9 %copy-start = (f32[1,64,256]{2,1,0:T(8,128)S(1)}, f32[1,64,256]{2,1,0:T(8,128)}, u32[]{:S(2)}) copy-start(f32[1,64,256]{2,1,0:T(8,128)} %param.4) | copy-start | bytes 196612
  1.6 11.6 %collective-permute-start = (f32[2,64,2]{2,1,0:T(8,128)S(1)}, f32[2,64,2]{2,1,0:T(8,128)S(1)}, u32[]{:S(2)}, u32[]{:S(2)}) collective-permute-start(f32[2,64,2]{2,1,0:T(8,128)S(1)} %slice_select_fusion.3), channel_id=1, source_target_pairs={{128,1},{1,128},{129,2},{2,129},{130,3},{3,130},{131,4},{4,131},{1... | collective-permute-start | bytes 3080 | tf_op jit(solution)/shard_map/ppermute | solution.py:48
  6.0 0.7 %copy-start.1 = (f32[1024]{0:T(1024)S(1)}, f32[1024]{0:T(1024)}, u32[]{:S(2)}) copy-start(f32[1024]{0:T(1024)} %param.5) | copy-start | bytes 12292
  13.4 6.7 %collective-permute-start.2 = (f32[2,2,384]{2,1,0:T(2,128)S(1)}, f32[2,2,384]{2,1,0:T(2,128)S(1)}, u32[]{:S(2)}, u32[]{:S(2)}) collective-permute-start(f32[2,2,384]{2,1,0:T(2,128)S(1)} %broadcast_select_fusion.2), channel_id=1, source_target_pairs={{0,8},{8,0},{16,24},{24,16},{32,40},{40,32},{48,56},{56,48},{64,72... | collective-permute-start | bytes 18440 | tf_op jit(solution)/shard_map/ppermute | solution.py:39
  14.9 7.6 %collective-permute-start.1 = (f32[2,2,384]{2,1,0:T(2,128)S(1)}, f32[2,2,384]{2,1,0:T(2,128)S(1)}, u32[]{:S(2)}, u32[]{:S(2)}) collective-permute-start(f32[2,2,384]{2,1,0:T(2,128)S(1)} %get-tuple-element.6), channel_id=1, source_target_pairs={{8,16},{16,8},{24,32},{32,24},{40,48},{48,40},{56,64},{64,56},{72,... | collective-permute-start | bytes 18440 | tf_op jit(solution)/shard_map/ppermute | solution.py:39
  22.8 1.4 %collective-permute-start.3 = (f32[2,72,2]{2,1,0:T(8,128)S(1)}, f32[2,72,2]{2,1,0:T(8,128)S(1)}, u32[]{:S(2)}, u32[]{:S(2)}) collective-permute-start(f32[2,72,2]{2,1,0:T(8,128)S(1)} %slice_select_fusion.2), channel_id=1, source_target_pairs={{0,128},{128,0},{1,129},{129,1},{2,130},{130,2},{3,131},{131,3},{4... | collective-permute-start | bytes 3464 | tf_op jit(solution)/shard_map/ppermute | solution.py:48

commit v11 on v8

--- a/solution.py
+++ b/solution.py
@@ -116,10 +116,11 @@
 
 def advance(state, friction_coef, step):
     depth, along_cols, along_rows = state
-    velocity = along_cols / depth
+    inverse = 1.0 / depth
+    velocity = along_cols * inverse
     flux = (along_cols, along_cols * velocity + 0.5 * depth * depth, along_rows * velocity)
     face_x = face_flux(state, flux, jnp.abs(velocity) + jnp.sqrt(depth), 1)
-    velocity = along_rows / depth
+    velocity = along_rows * inverse
     flux = (along_rows, along_cols * velocity, along_rows * velocity + 0.5 * depth * depth)
     face_y = face_flux(state, flux, jnp.abs(velocity) + jnp.sqrt(depth), 0)
     moved = [
@@ -127,8 +128,9 @@
         for u, fx, fy in zip(state, face_x, face_y)
     ]
     depth = moved[0]
-    speed = jnp.sqrt(moved[1] * moved[1] + moved[2] * moved[2]) / depth
-    damping = 1.0 / (1.0 + step * friction_coef * speed / depth)
+    inverse = 1.0 / depth
+    speed = jnp.sqrt(moved[1] * moved[1] + moved[2] * moved[2]) * inverse
+    damping = 1.0 / (1.0 + step * friction_coef * speed * inverse)
     return (depth, moved[1] * damping, moved[2] * damping)
 
 
@@ -142,7 +144,7 @@
 
 def advance_at_rest(state, friction_coef, step):
     depth, along_cols, _ = state
-    velocity = along_cols / depth
+    velocity = along_cols * (1.0 / depth)
     root = jnp.sqrt(depth)
     flux = (along_cols, along_cols * velocity + 0.5 * depth * depth)
     face_x = face_flux((depth, along_cols), flux, jnp.abs(velocity) + root, 1)
@@ -156,8 +158,9 @@
     ]
     moved.append(0.0 - step_ratio * (pressure_face - prev_of(pressure_face, 0)))
     depth = moved[0]
-    speed = jnp.sqrt(moved[1] * moved[1] + moved[2] * moved[2]) / depth
-    damping = 1.0 / (1.0 + step * friction_coef * speed / depth)
+    inverse = 1.0 / depth
+    speed = jnp.sqrt(moved[1] * moved[1] + moved[2] * moved[2]) * inverse
+    damping = 1.0 / (1.0 + step * friction_coef * speed * inverse)
     return (depth, moved[1] * damping, moved[2] * damping)
 
 

time: 26.5 us -> 26.5 us (level)
  no operation moved by 1% of the time
where the time goes in v11:
time: 26.5 us; the launch traced here: 26.3 us
  starting transfers between devices  8.89 us (34%)
  waiting for transfers between devices  8.72 us (33%)
  other arithmetic  3.17 us (12%)
  Pallas kernels  3.12 us (12%)
  local copies, waits for them, and re-layouts  1.68 us (6%)
  between operations  0.75 us (3%)
    ppermute x4, starting transfers between devices, swapped(): got.append(lax.ppermute(block, axis, swap_pairs(count, parity, place)))  8.89 us
    ppermute x4, waiting for transfers between devices, swapped(): got.append(lax.ppermute(block, axis, swap_pairs(count, parity, place)))  8.72 us
    pallas_call x1, Pallas kernels, body(): pl.pallas_call(level_kernel, out_shape=(out, out), in_specs=[pl.BlockSpec...  3.12 us
    add x2, other arithmetic, wrapped_rows(): return (0.5 + jnp.roll(window, -lead)).reshape(count, 1)  1.22 us
    unnamed x5, local copies, waits for them, and re-layouts  0.89 us
    concatenate x1, other arithmetic, with_halo(): jnp.concatenate([tall, east, jnp.zeros((fields, FINE_SHAPE[0], gap_cols),...  0.78 us
    convert_element_type x1, other arithmetic, body(): flags = jnp.stack([row_index == 0, row_index == lax.axis_size('row') - 1,...  0.65 us
  transfers between devices with their start and end apart: 4, of which 3 were waited for; matrix products, arithmetic and copies ran while one was open for 12% of the time, Pallas kernels for 0%

profile of v11, /device:TPU:192, one launch (start us, length us, event | category | flops | bytes accessed | tf_op | source)
XLA Modules:
  0.0 26.3 jit_solution(14946146713196406984)
XLA Ops:
  0.6 0.0 copy-start
  0.7 0.9 %constant_dynamic-update-slice_fusion.1 = f32[2,64,256]{2,1,0:T(8,128)S(1)} fusion(f32[1,64,256]{2,1,0:T(8,128)} %param.3), kind=kLoop, calls=%fused_computation.13 | loop fusion | bytes 131072
  1.5 0.0 copy-done
  1.6 0.0 copy-start.1
  1.6 5.1 %collective-permute-start = (f32[2,2,256]{2,1,0:T(2,128)S(1)}, f32[2,2,256]{2,1,0:T(2,128)S(1)}, u32[]{:S(2)}, u32[]{:S(2)}) collective-permute-start(f32[2,2,256]{2,1,0:T(2,128)S(1)} %get-tuple-element.10), channel_id=1, source_target_pairs={{8,16},{16,8},{24,32},{32,24},{40,48},{48,40},{56,64},{64,56},{72,... | collective-permute-start | bytes 12296 | tf_op jit(solution)/shard_map/ppermute | solution.py:39
  6.7 0.1 collective-permute-start.1
  6.8 0.0 copy-done.1
  6.8 0.2 reshape.70
  7.0 0.2 fusion.1
  7.2 0.1 pad_dynamic-slice_fusion.1
  7.3 0.1 slice_bitcast_fusion.1
  7.4 0.1 pad_dynamic-slice_fusion
  7.5 0.1 slice_bitcast_fusion.3
  7.6 0.1 pad_maximum_fusion.3
  7.6 0.1 copy.17
  7.7 0.1 pad_maximum_fusion.2
  7.8 0.1 copy.15
  7.9 0.6 %broadcast_add_fusion.fine_inflow_ref = f32[72,1]{1,0:T(8,128)} fusion(f32[72,1]{1,0:T(8,128)S(1)} %copy.15), kind=kLoop, calls=%fused_computation.9 | loop fusion | flops 72 | bytes 576 | tf_op jit(solution)/shard_map/add | solution.py:69
  8.5 0.6 %broadcast_add_fusion.1.coarse_inflow_ref = f32[40,1]{1,0:T(8,128)} fusion(f32[40,1]{1,0:T(8,128)S(1)} %copy.17), kind=kLoop, calls=%fused_computation.10 | loop fusion | flops 40 | bytes 320 | tf_op jit(solution)/shard_map/add | solution.py:69
  9.1 0.1 collective-permute-done
  9.2 1.2 %collective-permute-done.1 = f32[2,2,256]{2,1,0:T(2,128)S(1)} collective-permute-done((f32[2,2,256]{2,1,0:T(2,128)S(1)}, f32[2,2,256]{2,1,0:T(2,128)S(1)}, u32[]{:S(2)}, u32[]{:S(2)}) %collective-permute-start.1) | collective-permute-done | bytes 4128 | tf_op jit(solution)/shard_map/ppermute | solution.py:39
  10.4 0.1 slice_select_fusion.1
  10.5 2.3 %collective-permute-start.2 = (f32[2,72,2]{2,1,0:T(8,128)S(1)}, f32[2,72,2]{2,1,0:T(8,128)S(1)}, u32[]{:S(2)}, u32[]{:S(2)}) collective-permute-start(f32[2,72,2]{2,1,0:T(8,128)S(1)} %get-tuple-element.8), channel_id=1, source_target_pairs={{128,1},{1,128},{129,2},{2,129},{130,3},{3,130},{131,4},{4,131},{1... | collective-permute-start | bytes 3464 | tf_op jit(solution)/shard_map/ppermute | solution.py:39
  12.8 1.4 %collective-permute-start.3 = (f32[2,72,2]{2,1,0:T(8,128)S(1)}, f32[2,72,2]{2,1,0:T(8,128)S(1)}, u32[]{:S(2)}, u32[]{:S(2)}) collective-permute-start(f32[2,72,2]{2,1,0:T(8,128)S(1)} %get-tuple-element.9), channel_id=1, source_target_pairs={{0,128},{128,0},{1,129},{129,1},{2,130},{130,2},{3,131},{131,3},{4... | collective-permute-start | bytes 3464 | tf_op jit(solution)/shard_map/ppermute | solution.py:39
  14.2 0.7 %add_convert_fusion.flags_ref = s32[4]{0:T(128)} fusion(pred[1]{0:T(512)(128)(4,1)} %bitcast.3, pred[1]{0:T(512)(128)(4,1)} %bitcast.2, pred[1]{0:T(512)(128)(4,1)} %bitcast.1, pred[1]{0:T(512)(128)(4,1)} %bitcast), kind=kLoop, calls=%fused_computation.19 | loop fusion | flops 16 | bytes 20 | tf_op jit(solution)/shard_map/convert_element_type | solution.py:230
  14.9 0.1 pad.19.clone
  14.9 7.5 %collective-permute-done.2 = f32[2,72,2]{2,1,0:T(8,128)S(1)} collective-permute-done((f32[2,72,2]{2,1,0:T(8,128)S(1)}, f32[2,72,2]{2,1,0:T(8,128)S(1)}, u32[]{:S(2)}, u32[]{:S(2)}) %collective-permute-start.2) | collective-permute-done | bytes 1184 | tf_op jit(solution)/shard_map/ppermute | solution.py:39
  22.4 0.0 collective-permute-done.3
  22.4 0.8 %pad_maximum_fusion.noise_ref = f32[2,72,384]{2,1,0:T(8,128)} fusion(f32[2,72,2]{2,1,0:T(8,128)S(1)} %get-tuple-element.7, f32[2,72,2]{2,1,0:T(8,128)S(1)} %get-tuple-element.6, f32[2,2,256]{2,1,0:T(2,128)S(1)} %get-tuple-element.13, f32[2,4,256]{2,1,0:T(4,128)S(1)} %broadcast_in_dim.12, f32[2,2,256]{2,1,0:T(2,128)S(1)} %get-tuple-element.12, ...), kind=kLoop, calls=%fused_computation.3 | loop fusion | flops 331776 | bytes 372480 | tf_op jit(solution)/shard_map/concatenate | solution.py:61
  23.2 3.1 %shard_map.50 = (f32[3,32,128]{2,1,0:T(8,128)}, f32[3,32,128]{2,1,0:T(8,128)}) custom-call(s32[4]{0:T(128)} %add_convert_fusion.flags_ref, f32[2,72,384]{2,1,0:T(8,128)} %pad_maximum_fusion.noise_ref, f32[72,1]{1,0:T(8,128)} %broadcast_add_fusion.fine_inflow_ref, f32[40,1]{1,0:T(8,128)} %broadcast_add_fusion.1.coarse_inflow_ref), custom_call_target="tpu_custom_call" | custom-call | tf_op jit(solution)/shard_map/pallas_call | solution.py:242
  (9 shorter events, 0.1 us)
Async XLA Ops:
  0.6 0.9 %copy-start = (f32[1,64,256]{2,1,0:T(8,128)S(1)}, f32[1,64,256]{2,1,0:T(8,128)}, u32[]{:S(2)}) copy-start(f32[1,64,256]{2,1,0:T(8,128)} %param.4) | copy-start | bytes 196612
  1.6 5.2 %copy-start.1 = (f32[1024]{0:T(1024)S(1)}, f32[1024]{0:T(1024)}, u32[]{:S(2)}) copy-start(f32[1024]{0:T(1024)} %param.5) | copy-start | bytes 12292
  1.6 7.6 %collective-permute-start = (f32[2,2,256]{2,1,0:T(2,128)S(1)}, f32[2,2,256]{2,1,0:T(2,128)S(1)}, u32[]{:S(2)}, u32[]{:S(2)}) collective-permute-start(f32[2,2,256]{2,1,0:T(2,128)S(1)} %get-tuple-element.10), channel_id=1, source_target_pairs={{8,16},{16,8},{24,32},{32,24},{40,48},{48,40},{56,64},{64,56},{72,... | collective-permute-start | bytes 12296 | tf_op jit(solution)/shard_map/ppermute | solution.py:39
  6.7 3.7 %collective-permute-start.1 = (f32[2,2,256]{2,1,0:T(2,128)S(1)}, f32[2,2,256]{2,1,0:T(2,128)S(1)}, u32[]{:S(2)}, u32[]{:S(2)}) collective-permute-start(f32[2,2,256]{2,1,0:T(2,128)S(1)} %get-tuple-element.11), channel_id=1, source_target_pairs={{0,8},{8,0},{16,24},{24,16},{32,40},{40,32},{48,56},{56,48},{64,72... | collective-permute-start | bytes 12296 | tf_op jit(solution)/shard_map/ppermute | solution.py:39
  10.5 11.9 %collective-permute-start.2 = (f32[2,72,2]{2,1,0:T(8,128)S(1)}, f32[2,72,2]{2,1,0:T(8,128)S(1)}, u32[]{:S(2)}, u32[]{:S(2)}) collective-permute-start(f32[2,72,2]{2,1,0:T(8,128)S(1)} %get-tuple-element.8), channel_id=1, source_target_pairs={{128,1},{1,128},{129,2},{2,129},{130,3},{3,130},{131,4},{4,131},{1... | collective-permute-start | bytes 3464 | tf_op jit(solution)/shard_map/ppermute | solution.py:39
  12.8 9.6 %collective-permute-start.3 = (f32[2,72,2]{2,1,0:T(8,128)S(1)}, f32[2,72,2]{2,1,0:T(8,128)S(1)}, u32[]{:S(2)}, u32[]{:S(2)}) collective-permute-start(f32[2,72,2]{2,1,0:T(8,128)S(1)} %get-tuple-element.9), channel_id=1, source_target_pairs={{0,128},{128,0},{1,129},{129,1},{2,130},{130,2},{3,131},{131,3},{4... | collective-permute-start | bytes 3464 | tf_op jit(solution)/shard_map/ppermute | solution.py:39

commit v12 on v11

--- a/solution.py
+++ b/solution.py
@@ -57,10 +57,7 @@
     west, east = swapped(
         tall[:, :, :HALO], tall[:, :, -HALO:], strip, strips, ("level", "col"), strip_place
     )
-    gap_cols = FINE_SHAPE[1] - count_cols - 2 * HALO
-    return jnp.concatenate(
-        [tall, east, jnp.zeros((fields, FINE_SHAPE[0], gap_cols), noise.dtype), west], axis=2
-    )
+    return tall, west, east
 
 
 def wrapped_rows(values, start, count, lead):
@@ -77,14 +74,14 @@
     return pltpu.roll(values, 1, axis)
 
 
-def apply_walls(state, flags, inflow_speed, bottom_row, right_col):
+def apply_walls(state, flags, inflow_speed, bottom_row, right_col, left_col=-1):
     depth, along_cols, along_rows = state
     shape = depth.shape
     row_at = lax.broadcasted_iota(jnp.int32, shape, 0)
     col_at = lax.broadcasted_iota(jnp.int32, shape, 1)
     top = jnp.logical_and(row_at == shape[0] - 1, flags[0] == 1)
     bottom = jnp.logical_and(row_at == bottom_row, flags[1] == 1)
-    left = jnp.logical_and(col_at == shape[1] - 1, flags[2] == 1)
+    left = jnp.logical_and(col_at == left_col % shape[1], flags[2] == 1)
     right = jnp.logical_and(col_at == right_col, flags[3] == 1)
 
     def rows_fixed(values, sign):
@@ -134,10 +131,10 @@
     return (depth, moved[1] * damping, moved[2] * damping)
 
 
-def walls_at_rest(state, flags, inflow_speed, bottom_row, right_col):
+def walls_at_rest(state, flags, inflow_speed, bottom_row, right_col, left_col=-1):
     depth, along_cols, _ = state
     depth, along_cols, _ = apply_walls(
-        (depth, along_cols, depth), flags, inflow_speed, bottom_row, right_col
+        (depth, along_cols, depth), flags, inflow_speed, bottom_row, right_col, left_col
     )
     return (depth, along_cols, jnp.zeros_like(depth))
 
@@ -221,6 +218,67 @@
         corr_ref[field] = mean - coarse[field][:out_rows, :out_cols]
 
 
+EDGE_REACH = 32
+
+
+def edge_kernel(
+    flags_ref, noise_ref, fine_inflow_ref, coarse_inflow_ref, main_mean_ref, main_corr_ref,
+    mean_ref, corr_ref,
+):
+    flags = [flags_ref[i] for i in range(4)]
+    fine_rows = FINE_SHAPE[0]
+    coarse_rows = COARSE_SHAPE[0]
+    out_rows, out_cols = mean_ref.shape[1], mean_ref.shape[2]
+    tile_rows = 2 * out_rows
+    lanes = noise_ref.shape[2]
+    half = lanes // 2
+    fine_coef = noise_ref[0]
+    noise_height = noise_ref[1]
+    depth = 1.0 + 0.1 * noise_height
+    state = (depth, 0.5 * depth, jnp.zeros_like(depth))
+    fine_inflow = jnp.broadcast_to(fine_inflow_ref[...], fine_coef.shape)
+    fine_left, fine_right = EDGE_REACH - 1, half + EDGE_REACH
+    state = walls_at_rest(state, flags, fine_inflow, tile_rows, fine_right, fine_left)
+    state = advance_at_rest(state, fine_coef, fine_step)
+    state = apply_walls(state, flags, fine_inflow, tile_rows, fine_right, fine_left)
+    state = advance(state, fine_coef, fine_step)
+
+    rows_sum = pair_matrix((coarse_rows, fine_rows), 0, fine_rows - 2)
+    cols_sum = pair_matrix((lanes, lanes), 1, None)
+    paired = matmul(rows_sum, jnp.concatenate([fine_coef, noise_height], axis=1))
+    small = matmul(jnp.concatenate([paired[:, :lanes], paired[:, lanes:]], axis=0), cols_sum)
+    coarse_coef = small[:coarse_rows] * 0.25
+    depth = 1.0 + 0.1 * (small[coarse_rows:] * 0.25)
+    coarse = (depth, 0.5 * depth, jnp.zeros_like(depth))
+    coarse_inflow = jnp.broadcast_to(coarse_inflow_ref[...], depth.shape)
+    coarse_left, coarse_right = EDGE_REACH // 2 - 1, half // 2 + EDGE_REACH // 2
+    coarse = walls_at_rest(coarse, flags, coarse_inflow, out_rows, coarse_right, coarse_left)
+    coarse = advance_at_rest(coarse, coarse_coef, coarse_step)
+
+    rows_out = pair_matrix((out_rows, tile_rows), 0, None)
+    paired = matmul(
+        rows_out, jnp.concatenate([values[:tile_rows, :] for values in state], axis=1)
+    )
+    stacked = jnp.concatenate(
+        [paired[:, field * lanes: (field + 1) * lanes] for field in range(3)], axis=0
+    )
+    means = matmul(stacked, cols_sum)
+    lane_at = lax.broadcasted_iota(jnp.int32, (out_rows, lanes), 1)
+    first, last = EDGE_REACH // 2, half // 2 + EDGE_REACH // 2 - 1
+
+    def patched(edge_values, main_values):
+        to_first = pltpu.roll(edge_values, (lanes - first) % lanes, 1)
+        to_last = pltpu.roll(edge_values, (out_cols - 1 - last) % lanes, 1)
+        return jnp.where(
+            lane_at == 0, to_first, jnp.where(lane_at == out_cols - 1, to_last, main_values)
+        )
+
+    for field in range(3):
+        mean = means[field * out_rows: (field + 1) * out_rows] * 0.25
+        mean_ref[field] = patched(mean, main_mean_ref[field])
+        corr_ref[field] = patched(mean - coarse[field][:out_rows, :], main_corr_ref[field])
+
+
 def body(friction, height, inflow):
     strip = lax.axis_index("col") * lax.axis_size("level") + lax.axis_index("level")
     strips = lax.axis_size("col") * lax.axis_size("level")
@@ -231,7 +289,15 @@
     tile_rows, tile_cols = friction.shape[1], friction.shape[2]
     out_rows, out_cols = tile_rows // 2, tile_cols // 2
 
-    noise = with_halo(jnp.concatenate([friction, height], axis=0))
+    tall, west, east = with_halo(jnp.concatenate([friction, height], axis=0))
+    fields = tall.shape[0]
+    gap = jnp.zeros((fields, FINE_SHAPE[0], FINE_SHAPE[1] - tile_cols), tall.dtype)
+    noise = jnp.concatenate([tall, gap], axis=2)
+    pad = jnp.zeros((fields, FINE_SHAPE[0], EDGE_REACH - HALO), tall.dtype)
+    packed = jnp.concatenate(
+        [pad, west, tall[:, :, :EDGE_REACH], tall[:, :, tile_cols - EDGE_REACH:], east, pad],
+        axis=2,
+    )
     lead = FINE_SHAPE[0] - tile_rows - HALO
     fine_inflow = wrapped_rows(inflow, row_index * tile_rows, FINE_SHAPE[0], lead)
     lead = COARSE_SHAPE[0] - out_rows - 1
@@ -245,6 +311,12 @@
         in_specs=[pl.BlockSpec(memory_space=pltpu.SMEM), vmem, vmem, vmem],
         out_specs=(vmem, vmem),
     )(flags, noise, fine_inflow, coarse_inflow)
+    mean, corr = pl.pallas_call(
+        edge_kernel,
+        out_shape=(out, out),
+        in_specs=[pl.BlockSpec(memory_space=pltpu.SMEM)] + [vmem] * 5,
+        out_specs=(vmem, vmem),
+    )(flags, packed, fine_inflow, coarse_inflow, mean, corr)
     return (mean[None], corr[None])
 
 

time: 26.5 us -> 27.2 us (1.026)
  the two profiles are of different devices: /device:TPU:192 before, /device:TPU:25 now
where the time goes in v12:
time: 27.2 us; the launch traced here: 27 us
  starting transfers between devices  14.1 us (52%)
  Pallas kernels  5.78 us (21%)
  local copies, waits for them, and re-layouts  3.94 us (14%)
  other arithmetic  2.39 us (9%)
  between operations  0.75 us (3%)
    ppermute x4, starting transfers between devices, swapped(): got.append(lax.ppermute(block, axis, swap_pairs(count, parity, place)))  14.1 us
    pallas_call x1, Pallas kernels, body(): pl.pallas_call(level_kernel, out_shape=(out, out), in_specs=[pl.BlockSpec...  3.13 us
    pallas_call x1, Pallas kernels, body(): pl.pallas_call(edge_kernel, out_shape=(out, out), in_specs=[pl.BlockSpec(...  2.65 us
    unnamed x5, local copies, waits for them, and re-layouts  1.57 us
    add x2, other arithmetic, wrapped_rows(): return (0.5 + jnp.roll(window, -lead)).reshape(count, 1)  1.23 us
    concatenate x1, local copies, waits for them, and re-layouts, body(): jnp.concatenate([pad, west, tall[:, :, :EDGE_REACH], tall[:, :, tile_cols...  0.79 us
    concatenate x1, local copies, waits for them, and re-layouts, body(): noise = jnp.concatenate([tall, gap], axis=2)  0.71 us
    convert_element_type x1, other arithmetic, body(): flags = jnp.stack([row_index == 0, row_index == lax.axis_size('row') - 1,...  0.58 us
  transfers between devices with their start and end apart: 4, of which 0 were waited for; matrix products, arithmetic and copies ran while one was open for 14% of the time, Pallas kernels for 12%

profile of v12, /device:TPU:25, one launch (start us, length us, event | category | flops | bytes accessed | tf_op | source)
XLA Modules:
  0.0 27.0 jit_solution(18068966285508817070)
XLA Ops:
  0.6 0.0 copy-start
  0.7 0.9 %constant_dynamic-update-slice_fusion.1 = f32[2,64,256]{2,1,0:T(8,128)S(1)} fusion(f32[1,64,256]{2,1,0:T(8,128)} %param.3), kind=kLoop, calls=%fused_computation.12 | loop fusion | bytes 131072
  1.6 0.7 %collective-permute-start = (f32[2,2,256]{2,1,0:T(2,128)S(1)}, f32[2,2,256]{2,1,0:T(2,128)S(1)}, u32[]{:S(2)}, u32[]{:S(2)}) collective-permute-start(f32[2,2,256]{2,1,0:T(2,128)S(1)} %get-tuple-element.16), channel_id=1, source_target_pairs={{8,16},{16,8},{24,32},{32,24},{40,48},{48,40},{56,64},{64,56},{72,... | collective-permute-start | bytes 12296 | tf_op jit(solution)/shard_map/ppermute | solution.py:39
  2.2 3.8 %collective-permute-start.1 = (f32[2,2,256]{2,1,0:T(2,128)S(1)}, f32[2,2,256]{2,1,0:T(2,128)S(1)}, u32[]{:S(2)}, u32[]{:S(2)}) collective-permute-start(f32[2,2,256]{2,1,0:T(2,128)S(1)} %get-tuple-element.17), channel_id=1, source_target_pairs={{0,8},{8,0},{16,24},{24,16},{32,40},{40,32},{48,56},{56,48},{64,72... | collective-permute-start | bytes 12296 | tf_op jit(solution)/shard_map/ppermute | solution.py:39
  6.0 0.7 %copy-done.1 = f32[1024]{0:T(1024)S(1)} copy-done((f32[1024]{0:T(1024)S(1)}, f32[1024]{0:T(1024)}, u32[]{:S(2)}) %copy-start.1) | copy-done | bytes 4120
  6.7 0.1 pad_dynamic-slice_fusion
  6.8 0.1 slice_bitcast_fusion.3
  6.8 0.2 reshape.70
  7.0 0.2 fusion.1
  7.3 0.1 pad_dynamic-slice_fusion.1
  7.4 0.1 slice_bitcast_fusion.1
  7.4 0.1 pad_maximum_fusion.1
  7.5 0.1 copy.13
  7.6 0.6 %broadcast_add_fusion.fine_inflow_ref = f32[72,1]{1,0:T(8,128)} fusion(f32[72,1]{1,0:T(8,128)S(1)} %copy.13), kind=kLoop, calls=%fused_computation.8 | loop fusion | flops 72 | bytes 576 | tf_op jit(solution)/shard_map/add | solution.py:66
  8.2 0.1 pad_maximum_fusion.2
  8.3 0.1 copy.14
  8.4 0.6 %broadcast_add_fusion.1.coarse_inflow_ref = f32[40,1]{1,0:T(8,128)} fusion(f32[40,1]{1,0:T(8,128)S(1)} %copy.14), kind=kLoop, calls=%fused_computation.9 | loop fusion | flops 40 | bytes 320 | tf_op jit(solution)/shard_map/add | solution.py:66
  9.0 0.6 %add_convert_fusion.flags_ref = s32[4]{0:T(128)} fusion(pred[1]{0:T(512)(128)(4,1)} %bitcast.3, pred[1]{0:T(512)(128)(4,1)} %bitcast.2, pred[1]{0:T(512)(128)(4,1)} %bitcast.1, pred[1]{0:T(512)(128)(4,1)} %bitcast), kind=kLoop, calls=%fused_computation.18 | loop fusion | flops 16 | bytes 20 | tf_op jit(solution)/shard_map/convert_element_type | solution.py:288
  9.6 0.1 pad.17.clone
  9.7 0.0 collective-permute-done
  9.7 0.0 collective-permute-done.1
  9.7 0.1 pad_maximum_fusion
  9.8 0.1 slice_select_fusion
  9.9 9.6 %collective-permute-start.3 = (f32[2,72,2]{2,1,0:T(8,128)S(1)}, f32[2,72,2]{2,1,0:T(8,128)S(1)}, u32[]{:S(2)}, u32[]{:S(2)}) collective-permute-start(f32[2,72,2]{2,1,0:T(8,128)S(1)} %get-tuple-element.14), channel_id=1, source_target_pairs={{128,1},{1,128},{129,2},{2,129},{130,3},{3,130},{131,4},{4,131},{1... | collective-permute-start | bytes 3464 | tf_op jit(solution)/shard_map/ppermute | solution.py:39
  19.5 0.1 collective-permute-start.2
  19.6 0.1 fusion.2
  19.7 0.7 %concatenate.51.noise_ref = f32[2,72,384]{2,1,0:T(8,128)} pad(f32[2,72,256]{2,1,0:T(8,128)S(1)} %pad_maximum_fusion, f32[]{:T(128)} %constant.45.clone.1), padding=0_0x0_0x0_128 | pad | bytes 368644 | tf_op jit(solution)/shard_map/concatenate | solution.py:295
  20.4 3.1 %shard_map.50 = (f32[3,32,128]{2,1,0:T(8,128)}, f32[3,32,128]{2,1,0:T(8,128)}) custom-call(s32[4]{0:T(128)} %add_convert_fusion.flags_ref, f32[2,72,384]{2,1,0:T(8,128)} %concatenate.51.noise_ref, f32[72,1]{1,0:T(8,128)} %broadcast_add_fusion.fine_inflow_ref, f32[40,1]{1,0:T(8,128)} %broadcast_add_fusion.1.coarse_inflow_ref), custom_call_target="tpu_custom_call" | custom-call | tf_op jit(solution)/shard_map/pallas_call | solution.py:308
  23.5 0.0 collective-permute-done.3
  23.5 0.0 collective-permute-done.2
  23.5 0.8 %concatenate.44.noise_ref = f32[2,72,128]{2,1,0:T(8,128)} concatenate(f32[2,72,30]{2,1,0:T(8,128)S(1)} %broadcast_in_dim.13, f32[2,72,2]{2,1,0:T(8,128)S(1)} %get-tuple-element.11, f32[2,72,32]{2,1,0:T(8,128)S(1)} %get-tuple-element.13, f32[2,72,32]{2,1,0:T(8,128)S(1)} %get-tuple-element.12, f32[2,72,2]{2,1,0:T(8,128)S(1)} %get-tuple-element.10, f32[2,72,30]{2,1,0:T(8,128)S(1)} %broadcast_in_dim.13), dimensions={2} | concatenate | bytes 147456 | tf_op jit(solution)/shard_map/concatenate | solution.py:297
  24.3 2.6 %shard_map.51 = (f32[3,32,128]{2,1,0:T(8,128)}, f32[3,32,128]{2,1,0:T(8,128)}) custom-call(s32[4]{0:T(128)} %add_convert_fusion.flags_ref, f32[2,72,128]{2,1,0:T(8,128)} %concatenate.44.noise_ref, f32[72,1]{1,0:T(8,128)} %broadcast_add_fusion.fine_inflow_ref, f32[40,1]{1,0:T(8,128)} %broadcast_add_fusion.1.coarse_inflow_ref, ...), custom_call_target="tpu_custom_call" | custom-call | tf_op jit(solution)/shard_map/pallas_call | solution.py:314
  (10 shorter events, 0.1 us)
Async XLA Ops:
  0.6 0.9 %copy-start = (f32[1,64,256]{2,1,0:T(8,128)S(1)}, f32[1,64,256]{2,1,0:T(8,128)}, u32[]{:S(2)}) copy-start(f32[1,64,256]{2,1,0:T(8,128)} %param.4) | copy-start | bytes 196612
  1.6 8.1 %collective-permute-start = (f32[2,2,256]{2,1,0:T(2,128)S(1)}, f32[2,2,256]{2,1,0:T(2,128)S(1)}, u32[]{:S(2)}, u32[]{:S(2)}) collective-permute-start(f32[2,2,256]{2,1,0:T(2,128)S(1)} %get-tuple-element.16), channel_id=1, source_target_pairs={{8,16},{16,8},{24,32},{32,24},{40,48},{48,40},{56,64},{64,56},{72,... | collective-permute-start | bytes 12296 | tf_op jit(solution)/shard_map/ppermute | solution.py:39
  2.2 7.4 %collective-permute-start.1 = (f32[2,2,256]{2,1,0:T(2,128)S(1)}, f32[2,2,256]{2,1,0:T(2,128)S(1)}, u32[]{:S(2)}, u32[]{:S(2)}) collective-permute-start(f32[2,2,256]{2,1,0:T(2,128)S(1)} %get-tuple-element.17), channel_id=1, source_target_pairs={{0,8},{8,0},{16,24},{24,16},{32,40},{40,32},{48,56},{56,48},{64,72... | collective-permute-start | bytes 12296 | tf_op jit(solution)/shard_map/ppermute | solution.py:39
  6.0 0.7 %copy-start.1 = (f32[1024]{0:T(1024)S(1)}, f32[1024]{0:T(1024)}, u32[]{:S(2)}) copy-start(f32[1024]{0:T(1024)} %param.5) | copy-start | bytes 12292
  9.9 13.6 %collective-permute-start.3 = (f32[2,72,2]{2,1,0:T(8,128)S(1)}, f32[2,72,2]{2,1,0:T(8,128)S(1)}, u32[]{:S(2)}, u32[]{:S(2)}) collective-permute-start(f32[2,72,2]{2,1,0:T(8,128)S(1)} %get-tuple-element.14), channel_id=1, source_target_pairs={{128,1},{1,128},{129,2},{2,129},{130,3},{3,130},{131,4},{4,131},{1... | collective-permute-start | bytes 3464 | tf_op jit(solution)/shard_map/ppermute | solution.py:39
  19.5 4.0 %collective-permute-start.2 = (f32[2,72,2]{2,1,0:T(8,128)S(1)}, f32[2,72,2]{2,1,0:T(8,128)S(1)}, u32[]{:S(2)}, u32[]{:S(2)}) collective-permute-start(f32[2,72,2]{2,1,0:T(8,128)S(1)} %get-tuple-element.15), channel_id=1, source_target_pairs={{0,128},{128,0},{1,129},{129,1},{2,130},{130,2},{3,131},{131,3},{4... | collective-permute-start | bytes 3464 | tf_op jit(solution)/shard_map/ppermute | solution.py:39

commit v13 on v11

--- a/solution.py
+++ b/solution.py
@@ -178,8 +178,16 @@
     return jnp.dot(a, b, precision=lax.Precision.HIGHEST, preferred_element_type=jnp.float32)
 
 
-def level_kernel(flags_ref, noise_ref, fine_inflow_ref, coarse_inflow_ref, mean_ref, corr_ref):
-    flags = [flags_ref[i] for i in range(4)]
+def boundary_flags():
+    strip = lax.axis_index("col") * lax.axis_size("level") + lax.axis_index("level")
+    strips = lax.axis_size("col") * lax.axis_size("level")
+    row_index = lax.axis_index("row")
+    edges = (row_index == 0, row_index == lax.axis_size("row") - 1, strip == 0, strip == strips - 1)
+    return [edge.astype(jnp.int32) for edge in edges]
+
+
+def level_kernel(noise_ref, fine_inflow_ref, coarse_inflow_ref, mean_ref, corr_ref):
+    flags = boundary_flags()
     fine_rows, fine_cols = FINE_SHAPE
     coarse_rows, coarse_cols = COARSE_SHAPE
     out_rows, out_cols = mean_ref.shape[1], mean_ref.shape[2]
@@ -222,12 +230,7 @@
 
 
 def body(friction, height, inflow):
-    strip = lax.axis_index("col") * lax.axis_size("level") + lax.axis_index("level")
-    strips = lax.axis_size("col") * lax.axis_size("level")
     row_index = lax.axis_index("row")
-    flags = jnp.stack(
-        [row_index == 0, row_index == lax.axis_size("row") - 1, strip == 0, strip == strips - 1]
-    ).astype(jnp.int32)
     tile_rows, tile_cols = friction.shape[1], friction.shape[2]
     out_rows, out_cols = tile_rows // 2, tile_cols // 2
 
@@ -242,9 +245,9 @@
     mean, corr = pl.pallas_call(
         level_kernel,
         out_shape=(out, out),
-        in_specs=[pl.BlockSpec(memory_space=pltpu.SMEM), vmem, vmem, vmem],
+        in_specs=[vmem, vmem, vmem],
         out_specs=(vmem, vmem),
-    )(flags, noise, fine_inflow, coarse_inflow)
+    )(noise, fine_inflow, coarse_inflow)
     return (mean[None], corr[None])
 
 

time: 26.5 us -> 26.3 us (level)
  other arithmetic: 3.17 us -> 2.52 us
  waiting for transfers between devices: 8.72 us -> 9.18 us
    convert_element_type x1 -> x0, other arithmetic: 0.65 us -> none  [body(): flags = jnp.stack([row_index == 0, row_index == lax.axis_size('row') - 1,...]
    ppermute x4, waiting for transfers between devices: 8.72 us -> 9.18 us  [swapped(): got.append(lax.ppermute(block, axis, swap_pairs(count, parity, place)))]
  transfers between devices with their start and end apart: 4 -> 4, of which waited for: 3 -> 3; matrix products, arithmetic and copies ran while one was open for 12% -> 9% of each run, Pallas kernels for 0% -> 0%
where the time goes in v13:
time: 26.3 us; the launch traced here: 26.1 us
  waiting for transfers between devices  9.18 us (35%)
  starting transfers between devices  8.89 us (34%)
  Pallas kernels  3.11 us (12%)
  other arithmetic  2.52 us (10%)
  local copies, waits for them, and re-layouts  1.68 us (6%)
  between operations  0.75 us (3%)
    ppermute x4, waiting for transfers between devices, swapped(): got.append(lax.ppermute(block, axis, swap_pairs(count, parity, place)))  9.18 us
    ppermute x4, starting transfers between devices, swapped(): got.append(lax.ppermute(block, axis, swap_pairs(count, parity, place)))  8.89 us
    pallas_call x1, Pallas kernels, body(): pl.pallas_call(level_kernel, out_shape=(out, out), in_specs=[vmem, vmem,...  3.11 us
    add x2, other arithmetic, wrapped_rows(): return (0.5 + jnp.roll(window, -lead)).reshape(count, 1)  1.22 us
    unnamed x5, local copies, waits for them, and re-layouts  0.89 us
    concatenate x1, other arithmetic, with_halo(): jnp.concatenate([tall, east, jnp.zeros((fields, FINE_SHAPE[0], gap_cols),...  0.78 us
  transfers between devices with their start and end apart: 4, of which 3 were waited for; matrix products, arithmetic and copies ran while one was open for 9% of the time, Pallas kernels for 0%

profile of v13, /device:TPU:192, one launch (start us, length us, event | category | flops | bytes accessed | tf_op | source)
XLA Modules:
  0.0 26.1 jit_solution(15561948344501728994)
XLA Ops:
  0.6 0.0 copy-start
  0.7 0.9 %constant_dynamic-update-slice_fusion.1 = f32[2,64,256]{2,1,0:T(8,128)S(1)} fusion(f32[1,64,256]{2,1,0:T(8,128)} %param.3), kind=kLoop, calls=%fused_computation.13 | loop fusion | bytes 131072
  1.5 0.0 copy-done
  1.6 0.0 copy-start.1
  1.6 5.1 %collective-permute-start = (f32[2,2,256]{2,1,0:T(2,128)S(1)}, f32[2,2,256]{2,1,0:T(2,128)S(1)}, u32[]{:S(2)}, u32[]{:S(2)}) collective-permute-start(f32[2,2,256]{2,1,0:T(2,128)S(1)} %get-tuple-element.10), channel_id=1, source_target_pairs={{8,16},{16,8},{24,32},{32,24},{40,48},{48,40},{56,64},{64,56},{72,... | collective-permute-start | bytes 12296 | tf_op jit(solution)/shard_map/ppermute | solution.py:39
  6.7 0.1 collective-permute-start.1
  6.8 0.0 copy-done.1
  6.8 0.2 reshape.70
  7.0 0.2 fusion.1
  7.2 0.1 pad_dynamic-slice_fusion.1
  7.3 0.1 slice_bitcast_fusion.1
  7.4 0.1 pad_dynamic-slice_fusion
  7.5 0.1 slice_bitcast_fusion.3
  7.6 0.1 pad_maximum_fusion.2
  7.6 0.1 copy.15
  7.7 0.6 %broadcast_add_fusion.fine_inflow_ref = f32[72,1]{1,0:T(8,128)} fusion(f32[72,1]{1,0:T(8,128)S(1)} %copy.15), kind=kLoop, calls=%fused_computation.9 | loop fusion | flops 72 | bytes 576 | tf_op jit(solution)/shard_map/add | solution.py:69
  8.4 0.1 pad_maximum_fusion.3
  8.4 0.1 copy.17
  8.5 0.7 %collective-permute-done = f32[2,2,256]{2,1,0:T(2,128)S(1)} collective-permute-done((f32[2,2,256]{2,1,0:T(2,128)S(1)}, f32[2,2,256]{2,1,0:T(2,128)S(1)}, u32[]{:S(2)}, u32[]{:S(2)}) %collective-permute-start) | collective-permute-done | bytes 4128 | tf_op jit(solution)/shard_map/ppermute | solution.py:39
  9.2 1.2 %collective-permute-done.1 = f32[2,2,256]{2,1,0:T(2,128)S(1)} collective-permute-done((f32[2,2,256]{2,1,0:T(2,128)S(1)}, f32[2,2,256]{2,1,0:T(2,128)S(1)}, u32[]{:S(2)}, u32[]{:S(2)}) %collective-permute-start.1) | collective-permute-done | bytes 4128 | tf_op jit(solution)/shard_map/ppermute | solution.py:39
  10.4 0.1 slice_select_fusion.1
  10.5 2.0 %collective-permute-start.2 = (f32[2,72,2]{2,1,0:T(8,128)S(1)}, f32[2,72,2]{2,1,0:T(8,128)S(1)}, u32[]{:S(2)}, u32[]{:S(2)}) collective-permute-start(f32[2,72,2]{2,1,0:T(8,128)S(1)} %get-tuple-element.8), channel_id=1, source_target_pairs={{128,1},{1,128},{129,2},{2,129},{130,3},{3,130},{131,4},{4,131},{1... | collective-permute-start | bytes 3464 | tf_op jit(solution)/shard_map/ppermute | solution.py:39
  12.5 1.7 %collective-permute-start.3 = (f32[2,72,2]{2,1,0:T(8,128)S(1)}, f32[2,72,2]{2,1,0:T(8,128)S(1)}, u32[]{:S(2)}, u32[]{:S(2)}) collective-permute-start(f32[2,72,2]{2,1,0:T(8,128)S(1)} %get-tuple-element.9), channel_id=1, source_target_pairs={{0,128},{128,0},{1,129},{129,1},{2,130},{130,2},{3,131},{131,3},{4... | collective-permute-start | bytes 3464 | tf_op jit(solution)/shard_map/ppermute | solution.py:39
  14.2 0.6 %broadcast_add_fusion.1.coarse_inflow_ref = f32[40,1]{1,0:T(8,128)} fusion(f32[40,1]{1,0:T(8,128)S(1)} %copy.17), kind=kLoop, calls=%fused_computation.10 | loop fusion | flops 40 | bytes 320 | tf_op jit(solution)/shard_map/add | solution.py:69
  14.8 0.1 pad.19.clone
  14.9 7.3 %collective-permute-done.2 = f32[2,72,2]{2,1,0:T(8,128)S(1)} collective-permute-done((f32[2,72,2]{2,1,0:T(8,128)S(1)}, f32[2,72,2]{2,1,0:T(8,128)S(1)}, u32[]{:S(2)}, u32[]{:S(2)}) %collective-permute-start.2) | collective-permute-done | bytes 1184 | tf_op jit(solution)/shard_map/ppermute | solution.py:39
  22.2 0.0 collective-permute-done.3
  22.2 0.8 %pad_maximum_fusion.noise_ref = f32[2,72,384]{2,1,0:T(8,128)} fusion(f32[2,72,2]{2,1,0:T(8,128)S(1)} %get-tuple-element.7, f32[2,72,2]{2,1,0:T(8,128)S(1)} %get-tuple-element.6, f32[2,2,256]{2,1,0:T(2,128)S(1)} %get-tuple-element.13, f32[2,4,256]{2,1,0:T(4,128)S(1)} %broadcast_in_dim.12, f32[2,2,256]{2,1,0:T(2,128)S(1)} %get-tuple-element.12, ...), kind=kLoop, calls=%fused_computation.3 | loop fusion | flops 331776 | bytes 372480 | tf_op jit(solution)/shard_map/concatenate | solution.py:61
  23.0 3.1 %shard_map.50 = (f32[3,32,128]{2,1,0:T(8,128)}, f32[3,32,128]{2,1,0:T(8,128)}) custom-call(f32[2,72,384]{2,1,0:T(8,128)} %pad_maximum_fusion.noise_ref, f32[72,1]{1,0:T(8,128)} %broadcast_add_fusion.fine_inflow_ref, f32[40,1]{1,0:T(8,128)} %broadcast_add_fusion.1.coarse_inflow_ref), custom_call_target="tpu_custom_call" | custom-call | tf_op jit(solution)/shard_map/pallas_call | solution.py:245
  (9 shorter events, 0.1 us)
Async XLA Ops:
  0.6 0.9 %copy-start = (f32[1,64,256]{2,1,0:T(8,128)S(1)}, f32[1,64,256]{2,1,0:T(8,128)}, u32[]{:S(2)}) copy-start(f32[1,64,256]{2,1,0:T(8,128)} %param.4) | copy-start | bytes 196612
  1.6 5.2 %copy-start.1 = (f32[1024]{0:T(1024)S(1)}, f32[1024]{0:T(1024)}, u32[]{:S(2)}) copy-start(f32[1024]{0:T(1024)} %param.5) | copy-start | bytes 12292
  1.6 7.6 %collective-permute-start = (f32[2,2,256]{2,1,0:T(2,128)S(1)}, f32[2,2,256]{2,1,0:T(2,128)S(1)}, u32[]{:S(2)}, u32[]{:S(2)}) collective-permute-start(f32[2,2,256]{2,1,0:T(2,128)S(1)} %get-tuple-element.10), channel_id=1, source_target_pairs={{8,16},{16,8},{24,32},{32,24},{40,48},{48,40},{56,64},{64,56},{72,... | collective-permute-start | bytes 12296 | tf_op jit(solution)/shard_map/ppermute | solution.py:39
  6.7 3.7 %collective-permute-start.1 = (f32[2,2,256]{2,1,0:T(2,128)S(1)}, f32[2,2,256]{2,1,0:T(2,128)S(1)}, u32[]{:S(2)}, u32[]{:S(2)}) collective-permute-start(f32[2,2,256]{2,1,0:T(2,128)S(1)} %get-tuple-element.11), channel_id=1, source_target_pairs={{0,8},{8,0},{16,24},{24,16},{32,40},{40,32},{48,56},{56,48},{64,72... | collective-permute-start | bytes 12296 | tf_op jit(solution)/shard_map/ppermute | solution.py:39
  10.5 11.7 %collective-permute-start.2 = (f32[2,72,2]{2,1,0:T(8,128)S(1)}, f32[2,72,2]{2,1,0:T(8,128)S(1)}, u32[]{:S(2)}, u32[]{:S(2)}) collective-permute-start(f32[2,72,2]{2,1,0:T(8,128)S(1)} %get-tuple-element.8), channel_id=1, source_target_pairs={{128,1},{1,128},{129,2},{2,129},{130,3},{3,130},{131,4},{4,131},{1... | collective-permute-start | bytes 3464 | tf_op jit(solution)/shard_map/ppermute | solution.py:39
  12.5 9.7 %collective-permute-start.3 = (f32[2,72,2]{2,1,0:T(8,128)S(1)}, f32[2,72,2]{2,1,0:T(8,128)S(1)}, u32[]{:S(2)}, u32[]{:S(2)}) collective-permute-start(f32[2,72,2]{2,1,0:T(8,128)S(1)} %get-tuple-element.9), channel_id=1, source_target_pairs={{0,128},{128,0},{1,129},{129,1},{2,130},{130,2},{3,131},{131,3},{4... | collective-permute-start | bytes 3464 | tf_op jit(solution)/shard_map/ppermute | solution.py:39

commit v14 on v13

--- a/solution.py
+++ b/solution.py
@@ -174,8 +174,17 @@
     return hit.astype(jnp.float32)
 
 
-def matmul(a, b):
-    return jnp.dot(a, b, precision=lax.Precision.HIGHEST, preferred_element_type=jnp.float32)
+def pair_sum(pairs, values, pairs_first):
+    pairs = pairs.astype(jnp.bfloat16)
+    total = None
+    rest = values
+    for _ in range(3):
+        part = rest.astype(jnp.bfloat16)
+        rest = rest - part.astype(jnp.float32)
+        operands = (pairs, part) if pairs_first else (part, pairs)
+        product = jnp.dot(*operands, preferred_element_type=jnp.float32)
+        total = product if total is None else total + product
+    return total
 
 
 def boundary_flags():
@@ -205,8 +214,10 @@
 
     rows_sum = pair_matrix((coarse_rows, fine_rows), 0, fine_rows - 2)
     cols_sum = pair_matrix((fine_cols, coarse_cols), 1, fine_cols - 2)
-    paired = matmul(rows_sum, jnp.concatenate([fine_coef, noise_height], axis=1))
-    small = matmul(jnp.concatenate([paired[:, :fine_cols], paired[:, fine_cols:]], axis=0), cols_sum)
+    paired = pair_sum(rows_sum, jnp.concatenate([fine_coef, noise_height], axis=1), True)
+    small = pair_sum(
+        cols_sum, jnp.concatenate([paired[:, :fine_cols], paired[:, fine_cols:]], axis=0), False
+    )
     coarse_coef = small[:coarse_rows] * 0.25
     depth = 1.0 + 0.1 * (small[coarse_rows:] * 0.25)
     coarse = (depth, 0.5 * depth, jnp.zeros_like(depth))
@@ -216,13 +227,15 @@
 
     rows_out = pair_matrix((out_rows, tile_rows), 0, None)
     cols_out = pair_matrix((tile_cols, out_cols), 1, None)
-    paired = matmul(
-        rows_out, jnp.concatenate([values[:tile_rows, :tile_cols] for values in state], axis=1)
+    paired = pair_sum(
+        rows_out,
+        jnp.concatenate([values[:tile_rows, :tile_cols] for values in state], axis=1),
+        True,
     )
     stacked = jnp.concatenate(
         [paired[:, field * tile_cols: (field + 1) * tile_cols] for field in range(3)], axis=0
     )
-    means = matmul(stacked, cols_out)
+    means = pair_sum(cols_out, stacked, False)
     for field in range(3):
         mean = means[field * out_rows: (field + 1) * out_rows] * 0.25
         mean_ref[field] = mean

time: 26.3 us -> 26.1 us (level)
  no operation moved by 1% of the time
where the time goes in v14:
time: 26.1 us; the launch traced here: 25.9 us
  waiting for transfers between devices  9.18 us (35%)
  starting transfers between devices  8.89 us (34%)
  Pallas kernels  2.92 us (11%)
  other arithmetic  2.52 us (10%)
  local copies, waits for them, and re-layouts  1.68 us (6%)
  between operations  0.75 us (3%)
    ppermute x4, waiting for transfers between devices, swapped(): got.append(lax.ppermute(block, axis, swap_pairs(count, parity, place)))  9.18 us
    ppermute x4, starting transfers between devices, swapped(): got.append(lax.ppermute(block, axis, swap_pairs(count, parity, place)))  8.89 us
    pallas_call x1, Pallas kernels, body(): pl.pallas_call(level_kernel, out_shape=(out, out), in_specs=[vmem, vmem,...  2.92 us
    add x2, other arithmetic, wrapped_rows(): return (0.5 + jnp.roll(window, -lead)).reshape(count, 1)  1.22 us
    unnamed x5, local copies, waits for them, and re-layouts  0.89 us
    concatenate x1, other arithmetic, with_halo(): jnp.concatenate([tall, east, jnp.zeros((fields, FINE_SHAPE[0], gap_cols),...  0.78 us
  transfers between devices with their start and end apart: 4, of which 3 were waited for; matrix products, arithmetic and copies ran while one was open for 9% of the time, Pallas kernels for 0%

profile of v14, /device:TPU:192, one launch (start us, length us, event | category | flops | bytes accessed | tf_op | source)
XLA Modules:
  0.0 25.9 jit_solution(17817531713310297900)
XLA Ops:
  0.6 0.0 copy-start
  0.7 0.9 %constant_dynamic-update-slice_fusion.1 = f32[2,64,256]{2,1,0:T(8,128)S(1)} fusion(f32[1,64,256]{2,1,0:T(8,128)} %param.3), kind=kLoop, calls=%fused_computation.13 | loop fusion | bytes 131072
  1.5 0.0 copy-done
  1.6 0.0 copy-start.1
  1.6 5.1 %collective-permute-start = (f32[2,2,256]{2,1,0:T(2,128)S(1)}, f32[2,2,256]{2,1,0:T(2,128)S(1)}, u32[]{:S(2)}, u32[]{:S(2)}) collective-permute-start(f32[2,2,256]{2,1,0:T(2,128)S(1)} %get-tuple-element.10), channel_id=1, source_target_pairs={{8,16},{16,8},{24,32},{32,24},{40,48},{48,40},{56,64},{64,56},{72,... | collective-permute-start | bytes 12296 | tf_op jit(solution)/shard_map/ppermute | solution.py:39
  6.7 0.1 collective-permute-start.1
  6.8 0.0 copy-done.1
  6.8 0.2 reshape.70
  7.0 0.2 fusion.1
  7.2 0.1 pad_dynamic-slice_fusion.1
  7.3 0.1 slice_bitcast_fusion.1
  7.4 0.1 pad_dynamic-slice_fusion
  7.5 0.1 slice_bitcast_fusion.3
  7.6 0.1 pad_maximum_fusion.2
  7.6 0.1 copy.15
  7.7 0.6 %broadcast_add_fusion.fine_inflow_ref = f32[72,1]{1,0:T(8,128)} fusion(f32[72,1]{1,0:T(8,128)S(1)} %copy.15), kind=kLoop, calls=%fused_computation.9 | loop fusion | flops 72 | bytes 576 | tf_op jit(solution)/shard_map/add | solution.py:69
  8.4 0.1 pad_maximum_fusion.3
  8.4 0.1 copy.17
  8.5 0.7 %collective-permute-done = f32[2,2,256]{2,1,0:T(2,128)S(1)} collective-permute-done((f32[2,2,256]{2,1,0:T(2,128)S(1)}, f32[2,2,256]{2,1,0:T(2,128)S(1)}, u32[]{:S(2)}, u32[]{:S(2)}) %collective-permute-start) | collective-permute-done | bytes 4128 | tf_op jit(solution)/shard_map/ppermute | solution.py:39
  9.2 1.2 %collective-permute-done.1 = f32[2,2,256]{2,1,0:T(2,128)S(1)} collective-permute-done((f32[2,2,256]{2,1,0:T(2,128)S(1)}, f32[2,2,256]{2,1,0:T(2,128)S(1)}, u32[]{:S(2)}, u32[]{:S(2)}) %collective-permute-start.1) | collective-permute-done | bytes 4128 | tf_op jit(solution)/shard_map/ppermute | solution.py:39
  10.4 0.1 slice_select_fusion.1
  10.5 2.0 %collective-permute-start.2 = (f32[2,72,2]{2,1,0:T(8,128)S(1)}, f32[2,72,2]{2,1,0:T(8,128)S(1)}, u32[]{:S(2)}, u32[]{:S(2)}) collective-permute-start(f32[2,72,2]{2,1,0:T(8,128)S(1)} %get-tuple-element.8), channel_id=1, source_target_pairs={{128,1},{1,128},{129,2},{2,129},{130,3},{3,130},{131,4},{4,131},{1... | collective-permute-start | bytes 3464 | tf_op jit(solution)/shard_map/ppermute | solution.py:39
  12.5 1.7 %collective-permute-start.3 = (f32[2,72,2]{2,1,0:T(8,128)S(1)}, f32[2,72,2]{2,1,0:T(8,128)S(1)}, u32[]{:S(2)}, u32[]{:S(2)}) collective-permute-start(f32[2,72,2]{2,1,0:T(8,128)S(1)} %get-tuple-element.9), channel_id=1, source_target_pairs={{0,128},{128,0},{1,129},{129,1},{2,130},{130,2},{3,131},{131,3},{4... | collective-permute-start | bytes 3464 | tf_op jit(solution)/shard_map/ppermute | solution.py:39
  14.2 0.6 %broadcast_add_fusion.1.coarse_inflow_ref = f32[40,1]{1,0:T(8,128)} fusion(f32[40,1]{1,0:T(8,128)S(1)} %copy.17), kind=kLoop, calls=%fused_computation.10 | loop fusion | flops 40 | bytes 320 | tf_op jit(solution)/shard_map/add | solution.py:69
  14.8 0.1 pad.19.clone
  14.9 7.3 %collective-permute-done.2 = f32[2,72,2]{2,1,0:T(8,128)S(1)} collective-permute-done((f32[2,72,2]{2,1,0:T(8,128)S(1)}, f32[2,72,2]{2,1,0:T(8,128)S(1)}, u32[]{:S(2)}, u32[]{:S(2)}) %collective-permute-start.2) | collective-permute-done | bytes 1184 | tf_op jit(solution)/shard_map/ppermute | solution.py:39
  22.2 0.0 collective-permute-done.3
  22.2 0.8 %pad_maximum_fusion.noise_ref = f32[2,72,384]{2,1,0:T(8,128)} fusion(f32[2,72,2]{2,1,0:T(8,128)S(1)} %get-tuple-element.7, f32[2,72,2]{2,1,0:T(8,128)S(1)} %get-tuple-element.6, f32[2,2,256]{2,1,0:T(2,128)S(1)} %get-tuple-element.13, f32[2,4,256]{2,1,0:T(4,128)S(1)} %broadcast_in_dim.12, f32[2,2,256]{2,1,0:T(2,128)S(1)} %get-tuple-element.12, ...), kind=kLoop, calls=%fused_computation.3 | loop fusion | flops 331776 | bytes 372480 | tf_op jit(solution)/shard_map/concatenate | solution.py:61
  23.0 2.9 %shard_map.50 = (f32[3,32,128]{2,1,0:T(8,128)}, f32[3,32,128]{2,1,0:T(8,128)}) custom-call(f32[2,72,384]{2,1,0:T(8,128)} %pad_maximum_fusion.noise_ref, f32[72,1]{1,0:T(8,128)} %broadcast_add_fusion.fine_inflow_ref, f32[40,1]{1,0:T(8,128)} %broadcast_add_fusion.1.coarse_inflow_ref), custom_call_target="tpu_custom_call" | custom-call | tf_op jit(solution)/shard_map/pallas_call | solution.py:258
  (9 shorter events, 0.1 us)
Async XLA Ops:
  0.6 0.9 %copy-start = (f32[1,64,256]{2,1,0:T(8,128)S(1)}, f32[1,64,256]{2,1,0:T(8,128)}, u32[]{:S(2)}) copy-start(f32[1,64,256]{2,1,0:T(8,128)} %param.4) | copy-start | bytes 196612
  1.6 5.2 %copy-start.1 = (f32[1024]{0:T(1024)S(1)}, f32[1024]{0:T(1024)}, u32[]{:S(2)}) copy-start(f32[1024]{0:T(1024)} %param.5) | copy-start | bytes 12292
  1.6 7.6 %collective-permute-start = (f32[2,2,256]{2,1,0:T(2,128)S(1)}, f32[2,2,256]{2,1,0:T(2,128)S(1)}, u32[]{:S(2)}, u32[]{:S(2)}) collective-permute-start(f32[2,2,256]{2,1,0:T(2,128)S(1)} %get-tuple-element.10), channel_id=1, source_target_pairs={{8,16},{16,8},{24,32},{32,24},{40,48},{48,40},{56,64},{64,56},{72,... | collective-permute-start | bytes 12296 | tf_op jit(solution)/shard_map/ppermute | solution.py:39
  6.7 3.7 %collective-permute-start.1 = (f32[2,2,256]{2,1,0:T(2,128)S(1)}, f32[2,2,256]{2,1,0:T(2,128)S(1)}, u32[]{:S(2)}, u32[]{:S(2)}) collective-permute-start(f32[2,2,256]{2,1,0:T(2,128)S(1)} %get-tuple-element.11), channel_id=1, source_target_pairs={{0,8},{8,0},{16,24},{24,16},{32,40},{40,32},{48,56},{56,48},{64,72... | collective-permute-start | bytes 12296 | tf_op jit(solution)/shard_map/ppermute | solution.py:39
  10.5 11.7 %collective-permute-start.2 = (f32[2,72,2]{2,1,0:T(8,128)S(1)}, f32[2,72,2]{2,1,0:T(8,128)S(1)}, u32[]{:S(2)}, u32[]{:S(2)}) collective-permute-start(f32[2,72,2]{2,1,0:T(8,128)S(1)} %get-tuple-element.8), channel_id=1, source_target_pairs={{128,1},{1,128},{129,2},{2,129},{130,3},{3,130},{131,4},{4,131},{1... | collective-permute-start | bytes 3464 | tf_op jit(solution)/shard_map/ppermute | solution.py:39
  12.5 9.7 %collective-permute-start.3 = (f32[2,72,2]{2,1,0:T(8,128)S(1)}, f32[2,72,2]{2,1,0:T(8,128)S(1)}, u32[]{:S(2)}, u32[]{:S(2)}) collective-permute-start(f32[2,72,2]{2,1,0:T(8,128)S(1)} %get-tuple-element.9), channel_id=1, source_target_pairs={{0,128},{128,0},{1,129},{129,1},{2,130},{130,2},{3,131},{131,3},{4... | collective-permute-start | bytes 3464 | tf_op jit(solution)/shard_map/ppermute | solution.py:39

commit v15 on v14

--- a/solution.py
+++ b/solution.py
@@ -195,7 +195,7 @@
     return [edge.astype(jnp.int32) for edge in edges]
 
 
-def level_kernel(noise_ref, fine_inflow_ref, coarse_inflow_ref, mean_ref, corr_ref):
+def level_kernel(noise_ref, inflow_ref, mean_ref, corr_ref):
     flags = boundary_flags()
     fine_rows, fine_cols = FINE_SHAPE
     coarse_rows, coarse_cols = COARSE_SHAPE
@@ -206,7 +206,7 @@
     noise_height = noise_ref[1]
     depth = 1.0 + 0.1 * noise_height
     state = (depth, 0.5 * depth, jnp.zeros_like(depth))
-    fine_inflow = jnp.broadcast_to(fine_inflow_ref[...], FINE_SHAPE)
+    fine_inflow = jnp.broadcast_to(inflow_ref[: FINE_SHAPE[0]], FINE_SHAPE)
     state = walls_at_rest(state, flags, fine_inflow, tile_rows, tile_cols)
     state = advance_at_rest(state, fine_coef, fine_step)
     state = apply_walls(state, flags, fine_inflow, tile_rows, tile_cols)
@@ -221,7 +221,7 @@
     coarse_coef = small[:coarse_rows] * 0.25
     depth = 1.0 + 0.1 * (small[coarse_rows:] * 0.25)
     coarse = (depth, 0.5 * depth, jnp.zeros_like(depth))
-    coarse_inflow = jnp.broadcast_to(coarse_inflow_ref[...], COARSE_SHAPE)
+    coarse_inflow = jnp.broadcast_to(inflow_ref[FINE_SHAPE[0]:], COARSE_SHAPE)
     coarse = walls_at_rest(coarse, flags, coarse_inflow, out_rows, out_cols)
     coarse = advance_at_rest(coarse, coarse_coef, coarse_step)
 
@@ -258,9 +258,9 @@
     mean, corr = pl.pallas_call(
         level_kernel,
         out_shape=(out, out),
-        in_specs=[vmem, vmem, vmem],
+        in_specs=[vmem, vmem],
         out_specs=(vmem, vmem),
-    )(noise, fine_inflow, coarse_inflow)
+    )(noise, jnp.concatenate([fine_inflow, coarse_inflow], axis=0))
     return (mean[None], corr[None])
 
 

time: 26.1 us -> 26.1 us (level)
  other arithmetic: 2.52 us -> 1.38 us
  waiting for transfers between devices: 9.18 us -> 9.78 us
  local copies, waits for them, and re-layouts: 1.68 us -> 2.22 us
    add x2, other arithmetic: 1.22 us -> 0.15 us  [wrapped_rows(): return (0.5 + jnp.roll(window, -lead)).reshape(count, 1)]
    concatenate x0 -> x1, local copies, waits for them, and re-layouts: none -> 0.73 us  [body(): jnp.concatenate([fine_inflow, coarse_inflow], axis=0)]
    ppermute x4, waiting for transfers between devices: 9.18 us -> 9.78 us  [swapped(): got.append(lax.ppermute(block, axis, swap_pairs(count, parity, place)))]
  transfers between devices with their start and end apart: 4 -> 4, of which waited for: 3 -> 3; matrix products, arithmetic and copies ran while one was open for 9% -> 7% of each run, Pallas kernels for 0% -> 0%
where the time goes in v15:
time: 26.1 us; the launch traced here: 25.9 us
  waiting for transfers between devices  9.78 us (37%)
  starting transfers between devices  8.89 us (34%)
  Pallas kernels  2.9 us (11%)
  local copies, waits for them, and re-layouts  2.22 us (9%)
  other arithmetic  1.38 us (5%)
  between operations  0.75 us (3%)
    ppermute x4, waiting for transfers between devices, swapped(): got.append(lax.ppermute(block, axis, swap_pairs(count, parity, place)))  9.78 us
    ppermute x4, starting transfers between devices, swapped(): got.append(lax.ppermute(block, axis, swap_pairs(count, parity, place)))  8.89 us
    pallas_call x1, Pallas kernels, body(): pl.pallas_call(level_kernel, out_shape=(out, out), in_specs=[vmem, vmem],...  2.9 us
    unnamed x5, local copies, waits for them, and re-layouts  0.89 us
    concatenate x1, other arithmetic, with_halo(): jnp.concatenate([tall, east, jnp.zeros((fields, FINE_SHAPE[0], gap_cols),...  0.78 us
    concatenate x1, local copies, waits for them, and re-layouts, body(): jnp.concatenate([fine_inflow, coarse_inflow], axis=0)  0.73 us
  transfers between devices with their start and end apart: 4, of which 3 were waited for; matrix products, arithmetic and copies ran while one was open for 7% of the time, Pallas kernels for 0%

profile of v15, /device:TPU:192, one launch (start us, length us, event | category | flops | bytes accessed | tf_op | source)
XLA Modules:
  0.0 25.9 jit_solution(15771747889658366521)
XLA Ops:
  0.6 0.0 copy-start
  0.7 0.9 %constant_dynamic-update-slice_fusion.1 = f32[2,64,256]{2,1,0:T(8,128)S(1)} fusion(f32[1,64,256]{2,1,0:T(8,128)} %param.3), kind=kLoop, calls=%fused_computation.11 | loop fusion | bytes 131072
  1.5 0.0 copy-done
  1.6 0.0 copy-start.1
  1.6 5.1 %collective-permute-start = (f32[2,2,256]{2,1,0:T(2,128)S(1)}, f32[2,2,256]{2,1,0:T(2,128)S(1)}, u32[]{:S(2)}, u32[]{:S(2)}) collective-permute-start(f32[2,2,256]{2,1,0:T(2,128)S(1)} %get-tuple-element.10), channel_id=1, source_target_pairs={{8,16},{16,8},{24,32},{32,24},{40,48},{48,40},{56,64},{64,56},{72,... | collective-permute-start | bytes 12296 | tf_op jit(solution)/shard_map/ppermute | solution.py:39
  6.7 0.1 collective-permute-start.1
  6.8 0.0 copy-done.1
  6.8 0.2 reshape.70
  7.0 0.2 fusion.1
  7.2 0.1 pad_dynamic-slice_fusion.1
  7.3 0.1 slice_bitcast_fusion.1
  7.4 0.1 pad_dynamic-slice_fusion
  7.5 0.1 slice_bitcast_fusion.3
  7.6 0.1 maximum_add_fusion.1
  7.6 0.1 maximum_add_fusion
  7.7 1.5 %collective-permute-done = f32[2,2,256]{2,1,0:T(2,128)S(1)} collective-permute-done((f32[2,2,256]{2,1,0:T(2,128)S(1)}, f32[2,2,256]{2,1,0:T(2,128)S(1)}, u32[]{:S(2)}, u32[]{:S(2)}) %collective-permute-start) | collective-permute-done | bytes 4128 | tf_op jit(solution)/shard_map/ppermute | solution.py:39
  9.2 1.2 %collective-permute-done.1 = f32[2,2,256]{2,1,0:T(2,128)S(1)} collective-permute-done((f32[2,2,256]{2,1,0:T(2,128)S(1)}, f32[2,2,256]{2,1,0:T(2,128)S(1)}, u32[]{:S(2)}, u32[]{:S(2)}) %collective-permute-start.1) | collective-permute-done | bytes 4128 | tf_op jit(solution)/shard_map/ppermute | solution.py:39
  10.4 0.1 slice_select_fusion.1
  10.5 2.0 %collective-permute-start.2 = (f32[2,72,2]{2,1,0:T(8,128)S(1)}, f32[2,72,2]{2,1,0:T(8,128)S(1)}, u32[]{:S(2)}, u32[]{:S(2)}) collective-permute-start(f32[2,72,2]{2,1,0:T(8,128)S(1)} %get-tuple-element.8), channel_id=1, source_target_pairs={{128,1},{1,128},{129,2},{2,129},{130,3},{3,130},{131,4},{4,131},{1... | collective-permute-start | bytes 3464 | tf_op jit(solution)/shard_map/ppermute | solution.py:39
  12.5 1.7 %collective-permute-start.3 = (f32[2,72,2]{2,1,0:T(8,128)S(1)}, f32[2,72,2]{2,1,0:T(8,128)S(1)}, u32[]{:S(2)}, u32[]{:S(2)}) collective-permute-start(f32[2,72,2]{2,1,0:T(8,128)S(1)} %get-tuple-element.9), channel_id=1, source_target_pairs={{0,128},{128,0},{1,129},{129,1},{2,130},{130,2},{3,131},{131,3},{4... | collective-permute-start | bytes 3464 | tf_op jit(solution)/shard_map/ppermute | solution.py:39
  14.2 0.1 pad_maximum_fusion.2
  14.3 0.7 %copy.13.inflow_ref = f32[112,1]{1,0:T(8,128)} copy(f32[112,1]{0,1:T(1,128)S(1)} %pad_maximum_fusion.2) | data formatting | bytes 896 | tf_op jit(solution)/shard_map/concatenate | solution.py:263
  15.0 0.1 pad.21.clone
  15.1 7.1 %collective-permute-done.2 = f32[2,72,2]{2,1,0:T(8,128)S(1)} collective-permute-done((f32[2,72,2]{2,1,0:T(8,128)S(1)}, f32[2,72,2]{2,1,0:T(8,128)S(1)}, u32[]{:S(2)}, u32[]{:S(2)}) %collective-permute-start.2) | collective-permute-done | bytes 1184 | tf_op jit(solution)/shard_map/ppermute | solution.py:39
  22.2 0.0 collective-permute-done.3
  22.2 0.8 %pad_maximum_fusion.noise_ref = f32[2,72,384]{2,1,0:T(8,128)} fusion(f32[2,72,2]{2,1,0:T(8,128)S(1)} %get-tuple-element.7, f32[2,72,2]{2,1,0:T(8,128)S(1)} %get-tuple-element.6, f32[2,2,256]{2,1,0:T(2,128)S(1)} %get-tuple-element.13, f32[2,4,256]{2,1,0:T(4,128)S(1)} %broadcast_in_dim.12, f32[2,2,256]{2,1,0:T(2,128)S(1)} %get-tuple-element.12, ...), kind=kLoop, calls=%fused_computation.3 | loop fusion | flops 331776 | bytes 372480 | tf_op jit(solution)/shard_map/concatenate | solution.py:61
  23.0 2.9 %shard_map.50 = (f32[3,32,128]{2,1,0:T(8,128)}, f32[3,32,128]{2,1,0:T(8,128)}) custom-call(f32[2,72,384]{2,1,0:T(8,128)} %pad_maximum_fusion.noise_ref, f32[112,1]{1,0:T(8,128)} %copy.13.inflow_ref), custom_call_target="tpu_custom_call" | custom-call | tf_op jit(solution)/shard_map/pallas_call | solution.py:258
  (9 shorter events, 0.1 us)
Async XLA Ops:
  0.6 0.9 %copy-start = (f32[1,64,256]{2,1,0:T(8,128)S(1)}, f32[1,64,256]{2,1,0:T(8,128)}, u32[]{:S(2)}) copy-start(f32[1,64,256]{2,1,0:T(8,128)} %param.4) | copy-start | bytes 196612
  1.6 5.2 %copy-start.1 = (f32[1024]{0:T(1024)S(1)}, f32[1024]{0:T(1024)}, u32[]{:S(2)}) copy-start(f32[1024]{0:T(1024)} %param.5) | copy-start | bytes 12292
  1.6 7.6 %collective-permute-start = (f32[2,2,256]{2,1,0:T(2,128)S(1)}, f32[2,2,256]{2,1,0:T(2,128)S(1)}, u32[]{:S(2)}, u32[]{:S(2)}) collective-permute-start(f32[2,2,256]{2,1,0:T(2,128)S(1)} %get-tuple-element.10), channel_id=1, source_target_pairs={{8,16},{16,8},{24,32},{32,24},{40,48},{48,40},{56,64},{64,56},{72,... | collective-permute-start | bytes 12296 | tf_op jit(solution)/shard_map/ppermute | solution.py:39
  6.7 3.7 %collective-permute-start.1 = (f32[2,2,256]{2,1,0:T(2,128)S(1)}, f32[2,2,256]{2,1,0:T(2,128)S(1)}, u32[]{:S(2)}, u32[]{:S(2)}) collective-permute-start(f32[2,2,256]{2,1,0:T(2,128)S(1)} %get-tuple-element.11), channel_id=1, source_target_pairs={{0,8},{8,0},{16,24},{24,16},{32,40},{40,32},{48,56},{56,48},{64,72... | collective-permute-start | bytes 12296 | tf_op jit(solution)/shard_map/ppermute | solution.py:39
  10.5 11.7 %collective-permute-start.2 = (f32[2,72,2]{2,1,0:T(8,128)S(1)}, f32[2,72,2]{2,1,0:T(8,128)S(1)}, u32[]{:S(2)}, u32[]{:S(2)}) collective-permute-start(f32[2,72,2]{2,1,0:T(8,128)S(1)} %get-tuple-element.8), channel_id=1, source_target_pairs={{128,1},{1,128},{129,2},{2,129},{130,3},{3,130},{131,4},{4,131},{1... | collective-permute-start | bytes 3464 | tf_op jit(solution)/shard_map/ppermute | solution.py:39
  12.5 9.7 %collective-permute-start.3 = (f32[2,72,2]{2,1,0:T(8,128)S(1)}, f32[2,72,2]{2,1,0:T(8,128)S(1)}, u32[]{:S(2)}, u32[]{:S(2)}) collective-permute-start(f32[2,72,2]{2,1,0:T(8,128)S(1)} %get-tuple-element.9), channel_id=1, source_target_pairs={{0,128},{128,0},{1,129},{129,1},{2,130},{130,2},{3,131},{131,3},{4... | collective-permute-start | bytes 3464 | tf_op jit(solution)/shard_map/ppermute | solution.py:39
